TPU v7x, 768 devices: a whole 4x8x12 slice. The times are simulated.
768 devices in a mesh: gx: 24 (over y_hi, z), gy: 32 (over x, y_lo, core).
Axes of the slice: x: 4, y: 8 (y_hi: 2, y_lo: 4; y = y_hi * 4 + y_lo), z: 12, core: 2. Of those that a mesh axis runs over, the one named last changes fastest.
Arguments:
- coarse_state: float32 [3, 768, 4096], P(None, 'gx', 'gy'), may hold values from -6 to 6
- refined_box_state: float32 [24, 64, 3, 64, 256], P('gx', 'gy'), may hold values from -6 to 6
- box_parent: int32 [24, 64], replicated, may hold values from 0 to 32, as said below
Outputs:
- coarse_next: float32 [3, 768, 4096], P(None, 'gx', 'gy')
- fine_next: float32 [24, 64, 3, 64, 256], P('gx', 'gy')
Inputs may be any that keep to these rules, and one draw needn't show every extreme that they name: `box_parent`: entry k of row a names the block row whose refined box sits in slot k of column a; slot k lies on the device of index k // 2 along gy. No block row is named twice in a row; the named blocks of a row form one cyclic run of 16 to 32 consecutive block rows; the value 32 marks an empty slot.
All inputs are finite; a program needn't handle non-finite values.
Results may differ from a plain program's by a relative error of at most 0.00002.
Values sent between devices are 32-bit elements; how exact they have to be, the bound alone decides.
No kernel may reach another device: no remote copies, remote signals or barrier semaphores. Data moves between devices by JAX's collectives and lax.ppermute only.
A program may use at most 64 MiB of HBM per device.

v0:
```python
import jax
import jax.numpy as jnp
from jax import lax
from jax.sharding import PartitionSpec as P

LAM_COARSE = 0.2
LAM_FINE = 0.4


def extended(cells, sides, width):
    for axis, dim in sides:
        count = lax.axis_size(axis)
        head = lax.slice_in_dim(cells, 0, width, axis=dim)
        tail = lax.slice_in_dim(cells, cells.shape[dim] - width, cells.shape[dim], axis=dim)
        cells = jnp.concatenate(
            [
                lax.ppermute(tail, axis, [(i, (i + 1) % count) for i in range(count)]),
                cells,
                lax.ppermute(head, axis, [((i + 1) % count, i) for i in range(count)]),
            ],
            axis=dim,
        )
    return cells


def face_flux_x(padded, span_x, span_y):
    cell_minus = padded[:, 0 : span_x + 1, 2 : span_y + 2]
    cell_left = padded[:, 1 : span_x + 2, 2 : span_y + 2]
    cell_right = padded[:, 2 : span_x + 3, 2 : span_y + 2]
    cell_plus = padded[:, 3 : span_x + 4, 2 : span_y + 2]
    face_mean = (7.0 * (cell_left + cell_right) - (cell_minus + cell_plus)) / 12.0
    face_jump = cell_right - cell_left
    return jnp.stack(
        [face_mean[1] - 0.5 * face_jump[0], face_mean[0] - 0.5 * face_jump[1], -0.5 * face_jump[2]]
    )


def face_flux_y(padded, span_x, span_y):
    cell_minus = padded[:, 2 : span_x + 2, 0 : span_y + 1]
    cell_left = padded[:, 2 : span_x + 2, 1 : span_y + 2]
    cell_right = padded[:, 2 : span_x + 2, 2 : span_y + 3]
    cell_plus = padded[:, 2 : span_x + 2, 3 : span_y + 4]
    face_mean = (7.0 * (cell_left + cell_right) - (cell_minus + cell_plus)) / 12.0
    face_jump = cell_right - cell_left
    return jnp.stack(
        [face_mean[2] - 0.5 * face_jump[0], -0.5 * face_jump[1], face_mean[0] - 0.5 * face_jump[2]]
    )


def advance_rate(padded, factor):
    span_x = padded.shape[1] - 4
    span_y = padded.shape[2] - 4
    flux_x = face_flux_x(padded, span_x, span_y)
    flux_y = face_flux_y(padded, span_x, span_y)
    change = -factor * (flux_x[:, 1:] - flux_x[:, :-1] + (flux_y[:, :, 1:] - flux_y[:, :, :-1]))
    return (change, flux_x, flux_y)


def inject_side(coarse_edge):
    doubled = jnp.repeat(coarse_edge, 2, axis=-1)
    return jnp.broadcast_to(doubled[..., None, :], doubled.shape[:-1] + (2, doubled.shape[-1]))


def inject_end(coarse_edge):
    doubled = jnp.repeat(coarse_edge, 2, axis=-1)
    return jnp.broadcast_to(doubled[..., None], doubled.shape + (2,))


def assemble(field, ghost_left, ghost_right, ghost_low, ghost_high):
    middle = jnp.concatenate([ghost_low, field, ghost_high], axis=-1)
    zero_band = jnp.zeros(ghost_left.shape[:-1] + (2,), field.dtype)
    left_full = jnp.concatenate([zero_band, ghost_left, zero_band], axis=-1)
    right_full = jnp.concatenate([zero_band, ghost_right, zero_band], axis=-1)
    return jnp.concatenate([left_full, middle, right_full], axis=-2)


def fine_section(field, ghost_left, ghost_right, ghost_low, ghost_high):
    padded = assemble(field, ghost_left, ghost_right, ghost_low, ghost_high)
    change, flux_x, flux_y = advance_rate(padded, LAM_FINE)
    return (change, flux_x[:, 0], flux_x[:, -1], flux_y[:, :, 0], flux_y[:, :, -1])


def pair_mean(values):
    return 0.5 * (values[..., 0::2] + values[..., 1::2])


def restrict(field):
    return 0.25 * (
        field[..., 0::2, 0::2]
        + field[..., 1::2, 0::2]
        + (field[..., 0::2, 1::2] + field[..., 1::2, 1::2])
    )


def coarse_margin(field):
    return extended(field, (("gx", 1), ("gy", 2)), 2)


def pick_from(row_index, strips, coarse_edges, targets):
    flag, fine_row, fine_sub, edge_row = targets
    sub_index = jnp.arange(strips.shape[1], dtype=jnp.int32)
    hit_mask = (
        (row_index[None, :, None] == fine_row[:, None, None])
        & (sub_index[None, None, :] == fine_sub[:, None, None])
        & flag[:, None, None]
    )
    fine_part = jnp.sum(
        jnp.where(hit_mask[:, :, :, None, None, None], strips[None], 0.0), axis=(1, 2)
    )
    edge_mask = (row_index[None, :] == edge_row[:, None]) & jnp.logical_not(flag)[:, None]
    edge_part = jnp.sum(jnp.where(edge_mask[:, :, None, None], coarse_edges[None], 0.0), axis=1)
    return (fine_part, edge_part)


def shards(coarse_state, refined_box_state, box_parent):
    count_x = lax.axis_size("gx")
    count_y = lax.axis_size("gy")
    column = lax.axis_index("gx")
    device_row = lax.axis_index("gy")
    slot_count = refined_box_state.shape[1]
    fine_box = refined_box_state[0]
    span_x = coarse_state.shape[1]
    span_y = coarse_state.shape[2]
    block_ids = jnp.arange(count_y, dtype=jnp.int32)
    block_hits = box_parent[:, :, None] == block_ids[None, None, :]
    refined = jnp.any(block_hits, axis=1)
    slot_ids = jnp.arange(box_parent.shape[1], dtype=jnp.int32)
    slot_of = jnp.sum(jnp.where(block_hits, slot_ids[None, :, None], 0), axis=1)
    column_left = (column - 1) % count_x
    column_right = (column + 1) % count_x
    below_block = (device_row - 1) % count_y
    above_block = (device_row + 1) % count_y
    own_table = lax.dynamic_index_in_dim(box_parent, column, 0, keepdims=False)
    left_table = lax.dynamic_index_in_dim(box_parent, column_left, 0, keepdims=False)
    right_table = lax.dynamic_index_in_dim(box_parent, column_right, 0, keepdims=False)
    own_parents = lax.dynamic_slice_in_dim(own_table, device_row * slot_count, slot_count)
    is_live = own_parents < count_y
    parent = jnp.minimum(own_parents, count_y - 1)

    def fine_source(table_column, block):
        flag = refined[table_column, block]
        slot_index = slot_of[table_column, block]
        return (flag, slot_index // slot_count, slot_index % slot_count, block)

    targets_left = fine_source(column_left, parent)
    targets_right = fine_source(column_right, parent)
    targets_low = fine_source(column, (parent - 1) % count_y)
    targets_high = fine_source(column, (parent + 1) % count_y)
    rate_one, flux_x1, flux_y1 = advance_rate(coarse_margin(coarse_state), LAM_COARSE)
    coarse_one = coarse_state + rate_one
    rate_two, flux_x2, flux_y2 = advance_rate(coarse_margin(coarse_one), LAM_COARSE)
    coarse_heun = 0.5 * (coarse_state + coarse_one + rate_two)

    def fine_rates(field, coarse_now):
        strip_left = field[:, :, :2, :]
        strip_right = field[:, :, -2:, :]
        strip_low = field[..., :2]
        strip_high = field[..., -2:]
        edge_left = coarse_now[:, 0, :]
        edge_right = coarse_now[:, -1, :]
        edge_low = coarse_now[:, :, 0]
        edge_high = coarse_now[:, :, -1]
        strip_size = strip_left.size
        edge_size = edge_left.size
        side_pack = jnp.concatenate(
            [
                strip_right.reshape(-1),
                edge_right.reshape(-1),
                strip_left.reshape(-1),
                edge_left.reshape(-1),
            ]
        )[None]
        sides = extended(side_pack, (("gx", 0),), 1)
        from_left = sides[0]
        from_right = sides[2]
        left_strips = from_left[:strip_size].reshape(strip_right.shape)
        left_edges = from_left[strip_size : strip_size + edge_size].reshape(edge_right.shape)
        right_strips = from_right[strip_size + edge_size : 2 * strip_size + edge_size].reshape(
            strip_left.shape
        )
        right_edges = from_right[2 * strip_size + edge_size :].reshape(edge_left.shape)
        pieces = (
            lax.all_gather(left_strips[None], "gy", axis=0, tiled=True),
            lax.all_gather(left_edges[None], "gy", axis=0, tiled=True),
            lax.all_gather(right_strips[None], "gy", axis=0, tiled=True),
            lax.all_gather(right_edges[None], "gy", axis=0, tiled=True),
            lax.all_gather(strip_high[None], "gy", axis=0, tiled=True),
            lax.all_gather(edge_high[None], "gy", axis=0, tiled=True),
            lax.all_gather(strip_low[None], "gy", axis=0, tiled=True),
            lax.all_gather(edge_low[None], "gy", axis=0, tiled=True),
        )
        row_index = jnp.arange(pieces[0].shape[0], dtype=jnp.int32)
        fine_l, edge_l = pick_from(row_index, pieces[0], pieces[1], targets_left)
        fine_r, edge_r = pick_from(row_index, pieces[2], pieces[3], targets_right)
        fine_lo, edge_lo = pick_from(row_index, pieces[4], pieces[5], targets_low)
        fine_hi, edge_hi = pick_from(row_index, pieces[6], pieces[7], targets_high)
        parts = (fine_l, edge_l, fine_r, edge_r, fine_lo, edge_lo, fine_hi, edge_hi)
        picked = tuple((extra for extra in parts))
        ghost_left = picked[0] + inject_side(picked[1])
        ghost_right = picked[2] + inject_side(picked[3])
        ghost_low = picked[4] + inject_end(picked[5])
        ghost_high = picked[6] + inject_end(picked[7])
        return jax.vmap(fine_section)(field, ghost_left, ghost_right, ghost_low, ghost_high)

    rate_f1, left_one, right_one, low_one, high_one = fine_rates(fine_box, coarse_state)
    fine_one = fine_box + rate_f1
    rate_f2, left_two, right_two, low_two, high_two = fine_rates(fine_one, coarse_one)
    fine_final = 0.5 * (fine_box + fine_one + rate_f2)
    reg_left = pair_mean(0.5 * (left_one + left_two))
    reg_right = pair_mean(0.5 * (right_one + right_two))
    reg_low = pair_mean(0.5 * (low_one + low_two))
    reg_high = pair_mean(0.5 * (high_one + high_two))
    restricted = restrict(fine_final)
    side_regs = extended(jnp.stack([reg_left, reg_right])[None], (("gx", 0),), 1)
    left_regs = side_regs[0, 1]
    right_regs = side_regs[2, 0]
    own_grid = own_table.reshape(count_y, slot_count)
    left_grid = left_table.reshape(count_y, slot_count)
    right_grid = right_table.reshape(count_y, slot_count)
    pieces = (
        lax.all_gather(restricted[None], "gy", axis=0, tiled=True),
        lax.all_gather(reg_high[None], "gy", axis=0, tiled=True),
        lax.all_gather(reg_low[None], "gy", axis=0, tiled=True),
        lax.all_gather(left_regs[None], "gy", axis=0, tiled=True),
        lax.all_gather(right_regs[None], "gy", axis=0, tiled=True),
    )

    def select(hit_mask, payload):
        extra = (1,) * (payload.ndim - 2)
        return jnp.sum(
            jnp.where(hit_mask.reshape(hit_mask.shape + extra), payload, 0.0), axis=(0, 1)
        )

    parts = (
        select(own_grid == device_row, pieces[0]),
        select(own_grid == below_block, pieces[1]),
        select(own_grid == above_block, pieces[2]),
        select(left_grid == device_row, pieces[3]),
        select(right_grid == device_row, pieces[4]),
    )
    home_mean, got_below, got_above, got_left, got_right = tuple(
        (extra_part for extra_part in parts)
    )
    face_left = 0.5 * (flux_x1[:, 0] + flux_x2[:, 0])
    face_right = 0.5 * (flux_x1[:, -1] + flux_x2[:, -1])
    face_low = 0.5 * (flux_y1[:, :, 0] + flux_y2[:, :, 0])
    face_high = 0.5 * (flux_y1[:, :, -1] + flux_y2[:, :, -1])
    corr_left = jnp.where(
        refined[column_left, device_row], LAM_COARSE * (got_left - face_left), 0.0
    )
    corr_right = jnp.where(
        refined[column_right, device_row], LAM_COARSE * (face_right - got_right), 0.0
    )
    corr_low = jnp.where(refined[column, below_block], LAM_COARSE * (got_below - face_low), 0.0)
    corr_high = jnp.where(refined[column, above_block], LAM_COARSE * (face_high - got_above), 0.0)
    corr_x = jnp.concatenate(
        [
            corr_left[:, None, :],
            jnp.zeros((3, span_x - 2, span_y), jnp.float32),
            corr_right[:, None, :],
        ],
        axis=1,
    )
    corr_y = jnp.concatenate(
        [
            corr_low[:, :, None],
            jnp.zeros((3, span_x, span_y - 2), jnp.float32),
            corr_high[:, :, None],
        ],
        axis=2,
    )
    coarse_next = coarse_heun + corr_x + corr_y
    coarse_next = jnp.where(refined[column, device_row], home_mean, coarse_next)
    fine_next = jnp.where(is_live[:, None, None, None], fine_final, 0.0)[None]
    return (coarse_next, fine_next)


def solution(mesh):
    in_specs = (P(None, "gx", "gy"), P("gx", "gy", None, None, None), P())
    out_specs = (P(None, "gx", "gy"), P("gx", "gy", None, None, None))
    return jax.shard_map(shards, mesh=mesh, in_specs=in_specs, out_specs=out_specs, check_vma=False)
```

profile of v0, /device:TPU:1, one launch (start us, length us, event | category | flops | bytes accessed | tf_op | source)
XLA Modules:
  0.0 1013.3 jit_solution(8314017373213825743)
XLA Ops:
  7.2 1.0 copy.697
  9.1 4.8 collective-permute-start
  13.9 17.5 %collective-permute-start.1 = (f32[1,6912]{1,0:T(1,128)S(1)}, f32[1,6912]{1,0:T(1,128)S(1)}, u32[]{:S(2)}, u32[]{:S(2)}) collective-permute-start(f32[1,6912]{1,0:T(1,128)S(1)} %broadcast_in_dim.521), channel_id=1, source_target_pairs={{32,0},{64,32},{96,64},{128,96},{160,128},{192,160},{224,192},{256... | collective-permute-start | bytes 82952 | tf_op jit(solution)/shard_map/ppermute | solution.py:19
  32.2 1.9 collective-permute-start.2
  34.1 9.4 collective-permute-start.3
  43.5 0.8 constant_dynamic-update-slice_fusion.1
  44.3 0.9 copy.525
  45.2 1.2 fusion.13
  46.4 1.2 select_reduce_fusion.9
  53.7 1.3 compare_bitcast_fusion
  55.3 42.2 %all-gather.1 = f32[96,32,1]{1,2,0:T(1,128)S(1)} all-gather(f32[3,32,1]{1,2,0:T(1,128)S(1)} %get-tuple-element.84), channel_id=3, replica_groups=mesh['gx'=24,'gy'=32] {'gy'}, dimensions={0}, use_global_device_ids=true | all-gather | bytes 12672 | tf_op jit(solution)/shard_map/all_gather | solution.py:188
  97.8 38.7 %all-gather = f32[64,3,64,2]{2,3,1,0:T(2,128)S(1)} all-gather(f32[2,3,64,2]{2,3,1,0:T(2,128)S(1)} %copy.522), channel_id=2, replica_groups=mesh['gx'=24,'gy'=32] {'gy'}, dimensions={0}, use_global_device_ids=true | all-gather | bytes 101376 | tf_op jit(solution)/shard_map/all_gather | solution.py:187
  136.7 40.0 %all-gather.2 = f32[64,3,64,2]{2,3,1,0:T(2,128)S(1)} all-gather(f32[2,3,64,2]{2,3,1,0:T(2,128)S(1)} %copy.529), channel_id=4, replica_groups=mesh['gx'=24,'gy'=32] {'gy'}, dimensions={0}, use_global_device_ids=true | all-gather | bytes 101376 | tf_op jit(solution)/shard_map/all_gather | solution.py:189
  177.9 38.1 %all-gather.3 = f32[96,32,1]{1,2,0:T(1,128)S(1)} all-gather(f32[3,32,1]{1,2,0:T(1,128)S(1)} %get-tuple-element.83), channel_id=5, replica_groups=mesh['gx'=24,'gy'=32] {'gy'}, dimensions={0}, use_global_device_ids=true | all-gather | bytes 12672 | tf_op jit(solution)/shard_map/all_gather | solution.py:190
  218.4 0.9 pad_maximum_fusion.18
  219.4 3.3 collective-permute-start.4
  222.7 1.9 collective-permute-start.5
  224.7 1.0 fusion.54
  228.6 1.0 maximum_maximum_fusion.2
  230.1 41.3 %all-gather.5 = f32[96,32,1]{1,2,0:T(1,128)S(1)} all-gather(f32[3,32,1]{1,2,0:T(1,128)S(1)} %get-tuple-element.86), channel_id=7, replica_groups=mesh['gx'=24,'gy'=32] {'gy'}, dimensions={0}, use_global_device_ids=true | all-gather | bytes 12672 | tf_op jit(solution)/shard_map/all_gather | solution.py:188
  272.6 39.7 %all-gather.7 = f32[96,32,1]{1,2,0:T(1,128)S(1)} all-gather(f32[3,32,1]{1,2,0:T(1,128)S(1)} %get-tuple-element.85), channel_id=9, replica_groups=mesh['gx'=24,'gy'=32] {'gy'}, dimensions={0}, use_global_device_ids=true | all-gather | bytes 12672 | tf_op jit(solution)/shard_map/all_gather | solution.py:190
  313.7 0.8 fusion.5
  314.7 0.9 slice_reduce_fusion.1
  316.6 38.1 %all_gather.64 = f32[32,3,128]{2,1,0:T(4,128)S(1)} all-gather(f32[1,3,128]{2,1,0:T(4,128)S(1)} %bitcast.212), channel_id=1, replica_groups=mesh['gx'=24,'gy'=32] {'gy'}, dimensions={0}, use_global_device_ids=true | all-gather | bytes 50688 | tf_op jit(solution)/shard_map/all_gather | solution.py:184
  354.8 39.5 %all_gather.70 = f32[32,3,128]{2,1,0:T(4,128)S(1)} all-gather(f32[1,3,128]{2,1,0:T(4,128)S(1)} %bitcast.213), channel_id=1, replica_groups=mesh['gx'=24,'gy'=32] {'gy'}, dimensions={0}, use_global_device_ids=true | all-gather | bytes 50688 | tf_op jit(solution)/shard_map/all_gather | solution.py:186
  394.9 39.6 %all_gather.69 = f32[32,2,3,2,256]{4,3,2,1,0:T(2,128)S(1)} all-gather(f32[1,2,3,2,256]{4,3,2,1,0:T(2,128)S(1)} %broadcast_in_dim_reshape.34), channel_id=1, replica_groups=mesh['gx'=24,'gy'=32] {'gy'}, dimensions={0}, use_global_device_ids=true | all-gather | bytes 405504 | tf_op jit(solution)/shard_map/all_gather | solution.py:185
  435.1 40.9 %all_gather.63 = f32[32,2,3,2,256]{4,3,2,1,0:T(2,128)S(1)} all-gather(f32[1,2,3,2,256]{4,3,2,1,0:T(2,128)S(1)} %broadcast_in_dim_reshape.32), channel_id=1, replica_groups=mesh['gx'=24,'gy'=32] {'gy'}, dimensions={0}, use_global_device_ids=true | all-gather | bytes 405504 | tf_op jit(solution)/shard_map/all_gather | solution.py:183
  478.8 38.8 %all-gather.6 = f32[64,3,64,2]{2,3,1,0:T(2,128)S(1)} all-gather(f32[2,3,64,2]{2,3,1,0:T(2,128)S(1)} %copy.559), channel_id=8, replica_groups=mesh['gx'=24,'gy'=32] {'gy'}, dimensions={0}, use_global_device_ids=true | all-gather | bytes 101376 | tf_op jit(solution)/shard_map/all_gather | solution.py:189
  518.1 39.8 %all-gather.4 = f32[64,3,64,2]{2,3,1,0:T(2,128)S(1)} all-gather(f32[2,3,64,2]{2,3,1,0:T(2,128)S(1)} %copy.554), channel_id=6, replica_groups=mesh['gx'=24,'gy'=32] {'gy'}, dimensions={0}, use_global_device_ids=true | all-gather | bytes 101376 | tf_op jit(solution)/shard_map/all_gather | solution.py:187
  561.6 1.9 collective-permute-start.7
  563.5 3.4 collective-permute-start.6
  567.6 40.4 %all_gather.77 = f32[32,2,3,2,256]{4,3,2,1,0:T(2,128)S(1)} all-gather(f32[1,2,3,2,256]{4,3,2,1,0:T(2,128)S(1)} %broadcast_in_dim_reshape.38), channel_id=1, replica_groups=mesh['gx'=24,'gy'=32] {'gy'}, dimensions={0}, use_global_device_ids=true | all-gather | bytes 405504 | tf_op jit(solution)/shard_map/all_gather | solution.py:185
  608.1 1.4 select_reduce_fusion.1
  610.2 39.1 %all_gather.78 = f32[32,3,128]{2,1,0:T(4,128)S(1)} all-gather(f32[1,3,128]{2,1,0:T(4,128)S(1)} %bitcast.210), channel_id=1, replica_groups=mesh['gx'=24,'gy'=32] {'gy'}, dimensions={0}, use_global_device_ids=true | all-gather | bytes 50688 | tf_op jit(solution)/shard_map/all_gather | solution.py:186
  650.2 0.8 broadcast_in_dim.576
  651.1 1.3 copy.569
  653.1 39.8 %all_gather.71 = f32[32,2,3,2,256]{4,3,2,1,0:T(2,128)S(1)} all-gather(f32[1,2,3,2,256]{4,3,2,1,0:T(2,128)S(1)} %broadcast_in_dim_reshape.36), channel_id=1, replica_groups=mesh['gx'=24,'gy'=32] {'gy'}, dimensions={0}, use_global_device_ids=true | all-gather | bytes 405504 | tf_op jit(solution)/shard_map/all_gather | solution.py:183
  693.1 1.4 select_reduce_fusion.2
  695.1 39.3 %all_gather.72 = f32[32,3,128]{2,1,0:T(4,128)S(1)} all-gather(f32[1,3,128]{2,1,0:T(4,128)S(1)} %bitcast.211), channel_id=1, replica_groups=mesh['gx'=24,'gy'=32] {'gy'}, dimensions={0}, use_global_device_ids=true | all-gather | bytes 50688 | tf_op jit(solution)/shard_map/all_gather | solution.py:184
  735.3 0.9 broadcast_in_dim.559
  739.6 1.6 select_bitcast_fusion
  741.2 3.4 slice.584
  744.6 3.4 slice.585
  748.0 3.4 slice.586
  751.5 3.4 slice.587
  760.2 1.9 collective-permute-start.8
  762.1 9.4 collective-permute-start.9
  771.8 4.1 collective-permute-done.8
  776.6 3.7 collective-permute-start.10
  780.3 2.1 collective-permute-start.11
  782.8 3.9 collective-permute-done.11
  787.2 0.8 copy.627
  788.9 41.8 %all-gather.11 = f32[64,3,32]{2,1,0:T(4,128)S(1)} all-gather(f32[2,3,32]{2,1,0:T(4,128)S(1)} %copy.598), channel_id=13, replica_groups=mesh['gx'=24,'gy'=32] {'gy'}, dimensions={0}, use_global_device_ids=true | all-gather | bytes 25344 | tf_op jit(solution)/shard_map/all_gather | solution.py:222
  830.8 40.3 %all-gather.12 = f32[64,3,32]{2,1,0:T(4,128)S(1)} all-gather(f32[2,3,32]{2,1,0:T(4,128)S(1)} %copy.604), channel_id=14, replica_groups=mesh['gx'=24,'gy'=32] {'gy'}, dimensions={0}, use_global_device_ids=true | all-gather | bytes 25344 | tf_op jit(solution)/shard_map/all_gather | solution.py:223
  871.1 0.8 select_reduce_fusion.11
  871.9 0.8 select_reduce_fusion.10
  874.4 10.7 %collective-permute-start.13 = (f32[1,2,2,3,128]{4,2,3,1,0:T(2,128)S(1)}, f32[1,2,2,3,128]{4,2,3,1,0:T(2,128)S(1)}, u32[]{:S(2)}, u32[]{:S(2)}) collective-permute-start(f32[1,2,2,3,128]{4,2,3,1,0:T(2,128)S(1)} %maximum_bitcast_fusion), channel_id=1, source_target_pairs={{32,0},{64,32},{96,64},{128,96},{160,128},{192,160},{224,192},{256... | collective-permute-start | bytes 18440 | tf_op jit(solution)/shard_map/ppermute | solution.py:19
  885.1 1.9 collective-permute-start.12
  887.7 7.8 collective-permute-done.12
  895.5 39.4 %all-gather.10 = f32[32,1,2,3,128]{4,2,3,1,0:T(2,128)S(1)} all-gather(f32[1,1,2,3,128]{4,2,3,1,0:T(2,128)S(1)} %slice.773), channel_id=12, replica_groups=mesh['gx'=24,'gy'=32] {'gy'}, dimensions={0}, use_global_device_ids=true | all-gather | bytes 101376 | tf_op jit(solution)/shard_map/all_gather | solution.py:225
  934.8 39.9 %all-gather.9 = f32[32,1,2,3,128]{4,2,3,1,0:T(2,128)S(1)} all-gather(f32[1,1,2,3,128]{4,2,3,1,0:T(2,128)S(1)} %slice.772), channel_id=11, replica_groups=mesh['gx'=24,'gy'=32] {'gy'}, dimensions={0}, use_global_device_ids=true | all-gather | bytes 101376 | tf_op jit(solution)/shard_map/all_gather | solution.py:224
  975.0 2.0 broadcast_select_fusion.3
  977.3 16.0 %copy.581 = f32[32,2,3,32,128]{3,1,0,4,2:T(2,128)} copy(f32[32,2,3,32,128]{4,3,2,1,0:T(8,128)} %bitcast.185) | data formatting | bytes 6291456 | tf_op jit(solution)/shard_map/all_gather | solution.py:221
  993.3 11.6 %select_reduce_fusion = f32[3,32,128]{1,2,0:T(8,128)S(1)} fusion(f32[32,2,3,32,128]{3,1,0,4,2:T(2,128)} %copy.581, pred[32,2]{1,0:T(8,128)(4,1)S(1)} %eq.380), kind=kLoop, calls=%fused_computation.8 | loop fusion | flops 1560576 | bytes 3194944 | tf_op jit(solution)/shard_map/reduce_sum | solution.py:230
  (284 shorter events, 47.3 us)
Async XLA Ops:
  7.2 970.1 %all-gather.15.cloned.1.call-start = ((), (), s32[]{:S(2)}) async-start(), calls=%async_computation | async-start | bytes 3244032 | tf_op jit(solution)/shard_map/all_gather | solution.py:221
  9.1 307.5 %collective-permute-start = (f32[1,6912]{1,0:T(1,128)S(1)}, f32[1,6912]{1,0:T(1,128)S(1)}, u32[]{:S(2)}, u32[]{:S(2)}) collective-permute-start(f32[1,6912]{1,0:T(1,128)S(1)} %broadcast_in_dim.521), channel_id=1, source_target_pairs={{0,32},{32,64},{64,96},{96,128},{128,160},{160,192},{192,224},{224... | collective-permute-start | bytes 82952 | tf_op jit(solution)/shard_map/ppermute | solution.py:17
  13.9 340.8 %collective-permute-start.1 = (f32[1,6912]{1,0:T(1,128)S(1)}, f32[1,6912]{1,0:T(1,128)S(1)}, u32[]{:S(2)}, u32[]{:S(2)}) collective-permute-start(f32[1,6912]{1,0:T(1,128)S(1)} %broadcast_in_dim.521), channel_id=1, source_target_pairs={{32,0},{64,32},{96,64},{128,96},{160,128},{192,160},{224,192},{256... | collective-permute-start | bytes 82952 | tf_op jit(solution)/shard_map/ppermute | solution.py:19
  32.2 186.3 %collective-permute-start.2 = (f32[3,2,128]{2,1,0:T(2,128)S(1)}, f32[3,2,128]{2,1,0:T(2,128)S(1)}, u32[]{:S(2)}, u32[]{:S(2)}) collective-permute-start(f32[3,2,128]{2,1,0:T(2,128)S(1)} %get-tuple-element.123), channel_id=1, source_target_pairs={{0,32},{32,64},{64,96},{96,128},{128,160},{160,192},{192,224},{224... | collective-permute-start | bytes 9224 | tf_op jit(solution)/shard_map/ppermute | solution.py:17
  34.1 184.3 %collective-permute-start.3 = (f32[3,2,128]{2,1,0:T(2,128)S(1)}, f32[3,2,128]{2,1,0:T(2,128)S(1)}, u32[]{:S(2)}, u32[]{:S(2)}) collective-permute-start(f32[3,2,128]{2,1,0:T(2,128)S(1)} %get-tuple-element.124), channel_id=1, source_target_pairs={{32,0},{64,32},{96,64},{128,96},{160,128},{192,160},{224,192},{256... | collective-permute-start | bytes 9224 | tf_op jit(solution)/shard_map/ppermute | solution.py:19
  176.8 300.8 %copy-start.7 = (pred[2,32,2]{1,2,0:T(4,128)(4,1)}, pred[2,32,2]{1,2,0:T(4,128)(4,1)S(1)}, u32[]{:S(2)}) copy-start(pred[2,32,2]{1,2,0:T(4,128)(4,1)S(1)} %and_and_fusion) | copy-start | bytes 388
  176.9 300.8 %copy-start.6 = (pred[2,32,2]{1,2,0:T(4,128)(4,1)}, pred[2,32,2]{1,2,0:T(4,128)(4,1)S(1)}, u32[]{:S(2)}) copy-start(pred[2,32,2]{1,2,0:T(4,128)(4,1)S(1)} %and_and_fusion.3) | copy-start | bytes 388
  177.0 0.5 copy-start.8
  177.7 135.5 %copy-start.9 = (pred[2,32,2]{1,2,0:T(4,128)(4,1)}, pred[2,32,2]{1,2,0:T(4,128)(4,1)S(1)}, u32[]{:S(2)}) copy-start(pred[2,32,2]{1,2,0:T(4,128)(4,1)S(1)} %and_and_fusion.1) | copy-start | bytes 388
  177.9 256.6 %copy-start.12 = (pred[2,32]{1,0:T(4,128)(4,1)}, pred[2,32]{1,0:T(4,128)(4,1)S(1)}, u32[]{:S(2)}) copy-start(pred[2,32]{1,0:T(4,128)(4,1)S(1)} %get-tuple-element.134) | copy-start | bytes 196
  177.9 256.6 %copy-start.13 = (pred[2,32]{1,0:T(4,128)(4,1)}, pred[2,32]{1,0:T(4,128)(4,1)S(1)}, u32[]{:S(2)}) copy-start(pred[2,32]{1,0:T(4,128)(4,1)S(1)} %get-tuple-element.135) | copy-start | bytes 196
  218.4 260.0 %copy-start = (f32[1,2,3,64,256]{4,3,2,1,0:T(8,128)S(1)}, f32[1,2,3,64,256]{4,3,2,1,0:T(8,128)}, u32[]{:S(2)}) copy-start(f32[1,2,3,64,256]{4,3,2,1,0:T(8,128)} %param.4) | copy-start | bytes 1179652
  219.4 8.5 collective-permute-start.4
  222.7 5.8 collective-permute-start.5
  226.2 0.6 copy-start.4
  435.0 82.7 %copy-start.10 = (pred[2,32,2]{1,2,0:T(4,128)(4,1)S(1)}, pred[2,32,2]{1,2,0:T(4,128)(4,1)}, u32[]{:S(2)}) copy-start(pred[2,32,2]{1,2,0:T(4,128)(4,1)} %copy-done.9) | copy-start | bytes 388
  435.0 124.0 %copy-start.5 = (f32[2,3,64]{2,0,1:T(2,128)S(1)}, f32[2,3,64]{2,0,1:T(2,128)}, u32[]{:S(2)}) copy-start(f32[2,3,64]{2,0,1:T(2,128)} %broadcast_in_dim.565) | copy-start | bytes 4612
  477.7 0.7 copy-start.1
  561.6 5.3 collective-permute-start.7
  563.5 88.9 %collective-permute-start.6 = (f32[1,6912]{1,0:T(1,128)}, f32[1,6912]{1,0:T(1,128)}, u32[]{:S(2)}, u32[]{:S(2)}) collective-permute-start(f32[1,6912]{1,0:T(1,128)} %broadcast_in_dim.555), channel_id=1, source_target_pairs={{0,32},{32,64},{64,96},{96,128},{128,160},{160,192},{192,224},{224... | collective-permute-start | bytes 82952 | tf_op jit(solution)/shard_map/ppermute | solution.py:17
  566.9 0.6 copy-start.11
  736.2 137.2 %copy-start.2 = (f32[1,2,65,256]{3,2,1,0:T(8,128)S(1)}, f32[1,2,65,256]{3,2,1,0:T(8,128)}, u32[]{:S(2)}) copy-start(f32[1,2,65,256]{3,2,1,0:T(8,128)} %copy-done.1) | copy-start | bytes 399364
  760.2 15.7 %collective-permute-start.8 = (f32[3,2,128]{1,2,0:T(8,128)S(1)}, f32[3,2,128]{1,2,0:T(8,128)S(1)}, u32[]{:S(2)}, u32[]{:S(2)}) collective-permute-start(f32[3,2,128]{1,2,0:T(8,128)S(1)} %get-tuple-element.82), channel_id=1, source_target_pairs={{0,32},{32,64},{64,96},{96,128},{128,160},{160,192},{192,224},{224... | collective-permute-start | bytes 9224 | tf_op jit(solution)/shard_map/ppermute | solution.py:17
  762.1 14.3 %collective-permute-start.9 = (f32[3,2,128]{1,2,0:T(8,128)S(1)}, f32[3,2,128]{1,2,0:T(8,128)S(1)}, u32[]{:S(2)}, u32[]{:S(2)}) collective-permute-start(f32[3,2,128]{1,2,0:T(8,128)S(1)} %get-tuple-element.81), channel_id=1, source_target_pairs={{32,0},{64,32},{96,64},{128,96},{160,128},{192,160},{224,192},{256... | collective-permute-start | bytes 9224 | tf_op jit(solution)/shard_map/ppermute | solution.py:19
  776.6 6.1 collective-permute-start.10
  780.3 6.4 collective-permute-start.11
  874.4 13.3 %collective-permute-start.13 = (f32[1,2,2,3,128]{4,2,3,1,0:T(2,128)S(1)}, f32[1,2,2,3,128]{4,2,3,1,0:T(2,128)S(1)}, u32[]{:S(2)}, u32[]{:S(2)}) collective-permute-start(f32[1,2,2,3,128]{4,2,3,1,0:T(2,128)S(1)} %maximum_bitcast_fusion), channel_id=1, source_target_pairs={{32,0},{64,32},{96,64},{128,96},{160,128},{192,160},{224,192},{256... | collective-permute-start | bytes 18440 | tf_op jit(solution)/shard_map/ppermute | solution.py:19
  885.1 10.4 %collective-permute-start.12 = (f32[1,2,2,3,128]{4,2,3,1,0:T(2,128)S(1)}, f32[1,2,2,3,128]{4,2,3,1,0:T(2,128)S(1)}, u32[]{:S(2)}, u32[]{:S(2)}) collective-permute-start(f32[1,2,2,3,128]{4,2,3,1,0:T(2,128)S(1)} %maximum_bitcast_fusion), channel_id=1, source_target_pairs={{0,32},{32,64},{64,96},{96,128},{128,160},{160,192},{192,224},{224... | collective-permute-start | bytes 18440 | tf_op jit(solution)/shard_map/ppermute | solution.py:17
  977.3 27.6 %copy-start.3 = (f32[3,32,128]{1,2,0:T(8,128)S(1)}, f32[3,32,128]{1,2,0:T(8,128)}, u32[]{:S(2)}) copy-start(f32[3,32,128]{1,2,0:T(8,128)} %copy.627) | copy-start | bytes 147460
  977.3 27.6 %copy-start.14 = (f32[128]{0:T(128)S(1)}, f32[128]{0:T(128)}, u32[]{:S(2)}) copy-start(f32[128]{0:T(128)} %pad.5.clone) | copy-start | bytes 1540
  977.3 27.6 %copy-start.15 = (f32[32]{0:T(128)S(1)}, f32[32]{0:T(128)}, u32[]{:S(2)}) copy-start(f32[32]{0:T(128)} %pad.8.clone) | copy-start | bytes 388
Sparse Core Ops, SparseCore 0:
  755.7 63.4 all-gather.14
where the time goes:
time: 1020 us; the launch traced here: 1010 us
  blocking collectives  797 us (78%)
  starting transfers between devices  73.8 us (7%)
  local copies, waits for them, and re-layouts  62.5 us (6%)
  other arithmetic  47.5 us (5%)
  waiting for transfers between devices  17 us (2%)
  between operations  15.5 us (2%)
    all_gather x2, blocking collectives, fine_rates(): lax.all_gather(edge_high[None], 'gy', axis=0, tiled=True)  83.5 us
    all_gather x2, blocking collectives, fine_rates(): lax.all_gather(left_strips[None], 'gy', axis=0, tiled=True)  80.8 us
    all_gather x2, blocking collectives, fine_rates(): lax.all_gather(right_strips[None], 'gy', axis=0, tiled=True)  80 us
    all_gather x2, blocking collectives, fine_rates(): lax.all_gather(strip_low[None], 'gy', axis=0, tiled=True)  78.8 us
    all_gather x2, blocking collectives, fine_rates(): lax.all_gather(right_edges[None], 'gy', axis=0, tiled=True)  78.6 us
    all_gather x2, blocking collectives, fine_rates(): lax.all_gather(strip_high[None], 'gy', axis=0, tiled=True)  78.5 us
    all_gather x2, blocking collectives, fine_rates(): lax.all_gather(edge_low[None], 'gy', axis=0, tiled=True)  77.8 us
    all_gather x2, blocking collectives, fine_rates(): lax.all_gather(left_edges[None], 'gy', axis=0, tiled=True)  77.5 us
  transfers between devices with their start and end apart: 15, of which 5 were waited for; matrix products, arithmetic and copies ran while one was open for 5% of the time, Pallas kernels for 0%

commit v1 on v0

--- a/solution.py
+++ b/solution.py
@@ -110,6 +110,18 @@
     edge_mask = (row_index[None, :] == edge_row[:, None]) & jnp.logical_not(flag)[:, None]
     edge_part = jnp.sum(jnp.where(edge_mask[:, :, None, None], coarse_edges[None], 0.0), axis=1)
     return (fine_part, edge_part)
+
+
+def gather_rows(parts):
+    flat = jnp.concatenate([part.reshape(-1) for part in parts])[None]
+    rows = lax.all_gather(flat, "gy", axis=0, tiled=True)
+    count = rows.shape[0]
+    out = []
+    offset = 0
+    for part in parts:
+        out.append(rows[:, offset : offset + part.size].reshape((count,) + part.shape))
+        offset += part.size
+    return tuple(out)
 
 
 def shards(coarse_state, refined_box_state, box_parent):
@@ -179,15 +191,8 @@
             strip_left.shape
         )
         right_edges = from_right[2 * strip_size + edge_size :].reshape(edge_left.shape)
-        pieces = (
-            lax.all_gather(left_strips[None], "gy", axis=0, tiled=True),
-            lax.all_gather(left_edges[None], "gy", axis=0, tiled=True),
-            lax.all_gather(right_strips[None], "gy", axis=0, tiled=True),
-            lax.all_gather(right_edges[None], "gy", axis=0, tiled=True),
-            lax.all_gather(strip_high[None], "gy", axis=0, tiled=True),
-            lax.all_gather(edge_high[None], "gy", axis=0, tiled=True),
-            lax.all_gather(strip_low[None], "gy", axis=0, tiled=True),
-            lax.all_gather(edge_low[None], "gy", axis=0, tiled=True),
+        pieces = gather_rows(
+            (left_strips, left_edges, right_strips, right_edges, strip_high, edge_high, strip_low, edge_low)
         )
         row_index = jnp.arange(pieces[0].shape[0], dtype=jnp.int32)
         fine_l, edge_l = pick_from(row_index, pieces[0], pieces[1], targets_left)
@@ -217,13 +222,7 @@
     own_grid = own_table.reshape(count_y, slot_count)
     left_grid = left_table.reshape(count_y, slot_count)
     right_grid = right_table.reshape(count_y, slot_count)
-    pieces = (
-        lax.all_gather(restricted[None], "gy", axis=0, tiled=True),
-        lax.all_gather(reg_high[None], "gy", axis=0, tiled=True),
-        lax.all_gather(reg_low[None], "gy", axis=0, tiled=True),
-        lax.all_gather(left_regs[None], "gy", axis=0, tiled=True),
-        lax.all_gather(right_regs[None], "gy", axis=0, tiled=True),
-    )
+    pieces = gather_rows((restricted, reg_high, reg_low, left_regs, right_regs))
 
     def select(hit_mask, payload):
         extra = (1,) * (payload.ndim - 2)

time: 1020 us -> 783 us (0.77)
  blocking collectives: 797 us -> 0 us
  waiting for transfers between devices: 17 us -> 600 us
  other arithmetic: 47.5 us -> 28.2 us
    all_gather x20 -> x0, blocking collectives: 797 us -> none  [the longest x2 83.5 us: fine_rates(): lax.all_gather(edge_high[None], 'gy', axis=0, tiled=True)]
    unnamed x1 -> x5, waiting for transfers between devices: 0.02 us -> 561 us
    all_gather x1, waiting for transfers between devices: 0.02 us -> 30.9 us  [gather_rows(): rows = lax.all_gather(flat, 'gy', axis=0, tiled=True)]
    all_gather x22 -> x2, local copies, waits for them, and re-layouts: 17 us -> 3.2 us  [gather_rows(): rows = lax.all_gather(flat, 'gy', axis=0, tiled=True)]
  transfers between devices with their start and end apart: 15 -> 17, of which waited for: 5 -> 8; matrix products, arithmetic and copies ran while one was open for 5% -> 3% of each run, Pallas kernels for 0% -> 0%
where the time goes in v1:
time: 783 us; the launch traced here: 781 us
  waiting for transfers between devices  600 us (77%)
  starting transfers between devices  77.5 us (10%)
  local copies, waits for them, and re-layouts  59.9 us (8%)
  other arithmetic  28.2 us (4%)
  between operations  16.2 us (2%)
    unnamed x5, waiting for transfers between devices  561 us
    ppermute x7, starting transfers between devices, extended(): lax.ppermute(head, axis, [((i + 1) % count, i) for i in range(count)])  53.2 us
    all_gather x1, waiting for transfers between devices, gather_rows(): rows = lax.all_gather(flat, 'gy', axis=0, tiled=True)  30.9 us
    ppermute x7, starting transfers between devices, extended(): lax.ppermute(tail, axis, [(i, (i + 1) % count) for i in range(count)])  24 us
  transfers between devices with their start and end apart: 17, of which 8 were waited for; matrix products, arithmetic and copies ran while one was open for 3% of the time, Pallas kernels for 0%

profile of v1, /device:TPU:1, one launch (start us, length us, event | category | flops | bytes accessed | tf_op | source)
XLA Modules:
  0.0 781.5 jit_solution(10727735576472569293)
XLA Ops:
  7.2 0.7 slice_reduce_fusion.11
  8.0 1.0 copy.360
  9.1 4.8 collective-permute-start
  14.0 17.5 %collective-permute-start.1 = (f32[1,6912]{1,0:T(1,128)S(1)}, f32[1,6912]{1,0:T(1,128)S(1)}, u32[]{:S(2)}, u32[]{:S(2)}) collective-permute-start(f32[1,6912]{1,0:T(1,128)S(1)} %broadcast_in_dim.536), channel_id=1, source_target_pairs={{32,0},{64,32},{96,64},{128,96},{160,128},{192,160},{224,192},{256... | collective-permute-start | bytes 82952 | tf_op jit(solution)/shard_map/ppermute | solution.py:19
  31.4 0.7 fusion.122
  32.2 3.4 collective-permute-start.3
  35.5 1.9 collective-permute-start.2
  45.8 1.3 dynamic-slice.1
  47.8 3.7 collective-permute-start.4
  51.5 1.9 collective-permute-start.5
  54.8 1.0 copy-done.1
  55.9 1.9 collective-permute-done.5
  59.2 280.7 %all-reduce.9.cloned.1.call-done = f32[276480]{0:T(1024)} async-done(((f32[276480]{0:T(1024)}), f32[276480]{0:T(1024)}) %all-reduce.9.cloned.1.call-update) | async-done | bytes 1105936
  339.9 1.6 reshape.1038
  345.9 0.8 fusion.6
  349.7 3.1 collective-permute-start.6
  352.8 8.4 %collective-permute-start.7 = (f32[1,6912]{1,0:T(1,128)S(1)}, f32[1,6912]{1,0:T(1,128)S(1)}, u32[]{:S(2)}, u32[]{:S(2)}) collective-permute-start(f32[1,6912]{1,0:T(1,128)S(1)} %broadcast_in_dim.577), channel_id=1, source_target_pairs={{32,0},{64,32},{96,64},{128,96},{160,128},{192,160},{224,192},{256... | collective-permute-start | bytes 82952 | tf_op jit(solution)/shard_map/ppermute | solution.py:19
  363.0 1.0 copy-done
  364.3 0.7 compare_bitcast_fusion
  365.0 0.8 fusion.107
  365.8 280.0 %all-reduce.11.cloned.1.call-done = f32[276480]{0:T(1024)} async-done(((f32[276480]{0:T(1024)}), f32[276480]{0:T(1024)}) %all-reduce.11.cloned.1.call-update) | async-done | bytes 1105936
  645.8 1.6 reshape.1039
  647.4 0.7 fusion.111
  649.3 1.1 copy.271
  650.3 0.8 copy.272
  651.2 1.1 select_reduce_fusion.4
  652.4 0.7 select_reduce_fusion.10
  654.4 0.7 fusion.23
  655.1 0.8 fusion.26
  655.9 0.8 copy.278
  661.2 0.8 copy-done.9
  662.4 0.9 select_bitcast_fusion
  663.4 3.4 slice.689
  666.8 3.4 slice.690
  670.2 3.4 slice.687
  673.7 3.4 slice.688
  678.8 3.1 collective-permute-start.8
  681.9 8.4 %collective-permute-start.9 = (f32[1,2,2,3,128]{4,2,3,1,0:T(2,128)S(1)}, f32[1,2,2,3,128]{4,2,3,1,0:T(2,128)S(1)}, u32[]{:S(2)}, u32[]{:S(2)}) collective-permute-start(f32[1,2,2,3,128]{4,2,3,1,0:T(2,128)S(1)} %maximum_bitcast_fusion), channel_id=1, source_target_pairs={{32,0},{64,32},{96,64},{128,96},{160,128},{192,160},{224,192},{256... | collective-permute-start | bytes 18440 | tf_op jit(solution)/shard_map/ppermute | solution.py:19
  691.2 0.7 reshape.1047
  692.0 9.6 %collective-permute-start.11 = (f32[3,2,128]{2,1,0:T(2,128)S(1)}, f32[3,2,128]{2,1,0:T(2,128)S(1)}, u32[]{:S(2)}, u32[]{:S(2)}) collective-permute-start(f32[3,2,128]{2,1,0:T(2,128)S(1)} %get-tuple-element.120), channel_id=1, source_target_pairs={{32,0},{64,32},{96,64},{128,96},{160,128},{192,160},{224,192},{256... | collective-permute-start | bytes 9224 | tf_op jit(solution)/shard_map/ppermute | solution.py:19
  701.6 1.9 collective-permute-start.10
  703.6 0.7 eq.380
  704.6 0.7 broadcast_in_dim.611
  705.5 0.7 broadcast_in_dim.616
  706.4 0.7 broadcast_in_dim.618
  707.4 0.7 broadcast_in_dim.623
  709.3 0.7 fusion.123
  709.9 2.1 collective-permute-done.10
  712.2 5.5 collective-permute-start.12
  717.7 3.9 collective-permute-start.13
  721.7 2.9 collective-permute-done.13
  725.6 30.9 %all-gather.6.cloned.1.call-done = f32[32,1,26496]{2,1,0:T(1,128)} async-done(((f32[1,1,26496]{2,1,0:T(1,128)}), f32[32,1,26496]{2,1,0:T(1,128)}) %all-gather.6.cloned.1.call-update) | async-done | bytes 3391504 | tf_op jit(solution)/shard_map/all_gather | solution.py:117
  756.5 2.2 copy.359
  759.0 1.4 fusion
  761.1 1.3 reduce_sum.262
  763.0 1.4 fusion.73
  764.4 0.7 reduce_sum.270
  765.2 0.7 reduce_sum.274
  766.1 0.9 reduce_sum.260
  767.0 0.7 reduce_sum.263
  767.7 0.7 reduce_sum.267
  768.4 2.0 broadcast_select_fusion.1
  770.4 2.2 fusion.61
  772.6 2.3 fusion.68
  (331 shorter events, 34.5 us)
Async XLA Ops:
  7.2 30.4 %copy-start.3 = (f32[3,32,128]{2,1,0:T(8,128)S(1)}, f32[3,32,128]{2,1,0:T(8,128)}, u32[]{:S(2)}) copy-start(f32[3,32,128]{2,1,0:T(8,128)} %param.3) | copy-start | bytes 147460
  7.2 30.6 %copy-start.21 = (s32[24,64]{1,0:T(8,128)S(1)}, s32[24,64]{1,0:T(8,128)}, u32[]{:S(2)}) copy-start(s32[24,64]{1,0:T(8,128)} %param.5) | copy-start | bytes 18436
  7.2 332.8 %all-reduce.9.cloned.1.call-start = ((), (), s32[]{:S(2)}) async-start(), calls=%async_computation | async-start | bytes 2211840
  9.1 44.4 %collective-permute-start = (f32[1,6912]{1,0:T(1,128)S(1)}, f32[1,6912]{1,0:T(1,128)S(1)}, u32[]{:S(2)}, u32[]{:S(2)}) collective-permute-start(f32[1,6912]{1,0:T(1,128)S(1)} %broadcast_in_dim.536), channel_id=1, source_target_pairs={{0,32},{32,64},{64,96},{96,128},{128,160},{160,192},{192,224},{224... | collective-permute-start | bytes 82952 | tf_op jit(solution)/shard_map/ppermute | solution.py:17
  14.0 39.6 %collective-permute-start.1 = (f32[1,6912]{1,0:T(1,128)S(1)}, f32[1,6912]{1,0:T(1,128)S(1)}, u32[]{:S(2)}, u32[]{:S(2)}) collective-permute-start(f32[1,6912]{1,0:T(1,128)S(1)} %broadcast_in_dim.536), channel_id=1, source_target_pairs={{32,0},{64,32},{96,64},{128,96},{160,128},{192,160},{224,192},{256... | collective-permute-start | bytes 82952 | tf_op jit(solution)/shard_map/ppermute | solution.py:19
  32.2 15.5 %collective-permute-start.3 = (f32[3,2,128]{2,1,0:T(2,128)S(1)}, f32[3,2,128]{2,1,0:T(2,128)S(1)}, u32[]{:S(2)}, u32[]{:S(2)}) collective-permute-start(f32[3,2,128]{2,1,0:T(2,128)S(1)} %get-tuple-element.122), channel_id=1, source_target_pairs={{32,0},{64,32},{96,64},{128,96},{160,128},{192,160},{224,192},{256... | collective-permute-start | bytes 9224 | tf_op jit(solution)/shard_map/ppermute | solution.py:19
  35.5 12.1 %collective-permute-start.2 = (f32[3,2,128]{2,1,0:T(2,128)S(1)}, f32[3,2,128]{2,1,0:T(2,128)S(1)}, u32[]{:S(2)}, u32[]{:S(2)}) collective-permute-start(f32[3,2,128]{2,1,0:T(2,128)S(1)} %get-tuple-element.121), channel_id=1, source_target_pairs={{0,32},{32,64},{64,96},{96,128},{128,160},{160,192},{192,224},{224... | collective-permute-start | bytes 9224 | tf_op jit(solution)/shard_map/ppermute | solution.py:17
  44.8 297.8 %copy-start.23 = (pred[2,32,2]{1,2,0:T(4,128)(4,1)}, pred[2,32,2]{1,2,0:T(4,128)(4,1)S(1)}, u32[]{:S(2)}) copy-start(pred[2,32,2]{1,2,0:T(4,128)(4,1)S(1)} %and_and_fusion.1) | copy-start | bytes 388
  44.8 297.4 %copy-start.28 = (pred[2,32]{1,0:T(4,128)(4,1)}, pred[2,32]{1,0:T(4,128)(4,1)S(1)}, u32[]{:S(2)}) copy-start(pred[2,32]{1,0:T(4,128)(4,1)S(1)} %compare_and_fusion) | copy-start | bytes 196
  45.0 298.3 %copy-start.29 = (pred[2,32]{1,0:T(4,128)(4,1)}, pred[2,32]{1,0:T(4,128)(4,1)S(1)}, u32[]{:S(2)}) copy-start(pred[2,32]{1,0:T(4,128)(4,1)S(1)} %compare_and_fusion.1) | copy-start | bytes 196
  45.2 299.2 %copy-start.26 = (pred[2,32]{1,0:T(4,128)(4,1)}, pred[2,32]{1,0:T(4,128)(4,1)S(1)}, u32[]{:S(2)}) copy-start(pred[2,32]{1,0:T(4,128)(4,1)S(1)} %get-tuple-element.132) | copy-start | bytes 196
  45.2 300.1 %copy-start.24 = (pred[2,32]{1,0:T(4,128)(4,1)}, pred[2,32]{1,0:T(4,128)(4,1)S(1)}, u32[]{:S(2)}) copy-start(pred[2,32]{1,0:T(4,128)(4,1)S(1)} %get-tuple-element.133) | copy-start | bytes 196
  47.8 8.1 %collective-permute-start.4 = (f32[3,36,2]{2,1,0:T(8,128)S(1)}, f32[3,36,2]{2,1,0:T(8,128)S(1)}, u32[]{:S(2)}, u32[]{:S(2)}) collective-permute-start(f32[3,36,2]{2,1,0:T(8,128)S(1)} %get-tuple-element.111), channel_id=1, source_target_pairs={{0,1},{1,2},{2,3},{3,4},{4,5},{5,6},{6,7},{7,8},{8,9},{9,10},{10,1... | collective-permute-start | bytes 2600 | tf_op jit(solution)/shard_map/ppermute | solution.py:17
  51.5 6.3 collective-permute-start.5
  53.5 0.6 copy-start.13
  53.5 0.6 copy-start.14
  53.5 0.6 copy-start.15
  54.8 1.1 copy-start.1
  55.9 589.9 %all-reduce.11.cloned.1.call-start = ((), (), s32[]{:S(2)}) async-start(), calls=%async_computation.1 | async-start | bytes 2211840
  58.1 0.6 copy-start.7
  348.4 0.7 copy-start.5
  348.4 1.1 copy-start.2
  349.7 11.9 %collective-permute-start.6 = (f32[1,6912]{1,0:T(1,128)S(1)}, f32[1,6912]{1,0:T(1,128)S(1)}, u32[]{:S(2)}, u32[]{:S(2)}) collective-permute-start(f32[1,6912]{1,0:T(1,128)S(1)} %broadcast_in_dim.577), channel_id=1, source_target_pairs={{0,32},{32,64},{64,96},{96,128},{128,160},{160,192},{192,224},{224... | collective-permute-start | bytes 82952 | tf_op jit(solution)/shard_map/ppermute | solution.py:17
  352.8 9.4 %collective-permute-start.7 = (f32[1,6912]{1,0:T(1,128)S(1)}, f32[1,6912]{1,0:T(1,128)S(1)}, u32[]{:S(2)}, u32[]{:S(2)}) collective-permute-start(f32[1,6912]{1,0:T(1,128)S(1)} %broadcast_in_dim.577), channel_id=1, source_target_pairs={{32,0},{64,32},{96,64},{128,96},{160,128},{192,160},{224,192},{256... | collective-permute-start | bytes 82952 | tf_op jit(solution)/shard_map/ppermute | solution.py:19
  363.0 1.1 copy-start
  364.1 392.5 %all-gather.6.cloned.1.call-start = ((), (), s32[]{:S(2)}) async-start(), calls=%async_computation.2 | async-start | bytes 3497472 | tf_op jit(solution)/shard_map/all_gather | solution.py:117
  647.4 1.4 copy-start.30
  657.3 0.8 copy-start.12
  657.4 0.8 copy-start.27
  658.7 0.7 copy-start.25
  659.0 1.0 copy-start.8
  661.1 0.9 copy-start.9
  661.1 1.0 copy-start.10
  661.1 1.1 copy-start.11
  661.2 1.2 copy-start.4
  661.2 1.2 copy-start.31
  663.4 14.4 %copy-start.6 = (f32[1,2,65,256]{3,2,1,0:T(8,128)S(1)}, f32[1,2,65,256]{3,2,1,0:T(8,128)}, u32[]{:S(2)}) copy-start(f32[1,2,65,256]{3,2,1,0:T(8,128)} %copy-done.5) | copy-start | bytes 399364
  678.8 11.8 %collective-permute-start.8 = (f32[1,2,2,3,128]{4,2,3,1,0:T(2,128)S(1)}, f32[1,2,2,3,128]{4,2,3,1,0:T(2,128)S(1)}, u32[]{:S(2)}, u32[]{:S(2)}) collective-permute-start(f32[1,2,2,3,128]{4,2,3,1,0:T(2,128)S(1)} %maximum_bitcast_fusion), channel_id=1, source_target_pairs={{0,32},{32,64},{64,96},{96,128},{128,160},{160,192},{192,224},{224... | collective-permute-start | bytes 18440 | tf_op jit(solution)/shard_map/ppermute | solution.py:17
  681.9 9.2 %collective-permute-start.9 = (f32[1,2,2,3,128]{4,2,3,1,0:T(2,128)S(1)}, f32[1,2,2,3,128]{4,2,3,1,0:T(2,128)S(1)}, u32[]{:S(2)}, u32[]{:S(2)}) collective-permute-start(f32[1,2,2,3,128]{4,2,3,1,0:T(2,128)S(1)} %maximum_bitcast_fusion), channel_id=1, source_target_pairs={{32,0},{64,32},{96,64},{128,96},{160,128},{192,160},{224,192},{256... | collective-permute-start | bytes 18440 | tf_op jit(solution)/shard_map/ppermute | solution.py:19
  692.0 18.0 %collective-permute-start.11 = (f32[3,2,128]{2,1,0:T(2,128)S(1)}, f32[3,2,128]{2,1,0:T(2,128)S(1)}, u32[]{:S(2)}, u32[]{:S(2)}) collective-permute-start(f32[3,2,128]{2,1,0:T(2,128)S(1)} %get-tuple-element.120), channel_id=1, source_target_pairs={{32,0},{64,32},{96,64},{128,96},{160,128},{192,160},{224,192},{256... | collective-permute-start | bytes 9224 | tf_op jit(solution)/shard_map/ppermute | solution.py:19
  701.6 10.5 %collective-permute-start.10 = (f32[3,2,128]{2,1,0:T(2,128)S(1)}, f32[3,2,128]{2,1,0:T(2,128)S(1)}, u32[]{:S(2)}, u32[]{:S(2)}) collective-permute-start(f32[3,2,128]{2,1,0:T(2,128)S(1)} %get-tuple-element.119), channel_id=1, source_target_pairs={{0,32},{32,64},{64,96},{96,128},{128,160},{160,192},{192,224},{224... | collective-permute-start | bytes 9224 | tf_op jit(solution)/shard_map/ppermute | solution.py:17
  712.2 9.6 %collective-permute-start.12 = (f32[3,36,2]{2,1,0:T(8,128)S(1)}, f32[3,36,2]{2,1,0:T(8,128)S(1)}, u32[]{:S(2)}, u32[]{:S(2)}) collective-permute-start(f32[3,36,2]{2,1,0:T(8,128)S(1)} %get-tuple-element.108), channel_id=1, source_target_pairs={{0,1},{1,2},{2,3},{3,4},{4,5},{5,6},{6,7},{7,8},{8,9},{9,10},{10,1... | collective-permute-start | bytes 2600 | tf_op jit(solution)/shard_map/ppermute | solution.py:17
  717.7 7.0 collective-permute-start.13
  721.7 3.1 copy-start.16
  721.7 3.1 copy-start.17
  721.7 3.1 copy-start.18
  725.6 33.1 %copy-start.22 = (pred[32,2]{1,0:T(8,128)(4,1)S(1)}, pred[32,2]{1,0:T(8,128)(4,1)}, u32[]{:S(2)}) copy-start(pred[32,2]{1,0:T(8,128)(4,1)} %eq.380) | copy-start | bytes 196
  759.0 1.4 copy-start.19
  759.0 1.4 copy-start.20
Sparse Core Ops, SparseCore 0:
  56.0 283.9 all-reduce.8
  364.2 281.5 all-reduce.10
  692.1 64.4 all-gather.5

commit v2 on v1

--- a/solution.py
+++ b/solution.py
@@ -113,7 +113,8 @@
 
 
 def gather_rows(parts):
-    flat = jnp.concatenate([part.reshape(-1) for part in parts])[None]
+    flat = jnp.concatenate([part.reshape(-1) for part in parts])
+    flat = jnp.pad(flat, (0, -flat.size % 1024))[None]
     rows = lax.all_gather(flat, "gy", axis=0, tiled=True)
     count = rows.shape[0]
     out = []

time: 783 us -> 330 us (0.42)
  waiting for transfers between devices: 600 us -> 150 us
    unnamed x5 -> x3, waiting for transfers between devices: 561 us -> 0.05 us
    all_gather x1 -> x3, waiting for transfers between devices: 30.9 us -> 139 us  [gather_rows(): rows = lax.all_gather(flat, 'gy', axis=0, tiled=True)]
  transfers between devices with their start and end apart: 17 -> 17, of which waited for: 8 -> 8; matrix products, arithmetic and copies ran while one was open for 3% -> 6% of each run, Pallas kernels for 0% -> 0%
where the time goes in v2:
time: 330 us; the launch traced here: 329 us
  waiting for transfers between devices  150 us (45%)
  starting transfers between devices  76.2 us (23%)
  local copies, waits for them, and re-layouts  55.8 us (17%)
  other arithmetic  31.2 us (9%)
  between operations  15.5 us (5%)
    all_gather x3, waiting for transfers between devices, gather_rows(): rows = lax.all_gather(flat, 'gy', axis=0, tiled=True)  139 us
    ppermute x7, starting transfers between devices, extended(): lax.ppermute(head, axis, [((i + 1) % count, i) for i in range(count)])  51.4 us
    ppermute x7, starting transfers between devices, extended(): lax.ppermute(tail, axis, [(i, (i + 1) % count) for i in range(count)])  24.5 us
    ppermute x7, waiting for transfers between devices, extended(): lax.ppermute(head, axis, [((i + 1) % count, i) for i in range(count)])  8.55 us
    reduce_sum x8, other arithmetic, select(): jnp.sum(jnp.where(hit_mask.reshape(hit_mask.shape + extra), payload, 0.0)...  7.01 us
  transfers between devices with their start and end apart: 17, of which 8 were waited for; matrix products, arithmetic and copies ran while one was open for 6% of the time, Pallas kernels for 0%

profile of v2, /device:TPU:1, one launch (start us, length us, event | category | flops | bytes accessed | tf_op | source)
XLA Modules:
  0.0 328.6 jit_solution(4780845393062428173)
XLA Ops:
  7.2 0.7 slice_reduce_fusion.11
  8.0 1.0 copy.357
  9.1 4.8 %collective-permute-start = (f32[1,6912]{1,0:T(1,128)S(1)}, f32[1,6912]{1,0:T(1,128)S(1)}, u32[]{:S(2)}, u32[]{:S(2)}) collective-permute-start(f32[1,6912]{1,0:T(1,128)S(1)} %broadcast_in_dim.536), channel_id=1, source_target_pairs={{0,32},{32,64},{64,96},{96,128},{128,160},{160,192},{192,224},{224... | collective-permute-start | bytes 82952 | tf_op jit(solution)/shard_map/ppermute | solution.py:17
  13.9 17.5 %collective-permute-start.1 = (f32[1,6912]{1,0:T(1,128)S(1)}, f32[1,6912]{1,0:T(1,128)S(1)}, u32[]{:S(2)}, u32[]{:S(2)}) collective-permute-start(f32[1,6912]{1,0:T(1,128)S(1)} %broadcast_in_dim.536), channel_id=1, source_target_pairs={{32,0},{64,32},{96,64},{128,96},{160,128},{192,160},{224,192},{256... | collective-permute-start | bytes 82952 | tf_op jit(solution)/shard_map/ppermute | solution.py:19
  31.4 0.7 fusion.122
  32.2 3.4 %collective-permute-start.3 = (f32[3,2,128]{2,1,0:T(2,128)S(1)}, f32[3,2,128]{2,1,0:T(2,128)S(1)}, u32[]{:S(2)}, u32[]{:S(2)}) collective-permute-start(f32[3,2,128]{2,1,0:T(2,128)S(1)} %get-tuple-element.122), channel_id=1, source_target_pairs={{32,0},{64,32},{96,64},{128,96},{160,128},{192,160},{224,192},{256... | collective-permute-start | bytes 9224 | tf_op jit(solution)/shard_map/ppermute | solution.py:19
  35.5 1.9 collective-permute-start.2
  38.7 0.6 gather_fusion.5
  46.7 4.1 %collective-permute-start.4 = (f32[3,36,2]{2,1,0:T(8,128)S(1)}, f32[3,36,2]{2,1,0:T(8,128)S(1)}, u32[]{:S(2)}, u32[]{:S(2)}) collective-permute-start(f32[3,36,2]{2,1,0:T(8,128)S(1)} %get-tuple-element.111), channel_id=1, source_target_pairs={{0,1},{1,2},{2,3},{3,4},{4,5},{5,6},{6,7},{7,8},{8,9},{9,10},{10,1... | collective-permute-start | bytes 2600 | tf_op jit(solution)/shard_map/ppermute | solution.py:17
  50.8 1.9 collective-permute-start.5
  53.4 3.7 %collective-permute-done.5 = f32[3,36,2]{2,1,0:T(8,128)S(1)} collective-permute-done((f32[3,36,2]{2,1,0:T(8,128)S(1)}, f32[3,36,2]{2,1,0:T(8,128)S(1)}, u32[]{:S(2)}, u32[]{:S(2)}) %collective-permute-start.5) | collective-permute-done | bytes 896 | tf_op jit(solution)/shard_map/ppermute | solution.py:19
  58.6 49.2 %all-gather.7.cloned.1.call-done = f32[294912]{0:T(1024)} async-done(((f32[9216]{0:T(1024)}), f32[294912]{0:T(1024)}) %all-gather.7.cloned.1.call-update) | async-done | bytes 1179664 | tf_op jit(solution)/shard_map/all_gather | solution.py:118
  107.8 1.4 reshape.1038
  113.6 0.8 fusion.6
  117.5 3.3 collective-permute-start.6
  120.7 8.5 %collective-permute-start.7 = (f32[1,6912]{1,0:T(1,128)S(1)}, f32[1,6912]{1,0:T(1,128)S(1)}, u32[]{:S(2)}, u32[]{:S(2)}) collective-permute-start(f32[1,6912]{1,0:T(1,128)S(1)} %broadcast_in_dim.577), channel_id=1, source_target_pairs={{32,0},{64,32},{96,64},{128,96},{160,128},{192,160},{224,192},{256... | collective-permute-start | bytes 82952 | tf_op jit(solution)/shard_map/ppermute | solution.py:19
  131.2 0.7 compare_bitcast_fusion
  131.9 0.8 fusion.107
  132.7 58.5 %all-gather.9.cloned.1.call-done = f32[294912]{0:T(1024)} async-done(((f32[9216]{0:T(1024)}), f32[294912]{0:T(1024)}) %all-gather.9.cloned.1.call-update) | async-done | bytes 1179664 | tf_op jit(solution)/shard_map/all_gather | solution.py:118
  191.2 1.4 reshape.1039
  192.6 0.7 fusion.111
  193.3 0.7 fusion.110
  194.3 0.8 select_reduce_fusion.5
  195.2 0.8 broadcast_in_dim.588
  196.0 0.7 select_reduce_fusion.11
  197.1 1.1 copy.271
  198.1 0.8 copy.272
  199.0 1.1 select_reduce_fusion.4
  200.0 0.8 broadcast_in_dim.595
  200.8 0.7 select_reduce_fusion.10
  202.8 0.7 fusion.23
  203.5 0.8 fusion.26
  204.3 0.8 copy.278
  209.8 0.8 copy-done.7
  211.0 0.9 select_bitcast_fusion
  211.9 3.4 %slice.689 = f32[2,3,32,128]{3,2,1,0:T(8,128)S(1)} slice(f32[2,3,64,256]{3,2,1,0:T(8,128)S(1)} %get-tuple-element.32), slice={[0:2:1], [0:3:1], [0:64:2], [1:256:2]} | slice | bytes 196608 | tf_op jit(solution)/shard_map/slice | solution.py:91
  215.3 3.4 %slice.690 = f32[2,3,32,128]{3,2,1,0:T(8,128)S(1)} slice(f32[2,3,64,256]{3,2,1,0:T(8,128)S(1)} %get-tuple-element.32), slice={[0:2:1], [0:3:1], [1:64:2], [1:256:2]} | slice | bytes 196608 | tf_op jit(solution)/shard_map/slice | solution.py:91
  218.8 3.4 %slice.687 = f32[2,3,32,128]{3,2,1,0:T(8,128)S(1)} slice(f32[2,3,64,256]{3,2,1,0:T(8,128)S(1)} %get-tuple-element.32), slice={[0:2:1], [0:3:1], [0:64:2], [0:256:2]} | slice | bytes 196608 | tf_op jit(solution)/shard_map/slice | solution.py:89
  222.2 3.4 %slice.688 = f32[2,3,32,128]{3,2,1,0:T(8,128)S(1)} slice(f32[2,3,64,256]{3,2,1,0:T(8,128)S(1)} %get-tuple-element.32), slice={[0:2:1], [0:3:1], [1:64:2], [0:256:2]} | slice | bytes 196608 | tf_op jit(solution)/shard_map/slice | solution.py:90
  227.4 3.3 %collective-permute-start.8 = (f32[1,2,2,3,128]{4,2,3,1,0:T(2,128)S(1)}, f32[1,2,2,3,128]{4,2,3,1,0:T(2,128)S(1)}, u32[]{:S(2)}, u32[]{:S(2)}) collective-permute-start(f32[1,2,2,3,128]{4,2,3,1,0:T(2,128)S(1)} %maximum_bitcast_fusion), channel_id=1, source_target_pairs={{0,32},{32,64},{64,96},{96,128},{128,160},{160,192},{192,224},{224... | collective-permute-start | bytes 18440 | tf_op jit(solution)/shard_map/ppermute | solution.py:17
  230.7 8.5 %collective-permute-start.9 = (f32[1,2,2,3,128]{4,2,3,1,0:T(2,128)S(1)}, f32[1,2,2,3,128]{4,2,3,1,0:T(2,128)S(1)}, u32[]{:S(2)}, u32[]{:S(2)}) collective-permute-start(f32[1,2,2,3,128]{4,2,3,1,0:T(2,128)S(1)} %maximum_bitcast_fusion), channel_id=1, source_target_pairs={{32,0},{64,32},{96,64},{128,96},{160,128},{192,160},{224,192},{256... | collective-permute-start | bytes 18440 | tf_op jit(solution)/shard_map/ppermute | solution.py:19
  240.1 0.7 pad.17
  240.8 9.6 %collective-permute-start.11 = (f32[3,2,128]{2,1,0:T(2,128)S(1)}, f32[3,2,128]{2,1,0:T(2,128)S(1)}, u32[]{:S(2)}, u32[]{:S(2)}) collective-permute-start(f32[3,2,128]{2,1,0:T(2,128)S(1)} %get-tuple-element.120), channel_id=1, source_target_pairs={{32,0},{64,32},{96,64},{128,96},{160,128},{192,160},{224,192},{256... | collective-permute-start | bytes 9224 | tf_op jit(solution)/shard_map/ppermute | solution.py:19
  250.4 1.9 collective-permute-start.10
  252.8 0.7 broadcast_in_dim.611
  253.7 0.7 broadcast_in_dim.616
  254.7 0.7 broadcast_in_dim.618
  255.6 0.7 broadcast_in_dim.623
  257.5 0.7 fusion.123
  258.2 2.7 collective-permute-done.10
  261.0 5.2 %collective-permute-start.12 = (f32[3,36,2]{2,1,0:T(8,128)S(1)}, f32[3,36,2]{2,1,0:T(8,128)S(1)}, u32[]{:S(2)}, u32[]{:S(2)}) collective-permute-start(f32[3,36,2]{2,1,0:T(8,128)S(1)} %get-tuple-element.108), channel_id=1, source_target_pairs={{0,1},{1,2},{2,3},{3,4},{4,5},{5,6},{6,7},{7,8},{8,9},{9,10},{10,1... | collective-permute-start | bytes 2600 | tf_op jit(solution)/shard_map/ppermute | solution.py:17
  266.2 1.9 collective-permute-start.13
  268.8 3.8 %collective-permute-done.13 = f32[3,36,2]{2,1,0:T(8,128)S(1)} collective-permute-done((f32[3,36,2]{2,1,0:T(8,128)S(1)}, f32[3,36,2]{2,1,0:T(8,128)S(1)}, u32[]{:S(2)}, u32[]{:S(2)}) %collective-permute-start.13) | collective-permute-done | bytes 896 | tf_op jit(solution)/shard_map/ppermute | solution.py:19
  273.6 30.8 %all-gather.11.cloned.1.call-done = f32[851968]{0:T(1024)} async-done(((f32[26624]{0:T(1024)}), f32[851968]{0:T(1024)}) %all-gather.11.cloned.1.call-update) | async-done | bytes 3407888 | tf_op jit(solution)/shard_map/all_gather | solution.py:118
  304.4 2.2 reshape.1040
  307.0 1.4 fusion
  308.4 1.5 reduce_sum.260
  309.9 0.8 fusion.44
  311.3 1.3 reduce_sum.263
  313.2 1.3 fusion.73
  314.6 0.7 reduce_sum.270
  315.6 1.9 broadcast_select_fusion.1
  317.5 2.2 fusion.61
  319.8 2.3 fusion.68
  (336 shorter events, 34.2 us)
Async XLA Ops:
  7.2 30.5 %copy-start.20 = (s32[24,64]{1,0:T(8,128)S(1)}, s32[24,64]{1,0:T(8,128)}, u32[]{:S(2)}) copy-start(s32[24,64]{1,0:T(8,128)} %param.5) | copy-start | bytes 18436
  7.2 100.6 %all-gather.7.cloned.1.call-start = ((), (), s32[]{:S(2)}) async-start(), calls=%async_computation | async-start | bytes 1216512 | tf_op jit(solution)/shard_map/all_gather | solution.py:118
  9.1 36.6 %collective-permute-start = (f32[1,6912]{1,0:T(1,128)S(1)}, f32[1,6912]{1,0:T(1,128)S(1)}, u32[]{:S(2)}, u32[]{:S(2)}) collective-permute-start(f32[1,6912]{1,0:T(1,128)S(1)} %broadcast_in_dim.536), channel_id=1, source_target_pairs={{0,32},{32,64},{64,96},{96,128},{128,160},{160,192},{192,224},{224... | collective-permute-start | bytes 82952 | tf_op jit(solution)/shard_map/ppermute | solution.py:17
  13.9 31.8 %collective-permute-start.1 = (f32[1,6912]{1,0:T(1,128)S(1)}, f32[1,6912]{1,0:T(1,128)S(1)}, u32[]{:S(2)}, u32[]{:S(2)}) collective-permute-start(f32[1,6912]{1,0:T(1,128)S(1)} %broadcast_in_dim.536), channel_id=1, source_target_pairs={{32,0},{64,32},{96,64},{128,96},{160,128},{192,160},{224,192},{256... | collective-permute-start | bytes 82952 | tf_op jit(solution)/shard_map/ppermute | solution.py:19
  32.2 14.4 %collective-permute-start.3 = (f32[3,2,128]{2,1,0:T(2,128)S(1)}, f32[3,2,128]{2,1,0:T(2,128)S(1)}, u32[]{:S(2)}, u32[]{:S(2)}) collective-permute-start(f32[3,2,128]{2,1,0:T(2,128)S(1)} %get-tuple-element.122), channel_id=1, source_target_pairs={{32,0},{64,32},{96,64},{128,96},{160,128},{192,160},{224,192},{256... | collective-permute-start | bytes 9224 | tf_op jit(solution)/shard_map/ppermute | solution.py:19
  35.5 11.1 %collective-permute-start.2 = (f32[3,2,128]{2,1,0:T(2,128)S(1)}, f32[3,2,128]{2,1,0:T(2,128)S(1)}, u32[]{:S(2)}, u32[]{:S(2)}) collective-permute-start(f32[3,2,128]{2,1,0:T(2,128)S(1)} %get-tuple-element.121), channel_id=1, source_target_pairs={{0,32},{32,64},{64,96},{96,128},{128,160},{160,192},{192,224},{224... | collective-permute-start | bytes 9224 | tf_op jit(solution)/shard_map/ppermute | solution.py:17
  41.3 3.8 %copy-start.1 = (f32[3,32,128]{2,1,0:T(8,128)S(1)}, f32[3,32,128]{2,1,0:T(8,128)}, u32[]{:S(2)}) copy-start(f32[3,32,128]{2,1,0:T(8,128)} %param.3) | copy-start | bytes 147460
  44.6 65.7 %copy-start.27 = (pred[2,32,2]{1,2,0:T(4,128)(4,1)}, pred[2,32,2]{1,2,0:T(4,128)(4,1)S(1)}, u32[]{:S(2)}) copy-start(pred[2,32,2]{1,2,0:T(4,128)(4,1)S(1)} %and_and_fusion.1) | copy-start | bytes 388
  44.7 65.3 %copy-start.33 = (pred[2,32]{1,0:T(4,128)(4,1)}, pred[2,32]{1,0:T(4,128)(4,1)S(1)}, u32[]{:S(2)}) copy-start(pred[2,32]{1,0:T(4,128)(4,1)S(1)} %compare_and_fusion) | copy-start | bytes 196
  44.7 66.6 %copy-start.28 = (pred[2,32,2]{1,2,0:T(4,128)(4,1)}, pred[2,32,2]{1,2,0:T(4,128)(4,1)S(1)}, u32[]{:S(2)}) copy-start(pred[2,32,2]{1,2,0:T(4,128)(4,1)S(1)} %and_and_fusion.2) | copy-start | bytes 388
  44.8 66.2 %copy-start.34 = (pred[2,32]{1,0:T(4,128)(4,1)}, pred[2,32]{1,0:T(4,128)(4,1)S(1)}, u32[]{:S(2)}) copy-start(pred[2,32]{1,0:T(4,128)(4,1)S(1)} %compare_and_fusion.1) | copy-start | bytes 196
  44.9 69.6 %copy-start.25 = (pred[2,32,2]{1,2,0:T(4,128)(4,1)}, pred[2,32,2]{1,2,0:T(4,128)(4,1)S(1)}, u32[]{:S(2)}) copy-start(pred[2,32,2]{1,2,0:T(4,128)(4,1)S(1)} %and_and_fusion.3) | copy-start | bytes 388
  45.0 69.7 %copy-start.23 = (pred[2,32,2]{1,2,0:T(4,128)(4,1)}, pred[2,32,2]{1,2,0:T(4,128)(4,1)S(1)}, u32[]{:S(2)}) copy-start(pred[2,32,2]{1,2,0:T(4,128)(4,1)S(1)} %and_and_fusion) | copy-start | bytes 388
  45.1 67.0 %copy-start.31 = (pred[2,32]{1,0:T(4,128)(4,1)}, pred[2,32]{1,0:T(4,128)(4,1)S(1)}, u32[]{:S(2)}) copy-start(pred[2,32]{1,0:T(4,128)(4,1)S(1)} %get-tuple-element.132) | copy-start | bytes 196
  45.1 68.0 %copy-start.29 = (pred[2,32]{1,0:T(4,128)(4,1)}, pred[2,32]{1,0:T(4,128)(4,1)S(1)}, u32[]{:S(2)}) copy-start(pred[2,32]{1,0:T(4,128)(4,1)S(1)} %get-tuple-element.133) | copy-start | bytes 196
  46.5 144.6 %all-gather.9.cloned.1.call-start = ((), (), s32[]{:S(2)}) async-start(), calls=%async_computation.1 | async-start | bytes 1216512 | tf_op jit(solution)/shard_map/all_gather | solution.py:118
  46.7 6.2 %collective-permute-start.4 = (f32[3,36,2]{2,1,0:T(8,128)S(1)}, f32[3,36,2]{2,1,0:T(8,128)S(1)}, u32[]{:S(2)}, u32[]{:S(2)}) collective-permute-start(f32[3,36,2]{2,1,0:T(8,128)S(1)} %get-tuple-element.111), channel_id=1, source_target_pairs={{0,1},{1,2},{2,3},{3,4},{4,5},{5,6},{6,7},{7,8},{8,9},{9,10},{10,1... | collective-permute-start | bytes 2600 | tf_op jit(solution)/shard_map/ppermute | solution.py:17
  50.8 6.3 %collective-permute-start.5 = (f32[3,36,2]{2,1,0:T(8,128)S(1)}, f32[3,36,2]{2,1,0:T(8,128)S(1)}, u32[]{:S(2)}, u32[]{:S(2)}) collective-permute-start(f32[3,36,2]{2,1,0:T(8,128)S(1)} %get-tuple-element.112), channel_id=1, source_target_pairs={{1,0},{2,1},{3,2},{4,3},{5,4},{6,5},{7,6},{8,7},{9,8},{10,9},{11,1... | collective-permute-start | bytes 2600 | tf_op jit(solution)/shard_map/ppermute | solution.py:19
  52.8 0.6 copy-start.16
  52.8 4.6 %copy-start.12 = (f32[1,33,128]{2,1,0:T(8,128)}, f32[1,33,128]{2,1,0:T(8,128)S(1)}, u32[]{:S(2)}) copy-start(f32[1,33,128]{2,1,0:T(8,128)S(1)} %get-tuple-element.101) | copy-start | bytes 50692
  52.9 4.6 %copy-start.14 = (f32[1,33,128]{2,1,0:T(8,128)}, f32[1,33,128]{2,1,0:T(8,128)S(1)}, u32[]{:S(2)}) copy-start(f32[1,33,128]{2,1,0:T(8,128)S(1)} %get-tuple-element.102) | copy-start | bytes 50692
  57.5 0.6 copy-start.5
  114.9 0.6 copy-start.21
  116.1 0.7 copy-start.3
  116.1 1.1 copy-start
  117.5 12.2 %collective-permute-start.6 = (f32[1,6912]{1,0:T(1,128)S(1)}, f32[1,6912]{1,0:T(1,128)S(1)}, u32[]{:S(2)}, u32[]{:S(2)}) collective-permute-start(f32[1,6912]{1,0:T(1,128)S(1)} %broadcast_in_dim.577), channel_id=1, source_target_pairs={{0,32},{32,64},{64,96},{96,128},{128,160},{160,192},{192,224},{224... | collective-permute-start | bytes 82952 | tf_op jit(solution)/shard_map/ppermute | solution.py:17
  120.7 9.5 %collective-permute-start.7 = (f32[1,6912]{1,0:T(1,128)S(1)}, f32[1,6912]{1,0:T(1,128)S(1)}, u32[]{:S(2)}, u32[]{:S(2)}) collective-permute-start(f32[1,6912]{1,0:T(1,128)S(1)} %broadcast_in_dim.577), channel_id=1, source_target_pairs={{32,0},{64,32},{96,64},{128,96},{160,128},{192,160},{224,192},{256... | collective-permute-start | bytes 82952 | tf_op jit(solution)/shard_map/ppermute | solution.py:19
  131.0 173.5 %all-gather.11.cloned.1.call-start = ((), (), s32[]{:S(2)}) async-start(), calls=%async_computation.2 | async-start | bytes 3514368 | tf_op jit(solution)/shard_map/all_gather | solution.py:118
  205.8 0.7 copy-start.26
  205.8 0.8 copy-start.11
  205.8 0.8 copy-start.32
  206.8 0.9 copy-start.24
  207.0 0.9 copy-start.10
  207.0 0.9 copy-start.30
  207.6 0.9 copy-start.22
  207.6 1.0 copy-start.6
  209.6 0.9 copy-start.7
  209.7 1.0 copy-start.8
  209.7 1.1 copy-start.9
  209.7 1.2 copy-start.2
  209.7 1.2 copy-start.35
  211.9 14.4 %copy-start.4 = (f32[1,2,65,256]{3,2,1,0:T(8,128)S(1)}, f32[1,2,65,256]{3,2,1,0:T(8,128)}, u32[]{:S(2)}) copy-start(f32[1,2,65,256]{3,2,1,0:T(8,128)} %copy-done.3) | copy-start | bytes 399364
  227.4 12.1 %collective-permute-start.8 = (f32[1,2,2,3,128]{4,2,3,1,0:T(2,128)S(1)}, f32[1,2,2,3,128]{4,2,3,1,0:T(2,128)S(1)}, u32[]{:S(2)}, u32[]{:S(2)}) collective-permute-start(f32[1,2,2,3,128]{4,2,3,1,0:T(2,128)S(1)} %maximum_bitcast_fusion), channel_id=1, source_target_pairs={{0,32},{32,64},{64,96},{96,128},{128,160},{160,192},{192,224},{224... | collective-permute-start | bytes 18440 | tf_op jit(solution)/shard_map/ppermute | solution.py:17
  230.7 9.3 %collective-permute-start.9 = (f32[1,2,2,3,128]{4,2,3,1,0:T(2,128)S(1)}, f32[1,2,2,3,128]{4,2,3,1,0:T(2,128)S(1)}, u32[]{:S(2)}, u32[]{:S(2)}) collective-permute-start(f32[1,2,2,3,128]{4,2,3,1,0:T(2,128)S(1)} %maximum_bitcast_fusion), channel_id=1, source_target_pairs={{32,0},{64,32},{96,64},{128,96},{160,128},{192,160},{224,192},{256... | collective-permute-start | bytes 18440 | tf_op jit(solution)/shard_map/ppermute | solution.py:19
  240.8 17.4 %collective-permute-start.11 = (f32[3,2,128]{2,1,0:T(2,128)S(1)}, f32[3,2,128]{2,1,0:T(2,128)S(1)}, u32[]{:S(2)}, u32[]{:S(2)}) collective-permute-start(f32[3,2,128]{2,1,0:T(2,128)S(1)} %get-tuple-element.120), channel_id=1, source_target_pairs={{32,0},{64,32},{96,64},{128,96},{160,128},{192,160},{224,192},{256... | collective-permute-start | bytes 9224 | tf_op jit(solution)/shard_map/ppermute | solution.py:19
  250.4 10.5 %collective-permute-start.10 = (f32[3,2,128]{2,1,0:T(2,128)S(1)}, f32[3,2,128]{2,1,0:T(2,128)S(1)}, u32[]{:S(2)}, u32[]{:S(2)}) collective-permute-start(f32[3,2,128]{2,1,0:T(2,128)S(1)} %get-tuple-element.119), channel_id=1, source_target_pairs={{0,32},{32,64},{64,96},{96,128},{128,160},{160,192},{192,224},{224... | collective-permute-start | bytes 9224 | tf_op jit(solution)/shard_map/ppermute | solution.py:17
  261.0 7.8 %collective-permute-start.12 = (f32[3,36,2]{2,1,0:T(8,128)S(1)}, f32[3,36,2]{2,1,0:T(8,128)S(1)}, u32[]{:S(2)}, u32[]{:S(2)}) collective-permute-start(f32[3,36,2]{2,1,0:T(8,128)S(1)} %get-tuple-element.108), channel_id=1, source_target_pairs={{0,1},{1,2},{2,3},{3,4},{4,5},{5,6},{6,7},{7,8},{8,9},{9,10},{10,1... | collective-permute-start | bytes 2600 | tf_op jit(solution)/shard_map/ppermute | solution.py:17
  266.2 6.5 %collective-permute-start.13 = (f32[3,36,2]{2,1,0:T(8,128)S(1)}, f32[3,36,2]{2,1,0:T(8,128)S(1)}, u32[]{:S(2)}, u32[]{:S(2)}) collective-permute-start(f32[3,36,2]{2,1,0:T(8,128)S(1)} %get-tuple-element.109), channel_id=1, source_target_pairs={{1,0},{2,1},{3,2},{4,3},{5,4},{6,5},{7,6},{8,7},{9,8},{10,9},{11,1... | collective-permute-start | bytes 2600 | tf_op jit(solution)/shard_map/ppermute | solution.py:19
  268.2 0.7 copy-start.17
  268.2 0.7 copy-start.18
  268.2 0.7 copy-start.19
  307.0 8.6 %copy-start.13 = (f32[1,33,128]{2,1,0:T(8,128)S(1)}, f32[1,33,128]{2,1,0:T(8,128)}, u32[]{:S(2)}) copy-start(f32[1,33,128]{2,1,0:T(8,128)} %copy-done.12) | copy-start | bytes 50692
  307.0 8.6 %copy-start.15 = (f32[1,33,128]{2,1,0:T(8,128)S(1)}, f32[1,33,128]{2,1,0:T(8,128)}, u32[]{:S(2)}) copy-start(f32[1,33,128]{2,1,0:T(8,128)} %copy-done.14) | copy-start | bytes 50692
Sparse Core Ops, SparseCore 0:
  46.6 61.0 all-gather.6
  131.1 60.0 all-gather.8
  240.9 63.5 all-gather.10

commit v3 on v2

--- a/solution.py
+++ b/solution.py
@@ -164,53 +164,153 @@
     rate_two, flux_x2, flux_y2 = advance_rate(coarse_margin(coarse_one), LAM_COARSE)
     coarse_heun = 0.5 * (coarse_state + coarse_one + rate_two)
 
-    def fine_rates(field, coarse_now):
-        strip_left = field[:, :, :2, :]
-        strip_right = field[:, :, -2:, :]
-        strip_low = field[..., :2]
-        strip_high = field[..., -2:]
-        edge_left = coarse_now[:, 0, :]
-        edge_right = coarse_now[:, -1, :]
-        edge_low = coarse_now[:, :, 0]
-        edge_high = coarse_now[:, :, -1]
-        strip_size = strip_left.size
-        edge_size = edge_left.size
-        side_pack = jnp.concatenate(
-            [
-                strip_right.reshape(-1),
-                edge_right.reshape(-1),
-                strip_left.reshape(-1),
-                edge_left.reshape(-1),
-            ]
-        )[None]
-        sides = extended(side_pack, (("gx", 0),), 1)
-        from_left = sides[0]
-        from_right = sides[2]
-        left_strips = from_left[:strip_size].reshape(strip_right.shape)
-        left_edges = from_left[strip_size : strip_size + edge_size].reshape(edge_right.shape)
-        right_strips = from_right[strip_size + edge_size : 2 * strip_size + edge_size].reshape(
-            strip_left.shape
+    def pick(gathered, source):
+        flag, fine_row, fine_sub, _ = source
+        row_index = jnp.arange(gathered.shape[0], dtype=jnp.int32)
+        sub_index = jnp.arange(gathered.shape[1], dtype=jnp.int32)
+        hit_mask = (
+            (row_index[None, :, None] == fine_row[:, None, None])
+            & (sub_index[None, None, :] == fine_sub[:, None, None])
+            & flag[:, None, None]
         )
-        right_edges = from_right[2 * strip_size + edge_size :].reshape(edge_left.shape)
-        pieces = gather_rows(
-            (left_strips, left_edges, right_strips, right_edges, strip_high, edge_high, strip_low, edge_low)
+        extra = (1,) * (gathered.ndim - 2)
+        return jnp.sum(jnp.where(hit_mask.reshape(hit_mask.shape + extra), gathered[None], 0.0), axis=(1, 2))
+
+    def pick_edge(edges, source):
+        flag, _, _, edge_row = source
+        row_index = jnp.arange(edges.shape[0], dtype=jnp.int32)
+        edge_mask = (row_index[None, :] == edge_row[:, None]) & jnp.logical_not(flag)[:, None]
+        extra = (1,) * (edges.ndim - 1)
+        return jnp.sum(jnp.where(edge_mask.reshape(edge_mask.shape + extra), edges[None], 0.0), axis=1)
+
+    right_pack = jnp.concatenate(
+        [fine_box[:, :, -4:, :].reshape(-1), coarse_state[:, -1, :].reshape(-1), coarse_one[:, -1, :].reshape(-1)]
+    )
+    left_pack = jnp.concatenate(
+        [fine_box[:, :, :4, :].reshape(-1), coarse_state[:, 0, :].reshape(-1), coarse_one[:, 0, :].reshape(-1)]
+    )
+    from_left = lax.ppermute(right_pack, "gx", [(i, (i + 1) % count_x) for i in range(count_x)])
+    from_right = lax.ppermute(left_pack, "gx", [((i + 1) % count_x, i) for i in range(count_x)])
+    side_strip_shape = fine_box[:, :, :4, :].shape
+    side_strip_size = fine_box[:, :, :4, :].size
+    edge_x_shape = coarse_state[:, 0, :].shape
+    edge_x_size = coarse_state[:, 0, :].size
+    gathered = gather_rows(
+        (
+            from_left[:side_strip_size].reshape(side_strip_shape),
+            from_left[side_strip_size : side_strip_size + edge_x_size].reshape(edge_x_shape),
+            from_left[side_strip_size + edge_x_size :].reshape(edge_x_shape),
+            from_right[:side_strip_size].reshape(side_strip_shape),
+            from_right[side_strip_size : side_strip_size + edge_x_size].reshape(edge_x_shape),
+            from_right[side_strip_size + edge_x_size :].reshape(edge_x_shape),
+            fine_box[..., -4:],
+            fine_box[..., :4],
+            coarse_state[:, :, -1],
+            coarse_state[:, :, 0],
+            coarse_one[:, :, -1],
+            coarse_one[:, :, 0],
         )
-        row_index = jnp.arange(pieces[0].shape[0], dtype=jnp.int32)
-        fine_l, edge_l = pick_from(row_index, pieces[0], pieces[1], targets_left)
-        fine_r, edge_r = pick_from(row_index, pieces[2], pieces[3], targets_right)
-        fine_lo, edge_lo = pick_from(row_index, pieces[4], pieces[5], targets_low)
-        fine_hi, edge_hi = pick_from(row_index, pieces[6], pieces[7], targets_high)
-        parts = (fine_l, edge_l, fine_r, edge_r, fine_lo, edge_lo, fine_hi, edge_hi)
-        picked = tuple((extra for extra in parts))
-        ghost_left = picked[0] + inject_side(picked[1])
-        ghost_right = picked[2] + inject_side(picked[3])
-        ghost_low = picked[4] + inject_end(picked[5])
-        ghost_high = picked[6] + inject_end(picked[7])
-        return jax.vmap(fine_section)(field, ghost_left, ghost_right, ghost_low, ghost_high)
-
-    rate_f1, left_one, right_one, low_one, high_one = fine_rates(fine_box, coarse_state)
+    )
+    (
+        left_strips,
+        left_edges,
+        left_edges_one,
+        right_strips,
+        right_edges,
+        right_edges_one,
+        high_strips,
+        low_strips,
+        high_edges,
+        low_edges,
+        high_edges_one,
+        low_edges_one,
+    ) = gathered
+    targets_left_low = fine_source(column_left, (parent - 1) % count_y)
+    targets_left_high = fine_source(column_left, (parent + 1) % count_y)
+    targets_right_low = fine_source(column_right, (parent - 1) % count_y)
+    targets_right_high = fine_source(column_right, (parent + 1) % count_y)
+
+    def corner(strips, edges, source, rows, cols, edge_index):
+        fine_part = pick(strips[:, :, :, rows[0] : rows[1], cols[0] : cols[1]], source)
+        edge_part = pick_edge(edges[:, :, edge_index], source)
+        return fine_part + edge_part[:, :, None, None]
+
+    corner_left_low = corner(left_strips, left_edges, targets_left_low, (2, 4), (-2, None), -1)
+    corner_left_high = corner(left_strips, left_edges, targets_left_high, (2, 4), (0, 2), 0)
+    corner_right_low = corner(right_strips, right_edges, targets_right_low, (0, 2), (-2, None), -1)
+    corner_right_high = corner(right_strips, right_edges, targets_right_high, (0, 2), (0, 2), 0)
+
+    wide_left = pick(left_strips, targets_left)
+    wide_right = pick(right_strips, targets_right)
+    wide_low = pick(high_strips, targets_low)
+    wide_high = pick(low_strips, targets_high)
+    ghost_left = wide_left[:, :, 2:, :] + inject_side(pick_edge(left_edges, targets_left))
+    ghost_right = wide_right[:, :, :2, :] + inject_side(pick_edge(right_edges, targets_right))
+    ghost_low = wide_low[..., 2:] + inject_end(pick_edge(high_edges, targets_low))
+    ghost_high = wide_high[..., :2] + inject_end(pick_edge(low_edges, targets_high))
+    rate_f1, left_one, right_one, low_one, high_one = jax.vmap(fine_section)(
+        fine_box, ghost_left, ghost_right, ghost_low, ghost_high
+    )
     fine_one = fine_box + rate_f1
-    rate_f2, left_two, right_two, low_two, high_two = fine_rates(fine_one, coarse_one)
+
+    def rim_rate(padded):
+        return advance_rate(padded, LAM_FINE)[0]
+
+    zero_pair = jnp.zeros(fine_box.shape[:2] + (2, 2), jnp.float32)
+
+    def rows_of(low_end, middle, high_end):
+        return jnp.concatenate([low_end, middle, high_end], axis=3)
+
+    def cols_of(low_end, middle, high_end):
+        return jnp.concatenate([low_end, middle, high_end], axis=2)
+
+    padded_left = jnp.concatenate(
+        [
+            rows_of(zero_pair, wide_left[:, :, :2, :], zero_pair),
+            rows_of(corner_left_low, wide_left[:, :, 2:, :], corner_left_high),
+            rows_of(zero_pair, fine_box[:, :, :2, :], zero_pair),
+        ],
+        axis=2,
+    )
+    padded_right = jnp.concatenate(
+        [
+            rows_of(zero_pair, fine_box[:, :, -2:, :], zero_pair),
+            rows_of(corner_right_low, wide_right[:, :, :2, :], corner_right_high),
+            rows_of(zero_pair, wide_right[:, :, 2:, :], zero_pair),
+        ],
+        axis=2,
+    )
+    padded_low = jnp.concatenate(
+        [
+            cols_of(zero_pair, wide_low[..., :2], zero_pair),
+            cols_of(corner_left_low, wide_low[..., 2:], corner_right_low),
+            cols_of(zero_pair, fine_box[..., :2], zero_pair),
+        ],
+        axis=3,
+    )
+    padded_high = jnp.concatenate(
+        [
+            cols_of(zero_pair, fine_box[..., -2:], zero_pair),
+            cols_of(corner_left_high, wide_high[..., :2], corner_right_high),
+            cols_of(zero_pair, wide_high[..., 2:], zero_pair),
+        ],
+        axis=3,
+    )
+    rim_left = wide_left[:, :, 2:, :] + jax.vmap(rim_rate)(padded_left)
+    rim_right = wide_right[:, :, :2, :] + jax.vmap(rim_rate)(padded_right)
+    rim_low = wide_low[..., 2:] + jax.vmap(rim_rate)(padded_low)
+    rim_high = wide_high[..., :2] + jax.vmap(rim_rate)(padded_high)
+
+    def flagged(source, fine_part, coarse_part):
+        return jnp.where(source[0].reshape((-1,) + (1,) * (fine_part.ndim - 1)), fine_part, coarse_part)
+
+    ghost2_left = flagged(targets_left, rim_left, inject_side(pick_edge(left_edges_one, targets_left)))
+    ghost2_right = flagged(targets_right, rim_right, inject_side(pick_edge(right_edges_one, targets_right)))
+    ghost2_low = flagged(targets_low, rim_low, inject_end(pick_edge(high_edges_one, targets_low)))
+    ghost2_high = flagged(targets_high, rim_high, inject_end(pick_edge(low_edges_one, targets_high)))
+    rate_f2, left_two, right_two, low_two, high_two = jax.vmap(fine_section)(
+        fine_one, ghost2_left, ghost2_right, ghost2_low, ghost2_high
+    )
     fine_final = 0.5 * (fine_box + fine_one + rate_f2)
     reg_left = pair_mean(0.5 * (left_one + left_two))
     reg_right = pair_mean(0.5 * (right_one + right_two))

time: 330 us -> 289 us (0.88)
  waiting for transfers between devices: 150 us -> 94 us
  other arithmetic: 31.2 us -> 42 us
  local copies, waits for them, and re-layouts: 55.8 us -> 65.9 us
  starting transfers between devices: 76.2 us -> 69.7 us
    all_gather x3 -> x2, waiting for transfers between devices: 139 us -> 83.5 us  [gather_rows(): rows = lax.all_gather(flat, 'gy', axis=0, tiled=True)]
    ppermute x0 -> x2, starting transfers between devices: none -> 11.6 us  [the longest x1 9.66 us: shards(): lax.ppermute(left_pack, 'gx', [((i + 1) % count_x, i) for i in range(coun...]
    ppermute x7 -> x5, starting transfers between devices: 24.5 us -> 15.6 us  [extended(): lax.ppermute(tail, axis, [(i, (i + 1) % count) for i in range(count)])]
    ppermute x7 -> x5, starting transfers between devices: 51.4 us -> 42.4 us  [extended(): lax.ppermute(head, axis, [((i + 1) % count, i) for i in range(count)])]
    and x7 -> x11, other arithmetic: 0.53 us -> 7.2 us  [the longest x8 5.21 us: pick(): (row_index[None, :, None] == fine_row[:, None, None]) & (sub_index[None,...]
    slice x20 -> x34, local copies, waits for them, and re-layouts: 1.47 us -> 5.6 us  [the longest x6 1.12 us: corner(): fine_part = pick(strips[:, :, :, rows[0]:rows[1], cols[0]:cols[1]], source)]
    ppermute x7 -> x5, waiting for transfers between devices: 8.55 us -> 7.88 us  [extended(): lax.ppermute(head, axis, [((i + 1) % count, i) for i in range(count)])]
  transfers between devices with their start and end apart: 17 -> 14, of which waited for: 8 -> 7; matrix products, arithmetic and copies ran while one was open for 6% -> 13% of each run, Pallas kernels for 0% -> 0%
where the time goes in v3:
time: 289 us; the launch traced here: 288 us
  waiting for transfers between devices  94 us (33%)
  starting transfers between devices  69.7 us (24%)
  local copies, waits for them, and re-layouts  65.9 us (23%)
  other arithmetic  42 us (15%)
  between operations  16 us (6%)
    all_gather x2, waiting for transfers between devices, gather_rows(): rows = lax.all_gather(flat, 'gy', axis=0, tiled=True)  83.5 us
    ppermute x5, starting transfers between devices, extended(): lax.ppermute(head, axis, [((i + 1) % count, i) for i in range(count)])  42.4 us
    ppermute x5, starting transfers between devices, extended(): lax.ppermute(tail, axis, [(i, (i + 1) % count) for i in range(count)])  15.6 us
    ppermute x1, starting transfers between devices, shards(): lax.ppermute(left_pack, 'gx', [((i + 1) % count_x, i) for i in range(coun...  9.66 us
    ppermute x5, waiting for transfers between devices, extended(): lax.ppermute(head, axis, [((i + 1) % count, i) for i in range(count)])  7.88 us
    reduce_sum x8, other arithmetic, select(): jnp.sum(jnp.where(hit_mask.reshape(hit_mask.shape + extra), payload, 0.0)...  7.74 us
  transfers between devices with their start and end apart: 14, of which 7 were waited for; matrix products, arithmetic and copies ran while one was open for 13% of the time, Pallas kernels for 0%

profile of v3, /device:TPU:1, one launch (start us, length us, event | category | flops | bytes accessed | tf_op | source)
XLA Modules:
  0.0 287.5 jit_solution(13897491278725391658)
XLA Ops:
  7.2 0.7 fusion.224
  7.9 20.4 %collective-permute-start.1 = (f32[3,2,128]{2,1,0:T(2,128)S(1)}, f32[3,2,128]{2,1,0:T(2,128)S(1)}, u32[]{:S(2)}, u32[]{:S(2)}) collective-permute-start(f32[3,2,128]{2,1,0:T(2,128)S(1)} %get-tuple-element.149), channel_id=1, source_target_pairs={{32,0},{64,32},{96,64},{128,96},{160,128},{192,160},{224,192},{256... | collective-permute-start | bytes 9224 | tf_op jit(solution)/shard_map/ppermute | solution.py:19
  28.3 1.9 collective-permute-start
  30.3 1.2 fusion.24
  31.5 1.2 select_reduce_fusion.4
  32.7 0.8 constant_dynamic-update-slice_fusion.1
  33.5 1.0 copy.794
  34.7 1.1 slice_reduce_fusion.2
  35.9 0.8 or_bitcast_fusion.2
  48.4 0.7 copy.631
  49.1 0.7 copy.615
  50.0 3.1 %collective-permute-start.2 = (f32[3,36,2]{2,1,0:T(8,128)S(1)}, f32[3,36,2]{2,1,0:T(8,128)S(1)}, u32[]{:S(2)}, u32[]{:S(2)}) collective-permute-start(f32[3,36,2]{2,1,0:T(8,128)S(1)} %get-tuple-element.136), channel_id=1, source_target_pairs={{0,1},{1,2},{2,3},{3,4},{4,5},{5,6},{6,7},{7,8},{8,9},{9,10},{10,1... | collective-permute-start | bytes 2600 | tf_op jit(solution)/shard_map/ppermute | solution.py:17
  53.1 1.9 collective-permute-start.3
  55.7 3.7 %collective-permute-done.3 = f32[3,36,2]{2,1,0:T(8,128)S(1)} collective-permute-done((f32[3,36,2]{2,1,0:T(8,128)S(1)}, f32[3,36,2]{2,1,0:T(8,128)S(1)}, u32[]{:S(2)}, u32[]{:S(2)}) %collective-permute-start.3) | collective-permute-done | bytes 896 | tf_op jit(solution)/shard_map/ppermute | solution.py:19
  59.9 1.9 collective-permute-start.4
  61.8 9.7 %collective-permute-start.5 = (f32[6912]{0:T(1024)S(1)}, f32[6912]{0:T(1024)S(1)}, u32[]{:S(2)}, u32[]{:S(2)}) collective-permute-start(f32[6912]{0:T(1024)S(1)} %pad_maximum_fusion.33), channel_id=1, source_target_pairs={{32,0},{64,32},{96,64},{128,96},{160,128},{192,160},{224,192},{256... | collective-permute-start | bytes 82952 | tf_op jit(solution)/shard_map/ppermute | solution.py:193
  73.2 1.3 compare_bitcast_fusion
  82.8 53.9 %all-gather.5.cloned.1.call-done = f32[557056]{0:T(1024)} async-done(((f32[17408]{0:T(1024)}), f32[557056]{0:T(1024)}) %all-gather.5.cloned.1.call-update) | async-done | bytes 2228240 | tf_op jit(solution)/shard_map/all_gather | solution.py:118
  136.7 1.9 reshape.2022
  138.6 1.3 fusion.210
  139.9 0.7 fusion.209
  140.6 0.7 fusion.212
  141.3 0.7 fusion.211
  142.0 1.7 broadcast_in_dim.644
  144.2 0.8 select_reduce_fusion.15
  145.3 0.7 select_reduce_fusion.19
  146.5 0.8 select_reduce_fusion.16
  147.5 0.7 select_reduce_fusion.20
  160.4 0.8 fusion.10
  163.0 0.8 copy-done
  164.1 0.8 fusion.7
  165.0 0.8 fusion.4
  167.2 3.5 %slice.1073 = f32[2,3,32,128]{3,2,0,1:T(8,128)S(1)} slice(f32[2,3,64,256]{3,2,0,1:T(8,128)S(1)} %get-tuple-element.46), slice={[0:2:1], [0:3:1], [0:64:2], [1:256:2]} | slice | bytes 196608 | tf_op jit(solution)/shard_map/slice | solution.py:91
  170.7 3.5 %slice.1074 = f32[2,3,32,128]{3,2,0,1:T(8,128)S(1)} slice(f32[2,3,64,256]{3,2,0,1:T(8,128)S(1)} %get-tuple-element.46), slice={[0:2:1], [0:3:1], [1:64:2], [1:256:2]} | slice | bytes 196608 | tf_op jit(solution)/shard_map/slice | solution.py:91
  174.2 3.5 %slice.1071 = f32[2,3,32,128]{3,2,0,1:T(8,128)S(1)} slice(f32[2,3,64,256]{3,2,0,1:T(8,128)S(1)} %get-tuple-element.46), slice={[0:2:1], [0:3:1], [0:64:2], [0:256:2]} | slice | bytes 196608 | tf_op jit(solution)/shard_map/slice | solution.py:89
  177.7 3.5 %slice.1072 = f32[2,3,32,128]{3,2,0,1:T(8,128)S(1)} slice(f32[2,3,64,256]{3,2,0,1:T(8,128)S(1)} %get-tuple-element.46), slice={[0:2:1], [0:3:1], [1:64:2], [0:256:2]} | slice | bytes 196608 | tf_op jit(solution)/shard_map/slice | solution.py:90
  183.0 3.2 %collective-permute-start.6 = (f32[1,2,2,3,128]{4,2,3,1,0:T(2,128)S(1)}, f32[1,2,2,3,128]{4,2,3,1,0:T(2,128)S(1)}, u32[]{:S(2)}, u32[]{:S(2)}) collective-permute-start(f32[1,2,2,3,128]{4,2,3,1,0:T(2,128)S(1)} %maximum_bitcast_fusion), channel_id=1, source_target_pairs={{0,32},{32,64},{64,96},{96,128},{128,160},{160,192},{192,224},{224... | collective-permute-start | bytes 18440 | tf_op jit(solution)/shard_map/ppermute | solution.py:17
  186.2 8.6 %collective-permute-start.7 = (f32[1,2,2,3,128]{4,2,3,1,0:T(2,128)S(1)}, f32[1,2,2,3,128]{4,2,3,1,0:T(2,128)S(1)}, u32[]{:S(2)}, u32[]{:S(2)}) collective-permute-start(f32[1,2,2,3,128]{4,2,3,1,0:T(2,128)S(1)} %maximum_bitcast_fusion), channel_id=1, source_target_pairs={{32,0},{64,32},{96,64},{128,96},{160,128},{192,160},{224,192},{256... | collective-permute-start | bytes 18440 | tf_op jit(solution)/shard_map/ppermute | solution.py:19
  196.4 9.6 %collective-permute-start.9 = (f32[3,2,128]{2,1,0:T(2,128)S(1)}, f32[3,2,128]{2,1,0:T(2,128)S(1)}, u32[]{:S(2)}, u32[]{:S(2)}) collective-permute-start(f32[3,2,128]{2,1,0:T(2,128)S(1)} %get-tuple-element.145), channel_id=1, source_target_pairs={{32,0},{64,32},{96,64},{128,96},{160,128},{192,160},{224,192},{256... | collective-permute-start | bytes 9224 | tf_op jit(solution)/shard_map/ppermute | solution.py:19
  206.0 1.9 collective-permute-start.8
  208.0 0.8 compare_reduce_fusion.1
  211.0 0.7 broadcast_in_dim.740
  212.0 0.7 broadcast_in_dim.745
  213.9 0.7 fusion.233
  214.6 1.9 collective-permute-done.8
  216.6 5.3 %collective-permute-start.10 = (f32[3,36,2]{2,1,0:T(8,128)S(1)}, f32[3,36,2]{2,1,0:T(8,128)S(1)}, u32[]{:S(2)}, u32[]{:S(2)}) collective-permute-start(f32[3,36,2]{2,1,0:T(8,128)S(1)} %get-tuple-element.131), channel_id=1, source_target_pairs={{0,1},{1,2},{2,3},{3,4},{4,5},{5,6},{6,7},{7,8},{8,9},{9,10},{10,1... | collective-permute-start | bytes 2600 | tf_op jit(solution)/shard_map/ppermute | solution.py:17
  221.9 1.9 collective-permute-start.11
  224.6 3.7 %collective-permute-done.11 = f32[3,36,2]{2,1,0:T(8,128)S(1)} collective-permute-done((f32[3,36,2]{2,1,0:T(8,128)S(1)}, f32[3,36,2]{2,1,0:T(8,128)S(1)}, u32[]{:S(2)}, u32[]{:S(2)}) %collective-permute-start.11) | collective-permute-done | bytes 896 | tf_op jit(solution)/shard_map/ppermute | solution.py:19
  229.2 0.8 copy.670
  230.0 29.6 %all-gather.7.cloned.1.call-done = f32[851968]{0:T(1024)} async-done(((f32[26624]{0:T(1024)}), f32[851968]{0:T(1024)}) %all-gather.7.cloned.1.call-update) | async-done | bytes 3407888 | tf_op jit(solution)/shard_map/all_gather | solution.py:118
  259.6 2.2 reshape.2023
  262.2 1.4 fusion
  263.6 0.9 reduce_sum.300
  264.5 1.4 fusion.54
  265.9 1.3 reduce_sum.302
  267.2 1.3 reduce_sum.303
  268.5 1.3 reduce_sum.306
  269.8 1.3 reduce_sum.307
  271.0 1.4 fusion.85
  272.4 0.8 reduce_sum.310
  273.3 0.8 reduce_sum.314
  274.2 2.1 broadcast_select_fusion.5
  276.2 2.1 fusion.71
  278.4 2.3 fusion.78
  (403 shorter events, 48.1 us)
Async XLA Ops:
  7.2 129.5 %all-gather.5.cloned.1.call-start = ((), (), s32[]{:S(2)}) async-start(), calls=%async_computation | async-start | bytes 2297856 | tf_op jit(solution)/shard_map/all_gather | solution.py:118
  7.9 41.9 %collective-permute-start.1 = (f32[3,2,128]{2,1,0:T(2,128)S(1)}, f32[3,2,128]{2,1,0:T(2,128)S(1)}, u32[]{:S(2)}, u32[]{:S(2)}) collective-permute-start(f32[3,2,128]{2,1,0:T(2,128)S(1)} %get-tuple-element.149), channel_id=1, source_target_pairs={{32,0},{64,32},{96,64},{128,96},{160,128},{192,160},{224,192},{256... | collective-permute-start | bytes 9224 | tf_op jit(solution)/shard_map/ppermute | solution.py:19
  28.3 21.5 %collective-permute-start = (f32[3,2,128]{2,1,0:T(2,128)S(1)}, f32[3,2,128]{2,1,0:T(2,128)S(1)}, u32[]{:S(2)}, u32[]{:S(2)}) collective-permute-start(f32[3,2,128]{2,1,0:T(2,128)S(1)} %get-tuple-element.148), channel_id=1, source_target_pairs={{0,32},{32,64},{64,96},{96,128},{128,160},{160,192},{192,224},{224... | collective-permute-start | bytes 9224 | tf_op jit(solution)/shard_map/ppermute | solution.py:17
  34.7 6.7 %copy-start.1 = (f32[3,32,128]{2,1,0:T(8,128)S(1)}, f32[3,32,128]{2,1,0:T(8,128)}, u32[]{:S(2)}) copy-start(f32[3,32,128]{2,1,0:T(8,128)} %param.3) | copy-start | bytes 147460
  42.0 33.6 %copy-start.29 = (pred[2]{0:T(512)(128)(4,1)}, pred[2]{0:T(512)(128)(4,1)S(1)}, u32[]{:S(2)}) copy-start(pred[2]{0:T(512)(128)(4,1)S(1)} %gather_fusion.5) | copy-start | bytes 10
  44.0 33.6 %copy-start.27 = (pred[2]{0:T(512)(128)(4,1)}, pred[2]{0:T(512)(128)(4,1)S(1)}, u32[]{:S(2)}) copy-start(pred[2]{0:T(512)(128)(4,1)S(1)} %gather_fusion.3) | copy-start | bytes 10
  45.9 33.0 %copy-start.25 = (pred[2]{0:T(512)(128)(4,1)}, pred[2]{0:T(512)(128)(4,1)S(1)}, u32[]{:S(2)}) copy-start(pred[2]{0:T(512)(128)(4,1)S(1)} %gather_fusion.1) | copy-start | bytes 10
  47.8 31.7 %copy-start.23 = (pred[2]{0:T(512)(128)(4,1)}, pred[2]{0:T(512)(128)(4,1)S(1)}, u32[]{:S(2)}) copy-start(pred[2]{0:T(512)(128)(4,1)S(1)} %gather_fusion.7) | copy-start | bytes 10
  50.0 5.2 %collective-permute-start.2 = (f32[3,36,2]{2,1,0:T(8,128)S(1)}, f32[3,36,2]{2,1,0:T(8,128)S(1)}, u32[]{:S(2)}, u32[]{:S(2)}) collective-permute-start(f32[3,36,2]{2,1,0:T(8,128)S(1)} %get-tuple-element.136), channel_id=1, source_target_pairs={{0,1},{1,2},{2,3},{3,4},{4,5},{5,6},{6,7},{7,8},{8,9},{9,10},{10,1... | collective-permute-start | bytes 2600 | tf_op jit(solution)/shard_map/ppermute | solution.py:17
  53.1 6.3 %collective-permute-start.3 = (f32[3,36,2]{2,1,0:T(8,128)S(1)}, f32[3,36,2]{2,1,0:T(8,128)S(1)}, u32[]{:S(2)}, u32[]{:S(2)}) collective-permute-start(f32[3,36,2]{2,1,0:T(8,128)S(1)} %get-tuple-element.137), channel_id=1, source_target_pairs={{1,0},{2,1},{3,2},{4,3},{5,4},{6,5},{7,6},{8,7},{9,8},{10,9},{11,1... | collective-permute-start | bytes 2600 | tf_op jit(solution)/shard_map/ppermute | solution.py:19
  55.1 0.6 copy-start.9
  55.1 0.6 copy-start.10
  55.1 0.6 copy-start.11
  59.7 23.1 %copy-start.3 = (f32[3,32,129]{2,1,0:T(8,128)}, f32[3,32,129]{2,1,0:T(8,128)S(1)}, u32[]{:S(2)}) copy-start(f32[3,32,129]{2,1,0:T(8,128)S(1)} %pad_maximum_fusion.18) | copy-start | bytes 148612
  59.9 11.9 %collective-permute-start.4 = (f32[6912]{0:T(1024)S(1)}, f32[6912]{0:T(1024)S(1)}, u32[]{:S(2)}, u32[]{:S(2)}) collective-permute-start(f32[6912]{0:T(1024)S(1)} %pad_maximum_fusion.32), channel_id=1, source_target_pairs={{0,32},{32,64},{64,96},{96,128},{128,160},{160,192},{192,224},{224... | collective-permute-start | bytes 82952 | tf_op jit(solution)/shard_map/ppermute | solution.py:192
  61.8 10.6 %collective-permute-start.5 = (f32[6912]{0:T(1024)S(1)}, f32[6912]{0:T(1024)S(1)}, u32[]{:S(2)}, u32[]{:S(2)}) collective-permute-start(f32[6912]{0:T(1024)S(1)} %pad_maximum_fusion.33), channel_id=1, source_target_pairs={{32,0},{64,32},{96,64},{128,96},{160,128},{192,160},{224,192},{256... | collective-permute-start | bytes 82952 | tf_op jit(solution)/shard_map/ppermute | solution.py:193
  73.2 186.5 %all-gather.7.cloned.1.call-start = ((), (), s32[]{:S(2)}) async-start(), calls=%async_computation.1 | async-start | bytes 3514368 | tf_op jit(solution)/shard_map/all_gather | solution.py:118
  142.0 6.8 %copy-start.2 = (f32[32,6144]{1,0:T(8,128)S(1)}, f32[32,6144]{1,0:T(8,128)}, u32[]{:S(2)}) copy-start(f32[32,6144]{1,0:T(8,128)} %get-tuple-element.59) | copy-start | bytes 2359300
  146.3 3.5 %copy-start.36 = (pred[2,32,2]{1,2,0:T(4,128)(4,1)S(1)}, pred[2,32,2]{1,2,0:T(4,128)(4,1)}, u32[]{:S(2)}) copy-start(pred[2,32,2]{1,2,0:T(4,128)(4,1)} %and_and_fusion) | copy-start | bytes 388
  148.6 1.7 copy-start.42
  148.6 2.3 copy-start.35
  148.6 2.6 copy-start.41
  148.8 3.0 %copy-start.34 = (pred[2,32,2]{1,2,0:T(4,128)(4,1)S(1)}, pred[2,32,2]{1,2,0:T(4,128)(4,1)}, u32[]{:S(2)}) copy-start(pred[2,32,2]{1,2,0:T(4,128)(4,1)} %and_and_fusion.7) | copy-start | bytes 388
  149.4 2.8 copy-start.33
  149.6 3.1 %copy-start.19 = (f32[2,3,2,256]{3,2,0,1:T(2,128)S(1)}, f32[2,3,2,256]{3,2,0,1:T(2,128)}, u32[]{:S(2)}) copy-start(f32[2,3,2,256]{3,2,0,1:T(2,128)} %get-tuple-element.96) | copy-start | bytes 36868
  149.6 3.1 %copy-start.20 = (f32[2,3,2,256]{3,2,0,1:T(2,128)S(1)}, f32[2,3,2,256]{3,2,0,1:T(2,128)}, u32[]{:S(2)}) copy-start(f32[2,3,2,256]{3,2,0,1:T(2,128)} %get-tuple-element.97) | copy-start | bytes 36868
  150.3 3.1 %copy-start.4 = (f32[32,1536]{1,0:T(8,128)S(1)}, f32[32,1536]{1,0:T(8,128)}, u32[]{:S(2)}) copy-start(f32[32,1536]{1,0:T(8,128)} %get-tuple-element.64) | copy-start | bytes 589828
  151.9 2.1 copy-start.32
  152.1 2.2 copy-start.22
  152.1 2.5 copy-start.18
  152.1 2.6 copy-start.17
  152.2 2.7 copy-start.40
  152.8 2.7 copy-start.30
  153.9 2.5 copy-start.31
  154.1 2.7 copy-start.21
  154.4 2.7 copy-start.16
  154.7 2.5 copy-start.15
  154.8 2.5 copy-start.39
  155.4 2.5 copy-start.28
  155.7 2.5 copy-start.7
  155.7 2.5 copy-start.8
  155.9 2.3 copy-start.5
  155.9 2.3 copy-start.6
  155.9 2.4 copy-start.38
  156.5 2.8 copy-start.37
  160.2 1.3 copy-start.26
  160.2 1.4 copy-start.24
  162.9 1.0 copy-start
  166.3 0.7 copy-start.43
  183.0 12.1 %collective-permute-start.6 = (f32[1,2,2,3,128]{4,2,3,1,0:T(2,128)S(1)}, f32[1,2,2,3,128]{4,2,3,1,0:T(2,128)S(1)}, u32[]{:S(2)}, u32[]{:S(2)}) collective-permute-start(f32[1,2,2,3,128]{4,2,3,1,0:T(2,128)S(1)} %maximum_bitcast_fusion), channel_id=1, source_target_pairs={{0,32},{32,64},{64,96},{96,128},{128,160},{160,192},{192,224},{224... | collective-permute-start | bytes 18440 | tf_op jit(solution)/shard_map/ppermute | solution.py:17
  186.2 9.4 %collective-permute-start.7 = (f32[1,2,2,3,128]{4,2,3,1,0:T(2,128)S(1)}, f32[1,2,2,3,128]{4,2,3,1,0:T(2,128)S(1)}, u32[]{:S(2)}, u32[]{:S(2)}) collective-permute-start(f32[1,2,2,3,128]{4,2,3,1,0:T(2,128)S(1)} %maximum_bitcast_fusion), channel_id=1, source_target_pairs={{32,0},{64,32},{96,64},{128,96},{160,128},{192,160},{224,192},{256... | collective-permute-start | bytes 18440 | tf_op jit(solution)/shard_map/ppermute | solution.py:19
  196.4 18.2 %collective-permute-start.9 = (f32[3,2,128]{2,1,0:T(2,128)S(1)}, f32[3,2,128]{2,1,0:T(2,128)S(1)}, u32[]{:S(2)}, u32[]{:S(2)}) collective-permute-start(f32[3,2,128]{2,1,0:T(2,128)S(1)} %get-tuple-element.145), channel_id=1, source_target_pairs={{32,0},{64,32},{96,64},{128,96},{160,128},{192,160},{224,192},{256... | collective-permute-start | bytes 9224 | tf_op jit(solution)/shard_map/ppermute | solution.py:19
  206.0 10.5 %collective-permute-start.8 = (f32[3,2,128]{2,1,0:T(2,128)S(1)}, f32[3,2,128]{2,1,0:T(2,128)S(1)}, u32[]{:S(2)}, u32[]{:S(2)}) collective-permute-start(f32[3,2,128]{2,1,0:T(2,128)S(1)} %get-tuple-element.144), channel_id=1, source_target_pairs={{0,32},{32,64},{64,96},{96,128},{128,160},{160,192},{192,224},{224... | collective-permute-start | bytes 9224 | tf_op jit(solution)/shard_map/ppermute | solution.py:17
  216.6 8.0 %collective-permute-start.10 = (f32[3,36,2]{2,1,0:T(8,128)S(1)}, f32[3,36,2]{2,1,0:T(8,128)S(1)}, u32[]{:S(2)}, u32[]{:S(2)}) collective-permute-start(f32[3,36,2]{2,1,0:T(8,128)S(1)} %get-tuple-element.131), channel_id=1, source_target_pairs={{0,1},{1,2},{2,3},{3,4},{4,5},{5,6},{6,7},{7,8},{8,9},{9,10},{10,1... | collective-permute-start | bytes 2600 | tf_op jit(solution)/shard_map/ppermute | solution.py:17
  221.9 6.4 %collective-permute-start.11 = (f32[3,36,2]{2,1,0:T(8,128)S(1)}, f32[3,36,2]{2,1,0:T(8,128)S(1)}, u32[]{:S(2)}, u32[]{:S(2)}) collective-permute-start(f32[3,36,2]{2,1,0:T(8,128)S(1)} %get-tuple-element.132), channel_id=1, source_target_pairs={{1,0},{2,1},{3,2},{4,3},{5,4},{6,5},{7,6},{8,7},{9,8},{10,9},{11,1... | collective-permute-start | bytes 2600 | tf_op jit(solution)/shard_map/ppermute | solution.py:19
  223.9 0.7 copy-start.12
  223.9 0.7 copy-start.13
  223.9 0.7 copy-start.14
Sparse Core Ops, SparseCore 0:
  73.3 63.3 all-gather.4
  196.5 63.1 all-gather.6

commit v4 on v3

--- a/solution.py
+++ b/solution.py
@@ -116,13 +116,38 @@
     flat = jnp.concatenate([part.reshape(-1) for part in parts])
     flat = jnp.pad(flat, (0, -flat.size % 1024))[None]
     rows = lax.all_gather(flat, "gy", axis=0, tiled=True)
-    count = rows.shape[0]
-    out = []
+    offsets = []
     offset = 0
     for part in parts:
-        out.append(rows[:, offset : offset + part.size].reshape((count,) + part.shape))
+        offsets.append((offset, part.shape))
         offset += part.size
-    return tuple(out)
+    return rows, offsets
+
+
+def take_row(rows, place, row):
+    offset, shape = place
+    size = 1
+    for extent in shape:
+        size *= extent
+    return lax.dynamic_slice(rows, (row, offset), (1, size)).reshape(shape)
+
+
+def take_slot(rows, place, row, sub):
+    offset, shape = place
+    size = 1
+    for extent in shape[1:]:
+        size *= extent
+    return lax.dynamic_slice(rows, (row, offset + sub * size), (1, size)).reshape(shape[1:])
+
+
+def shift_x(values, step):
+    count = lax.axis_size("gx")
+    return lax.ppermute(values, "gx", [(i, (i + step) % count) for i in range(count)])
+
+
+def shift_y(values, step):
+    count = lax.axis_size("gy")
+    return lax.ppermute(values, "gy", [(i, (i + step) % count) for i in range(count)])
 
 
 def shards(coarse_state, refined_box_state, box_parent):
@@ -144,8 +169,6 @@
     below_block = (device_row - 1) % count_y
     above_block = (device_row + 1) % count_y
     own_table = lax.dynamic_index_in_dim(box_parent, column, 0, keepdims=False)
-    left_table = lax.dynamic_index_in_dim(box_parent, column_left, 0, keepdims=False)
-    right_table = lax.dynamic_index_in_dim(box_parent, column_right, 0, keepdims=False)
     own_parents = lax.dynamic_slice_in_dim(own_table, device_row * slot_count, slot_count)
     is_live = own_parents < count_y
     parent = jnp.minimum(own_parents, count_y - 1)
@@ -159,95 +182,83 @@
     targets_right = fine_source(column_right, parent)
     targets_low = fine_source(column, (parent - 1) % count_y)
     targets_high = fine_source(column, (parent + 1) % count_y)
-    rate_one, flux_x1, flux_y1 = advance_rate(coarse_margin(coarse_state), LAM_COARSE)
-    coarse_one = coarse_state + rate_one
-    rate_two, flux_x2, flux_y2 = advance_rate(coarse_margin(coarse_one), LAM_COARSE)
-    coarse_heun = 0.5 * (coarse_state + coarse_one + rate_two)
-
-    def pick(gathered, source):
-        flag, fine_row, fine_sub, _ = source
-        row_index = jnp.arange(gathered.shape[0], dtype=jnp.int32)
-        sub_index = jnp.arange(gathered.shape[1], dtype=jnp.int32)
-        hit_mask = (
-            (row_index[None, :, None] == fine_row[:, None, None])
-            & (sub_index[None, None, :] == fine_sub[:, None, None])
-            & flag[:, None, None]
-        )
-        extra = (1,) * (gathered.ndim - 2)
-        return jnp.sum(jnp.where(hit_mask.reshape(hit_mask.shape + extra), gathered[None], 0.0), axis=(1, 2))
-
-    def pick_edge(edges, source):
-        flag, _, _, edge_row = source
-        row_index = jnp.arange(edges.shape[0], dtype=jnp.int32)
-        edge_mask = (row_index[None, :] == edge_row[:, None]) & jnp.logical_not(flag)[:, None]
-        extra = (1,) * (edges.ndim - 1)
-        return jnp.sum(jnp.where(edge_mask.reshape(edge_mask.shape + extra), edges[None], 0.0), axis=1)
-
-    right_pack = jnp.concatenate(
-        [fine_box[:, :, -4:, :].reshape(-1), coarse_state[:, -1, :].reshape(-1), coarse_one[:, -1, :].reshape(-1)]
-    )
-    left_pack = jnp.concatenate(
-        [fine_box[:, :, :4, :].reshape(-1), coarse_state[:, 0, :].reshape(-1), coarse_one[:, 0, :].reshape(-1)]
-    )
-    from_left = lax.ppermute(right_pack, "gx", [(i, (i + 1) % count_x) for i in range(count_x)])
-    from_right = lax.ppermute(left_pack, "gx", [((i + 1) % count_x, i) for i in range(count_x)])
-    side_strip_shape = fine_box[:, :, :4, :].shape
-    side_strip_size = fine_box[:, :, :4, :].size
-    edge_x_shape = coarse_state[:, 0, :].shape
-    edge_x_size = coarse_state[:, 0, :].size
-    gathered = gather_rows(
-        (
-            from_left[:side_strip_size].reshape(side_strip_shape),
-            from_left[side_strip_size : side_strip_size + edge_x_size].reshape(edge_x_shape),
-            from_left[side_strip_size + edge_x_size :].reshape(edge_x_shape),
-            from_right[:side_strip_size].reshape(side_strip_shape),
-            from_right[side_strip_size : side_strip_size + edge_x_size].reshape(edge_x_shape),
-            from_right[side_strip_size + edge_x_size :].reshape(edge_x_shape),
-            fine_box[..., -4:],
-            fine_box[..., :4],
-            coarse_state[:, :, -1],
-            coarse_state[:, :, 0],
-            coarse_one[:, :, -1],
-            coarse_one[:, :, 0],
-        )
-    )
-    (
-        left_strips,
-        left_edges,
-        left_edges_one,
-        right_strips,
-        right_edges,
-        right_edges_one,
-        high_strips,
-        low_strips,
-        high_edges,
-        low_edges,
-        high_edges_one,
-        low_edges_one,
-    ) = gathered
     targets_left_low = fine_source(column_left, (parent - 1) % count_y)
     targets_left_high = fine_source(column_left, (parent + 1) % count_y)
     targets_right_low = fine_source(column_right, (parent - 1) % count_y)
     targets_right_high = fine_source(column_right, (parent + 1) % count_y)
 
-    def corner(strips, edges, source, rows, cols, edge_index):
-        fine_part = pick(strips[:, :, :, rows[0] : rows[1], cols[0] : cols[1]], source)
-        edge_part = pick_edge(edges[:, :, edge_index], source)
+    strip_size = fine_box[:, :, :4, :].size
+    right_pack = jnp.concatenate([fine_box[:, :, -4:, :].reshape(-1), coarse_state[:, -2:, :].reshape(-1)])
+    left_pack = jnp.concatenate([fine_box[:, :, :4, :].reshape(-1), coarse_state[:, :2, :].reshape(-1)])
+    from_left = shift_x(right_pack, 1)
+    from_right = shift_x(left_pack, -1)
+    strip_shape = fine_box[:, :, :4, :].shape
+    rim_shape = coarse_state[:, :2, :].shape
+    left_rim = from_left[strip_size:].reshape(rim_shape)
+    right_rim = from_right[strip_size:].reshape(rim_shape)
+
+    def coarse_padded(field, ghost_left, ghost_right):
+        ghost_low = shift_y(field[:, :, -2:], 1)
+        ghost_high = shift_y(field[:, :, :2], -1)
+        return assemble(field, ghost_left, ghost_right, ghost_low, ghost_high)
+
+    rate_one, flux_x1, flux_y1 = advance_rate(coarse_padded(coarse_state, left_rim, right_rim), LAM_COARSE)
+    coarse_one = coarse_state + rate_one
+    one_left = shift_x(coarse_one[:, -2:, :], 1)
+    one_right = shift_x(coarse_one[:, :2, :], -1)
+    rate_two, flux_x2, flux_y2 = advance_rate(coarse_padded(coarse_one, one_left, one_right), LAM_COARSE)
+    coarse_heun = 0.5 * (coarse_state + coarse_one + rate_two)
+
+    parts = (
+        from_left[:strip_size].reshape(strip_shape),
+        left_rim[:, 1, :],
+        from_right[:strip_size].reshape(strip_shape),
+        right_rim[:, 0, :],
+        fine_box[..., -4:],
+        fine_box[..., :4],
+        coarse_state[:, :, -1],
+        coarse_state[:, :, 0],
+        coarse_one[:, :, -1],
+        coarse_one[:, :, 0],
+        coarse_one[:, -1, :],
+        coarse_one[:, 0, :],
+    )
+    rows, places = gather_rows(parts)
+    column_edges_one = lax.slice_in_dim(rows, places[10][0], places[10][0] + 2 * coarse_one[:, 0, :].size, axis=1)
+    left_edges_one = shift_x(column_edges_one[:, : coarse_one[:, 0, :].size], 1)
+    right_edges_one = shift_x(column_edges_one[:, coarse_one[:, 0, :].size :], -1)
+
+    def pick(place, source):
+        flag, fine_row, fine_sub, _ = source
+        taken = jnp.stack([take_slot(rows, place, fine_row[s], fine_sub[s]) for s in range(slot_count)])
+        return jnp.where(flag.reshape((-1,) + (1,) * (taken.ndim - 1)), taken, 0.0)
+
+    def pick_edge_in(table, place, source):
+        flag, _, _, edge_row = source
+        taken = jnp.stack([take_row(table, place, edge_row[s]) for s in range(slot_count)])
+        return jnp.where(flag.reshape((-1,) + (1,) * (taken.ndim - 1)), 0.0, taken)
+
+    def pick_edge(place, source):
+        return pick_edge_in(rows, place, source)
+
+    def corner(place, edge_place, source, row_slice, col_slice, edge_index):
+        fine_part = pick(place, source)[:, :, row_slice, col_slice]
+        edge_part = pick_edge(edge_place, source)[:, :, edge_index]
         return fine_part + edge_part[:, :, None, None]
 
-    corner_left_low = corner(left_strips, left_edges, targets_left_low, (2, 4), (-2, None), -1)
-    corner_left_high = corner(left_strips, left_edges, targets_left_high, (2, 4), (0, 2), 0)
-    corner_right_low = corner(right_strips, right_edges, targets_right_low, (0, 2), (-2, None), -1)
-    corner_right_high = corner(right_strips, right_edges, targets_right_high, (0, 2), (0, 2), 0)
-
-    wide_left = pick(left_strips, targets_left)
-    wide_right = pick(right_strips, targets_right)
-    wide_low = pick(high_strips, targets_low)
-    wide_high = pick(low_strips, targets_high)
-    ghost_left = wide_left[:, :, 2:, :] + inject_side(pick_edge(left_edges, targets_left))
-    ghost_right = wide_right[:, :, :2, :] + inject_side(pick_edge(right_edges, targets_right))
-    ghost_low = wide_low[..., 2:] + inject_end(pick_edge(high_edges, targets_low))
-    ghost_high = wide_high[..., :2] + inject_end(pick_edge(low_edges, targets_high))
+    corner_left_low = corner(places[0], places[1], targets_left_low, slice(2, 4), slice(-2, None), -1)
+    corner_left_high = corner(places[0], places[1], targets_left_high, slice(2, 4), slice(0, 2), 0)
+    corner_right_low = corner(places[2], places[3], targets_right_low, slice(0, 2), slice(-2, None), -1)
+    corner_right_high = corner(places[2], places[3], targets_right_high, slice(0, 2), slice(0, 2), 0)
+
+    wide_left = pick(places[0], targets_left)
+    wide_right = pick(places[2], targets_right)
+    wide_low = pick(places[4], targets_low)
+    wide_high = pick(places[5], targets_high)
+    ghost_left = wide_left[:, :, 2:, :] + inject_side(pick_edge(places[1], targets_left))
+    ghost_right = wide_right[:, :, :2, :] + inject_side(pick_edge(places[3], targets_right))
+    ghost_low = wide_low[..., 2:] + inject_end(pick_edge(places[6], targets_low))
+    ghost_high = wide_high[..., :2] + inject_end(pick_edge(places[7], targets_high))
     rate_f1, left_one, right_one, low_one, high_one = jax.vmap(fine_section)(
         fine_box, ghost_left, ghost_right, ghost_low, ghost_high
     )
@@ -304,10 +315,10 @@
     def flagged(source, fine_part, coarse_part):
         return jnp.where(source[0].reshape((-1,) + (1,) * (fine_part.ndim - 1)), fine_part, coarse_part)
 
-    ghost2_left = flagged(targets_left, rim_left, inject_side(pick_edge(left_edges_one, targets_left)))
-    ghost2_right = flagged(targets_right, rim_right, inject_side(pick_edge(right_edges_one, targets_right)))
-    ghost2_low = flagged(targets_low, rim_low, inject_end(pick_edge(high_edges_one, targets_low)))
-    ghost2_high = flagged(targets_high, rim_high, inject_end(pick_edge(low_edges_one, targets_high)))
+    ghost2_left = flagged(targets_left, rim_left, inject_side(pick_edge_in(left_edges_one, (0, coarse_one[:, 0, :].shape), targets_left)))
+    ghost2_right = flagged(targets_right, rim_right, inject_side(pick_edge_in(right_edges_one, (0, coarse_one[:, 0, :].shape), targets_right)))
+    ghost2_low = flagged(targets_low, rim_low, inject_end(pick_edge(places[8], targets_low)))
+    ghost2_high = flagged(targets_high, rim_high, inject_end(pick_edge(places[9], targets_high)))
     rate_f2, left_two, right_two, low_two, high_two = jax.vmap(fine_section)(
         fine_one, ghost2_left, ghost2_right, ghost2_low, ghost2_high
     )
@@ -317,30 +328,19 @@
     reg_low = pair_mean(0.5 * (low_one + low_two))
     reg_high = pair_mean(0.5 * (high_one + high_two))
     restricted = restrict(fine_final)
-    side_regs = extended(jnp.stack([reg_left, reg_right])[None], (("gx", 0),), 1)
-    left_regs = side_regs[0, 1]
-    right_regs = side_regs[2, 0]
-    own_grid = own_table.reshape(count_y, slot_count)
-    left_grid = left_table.reshape(count_y, slot_count)
-    right_grid = right_table.reshape(count_y, slot_count)
-    pieces = gather_rows((restricted, reg_high, reg_low, left_regs, right_regs))
-
-    def select(hit_mask, payload):
-        extra = (1,) * (payload.ndim - 2)
-        return jnp.sum(
-            jnp.where(hit_mask.reshape(hit_mask.shape + extra), payload, 0.0), axis=(0, 1)
-        )
-
-    parts = (
-        select(own_grid == device_row, pieces[0]),
-        select(own_grid == below_block, pieces[1]),
-        select(own_grid == above_block, pieces[2]),
-        select(left_grid == device_row, pieces[3]),
-        select(right_grid == device_row, pieces[4]),
-    )
-    home_mean, got_below, got_above, got_left, got_right = tuple(
-        (extra_part for extra_part in parts)
-    )
+    left_regs = shift_x(reg_right, 1)
+    right_regs = shift_x(reg_left, -1)
+    rows, places = gather_rows((restricted, reg_high, reg_low, left_regs, right_regs))
+
+    def home_pick(place, table_column, block):
+        slot_index = slot_of[table_column, block]
+        return take_slot(rows, place, slot_index // slot_count, slot_index % slot_count)
+
+    home_mean = home_pick(places[0], column, device_row)
+    got_below = home_pick(places[1], column, below_block)
+    got_above = home_pick(places[2], column, above_block)
+    got_left = home_pick(places[3], column_left, device_row)
+    got_right = home_pick(places[4], column_right, device_row)
     face_left = 0.5 * (flux_x1[:, 0] + flux_x2[:, 0])
     face_right = 0.5 * (flux_x1[:, -1] + flux_x2[:, -1])
     face_low = 0.5 * (flux_y1[:, :, 0] + flux_y2[:, :, 0])

time: 289 us -> 262 us (0.907)
  between operations: 16 us -> 80.6 us
  waiting for transfers between devices: 94 us -> 38.3 us
  other arithmetic: 42 us -> 18.4 us
  starting transfers between devices: 69.7 us -> 60.5 us
  local copies, waits for them, and re-layouts: 65.9 us -> 62.1 us
    all_gather x2, waiting for transfers between devices: 83.5 us -> 20.7 us  [gather_rows(): rows = lax.all_gather(flat, 'gy', axis=0, tiled=True)]
    reduce_sum x24 -> x0, other arithmetic: 12.4 us -> none  [the longest x8 7.74 us: select(): jnp.sum(jnp.where(hit_mask.reshape(hit_mask.shape + extra), payload, 0.0)...]
    ppermute x12, starting transfers between devices: 69.6 us -> 60.5 us  [the longest x8 46.1 us: shift_x(): lax.ppermute(values, 'gx', [(i, (i + step) % count) for i in range(count)])]
    broadcast_in_dim x27 -> x0, local copies, waits for them, and re-layouts: 7.27 us -> none  [the longest x9 3.55 us: select(): jnp.where(hit_mask.reshape(hit_mask.shape + extra), payload, 0.0)]
    and x11 -> x0, other arithmetic: 7.2 us -> none  [the longest x8 5.21 us: pick(): (row_index[None, :, None] == fine_row[:, None, None]) & (sub_index[None,...]
    ppermute x12, waiting for transfers between devices: 10.4 us -> 17.5 us  [the longest x8 14.4 us: shift_x(): lax.ppermute(values, 'gx', [(i, (i + step) % count) for i in range(count)])]
    slice x29 -> x33, local copies, waits for them, and re-layouts: 6.51 us -> 13.1 us  [the longest x8 4.95 us: pick(): fine_sub[s]]
    reduce_sum x22 -> x0, local copies, waits for them, and re-layouts: 5.14 us -> none  [the longest x6 4.27 us: select(): jnp.sum(jnp.where(hit_mask.reshape(hit_mask.shape + extra), payload, 0.0)...]
  transfers between devices with their start and end apart: 14 -> 14, of which waited for: 7 -> 4; matrix products, arithmetic and copies ran while one was open for 13% -> 14% of each run, Pallas kernels for 0% -> 0%
where the time goes in v4:
time: 262 us; the launch traced here: 260 us
  between operations  80.6 us (31%)
  local copies, waits for them, and re-layouts  62.1 us (24%)
  starting transfers between devices  60.5 us (23%)
  waiting for transfers between devices  38.3 us (15%)
  other arithmetic  18.4 us (7%)
    ppermute x8, starting transfers between devices, shift_x(): lax.ppermute(values, 'gx', [(i, (i + step) % count) for i in range(count)])  46.1 us
    all_gather x2, waiting for transfers between devices, gather_rows(): rows = lax.all_gather(flat, 'gy', axis=0, tiled=True)  20.7 us
    ppermute x8, waiting for transfers between devices, shift_x(): lax.ppermute(values, 'gx', [(i, (i + step) % count) for i in range(count)])  14.4 us
    ppermute x4, starting transfers between devices, shift_y(): lax.ppermute(values, 'gy', [(i, (i + step) % count) for i in range(count)])  14.3 us
  transfers between devices with their start and end apart: 14, of which 4 were waited for; matrix products, arithmetic and copies ran while one was open for 14% of the time, Pallas kernels for 0%

profile of v4, /device:TPU:1, one launch (start us, length us, event | category | flops | bytes accessed | tf_op | source)
XLA Modules:
  0.0 259.9 jit_solution(12997656712709338944)
XLA Ops:
  7.2 1.0 copy.649
  8.3 0.7 fusion.240
  9.1 4.8 %collective-permute-start = (f32[6912]{0:T(1024)S(1)}, f32[6912]{0:T(1024)S(1)}, u32[]{:S(2)}, u32[]{:S(2)}) collective-permute-start(f32[6912]{0:T(1024)S(1)} %pad_maximum_fusion.36), channel_id=1, source_target_pairs={{0,32},{32,64},{64,96},{96,128},{128,160},{160,192},{192,224},{224... | collective-permute-start | bytes 82952 | tf_op jit(solution)/shard_map/ppermute | solution.py:145
  13.9 17.5 %collective-permute-start.1 = (f32[6912]{0:T(1024)S(1)}, f32[6912]{0:T(1024)S(1)}, u32[]{:S(2)}, u32[]{:S(2)}) collective-permute-start(f32[6912]{0:T(1024)S(1)} %pad_maximum_fusion.37), channel_id=1, source_target_pairs={{0,736},{32,0},{64,32},{96,64},{128,96},{160,128},{192,160},{224,1... | collective-permute-start | bytes 82952 | tf_op jit(solution)/shard_map/ppermute | solution.py:145
  31.4 1.0 fusion.239
  32.4 3.1 %collective-permute-start.2 = (f32[3,32,2]{2,1,0:T(8,128)S(1)}, f32[3,32,2]{2,1,0:T(8,128)S(1)}, u32[]{:S(2)}, u32[]{:S(2)}) collective-permute-start(f32[3,32,2]{2,1,0:T(8,128)S(1)} %get-tuple-element.147), channel_id=1, source_target_pairs={{0,1},{1,2},{2,3},{3,4},{4,5},{5,6},{6,7},{7,8},{8,9},{9,10},{10,1... | collective-permute-start | bytes 2312 | tf_op jit(solution)/shard_map/ppermute | solution.py:150
  35.5 1.9 collective-permute-start.3
  38.5 3.1 %collective-permute-done.3 = f32[3,32,2]{2,1,0:T(8,128)S(1)} collective-permute-done((f32[3,32,2]{2,1,0:T(8,128)S(1)}, f32[3,32,2]{2,1,0:T(8,128)S(1)}, u32[]{:S(2)}, u32[]{:S(2)}) %collective-permute-start.3) | collective-permute-done | bytes 800 | tf_op jit(solution)/shard_map/ppermute | solution.py:150
  43.5 0.6 pad.16
  44.2 0.6 fusion.263
  47.8 0.6 gather_fusion.3
  48.5 0.7 fusion.268
  51.8 0.7 fusion.269
  55.0 0.6 gather_fusion.5
  55.6 0.6 gather_fusion.7
  56.3 0.6 fusion.261
  58.2 0.6 gather_fusion.1
  66.5 0.7 gather_fusion.6
  67.1 0.6 gather_fusion
  67.8 0.6 gather_fusion.15
  68.4 0.6 gather_fusion.13
  70.8 0.7 fusion.257
  72.8 0.7 fusion.256
  79.2 0.6 gather_fusion.8
  79.8 0.6 gather_fusion.9
  91.2 0.6 gather_fusion.12
  91.8 0.6 gather_fusion.10
  92.5 0.6 gather_fusion.14
  93.1 0.6 gather_fusion.2
  93.8 0.6 fusion.266
  95.7 0.7 fusion.264
  97.8 0.7 fusion.267
  101.2 0.7 fusion.265
  104.4 0.6 gather_fusion.4
  119.5 1.8 reshape.1156
  125.0 1.9 collective-permute-start.4
  126.9 9.6 %collective-permute-start.5 = (f32[32,384]{1,0:T(8,128)S(1)}, f32[32,384]{1,0:T(8,128)S(1)}, u32[]{:S(2)}, u32[]{:S(2)}) collective-permute-start(f32[32,384]{1,0:T(8,128)S(1)} %get-tuple-element.76), channel_id=1, source_target_pairs={{0,736},{32,0},{64,32},{96,64},{128,96},{160,128},{192,160},{224,1... | collective-permute-start | bytes 147464 | tf_op jit(solution)/shard_map/ppermute | solution.py:145
  141.0 0.8 fusion.9
  148.3 0.8 fusion.6
  150.2 3.7 %slice.1215 = f32[2,3,32,128]{3,2,0,1:T(8,128)S(1)} slice(f32[2,3,64,256]{3,2,0,1:T(8,128)S(1)} %get-tuple-element.67), slice={[0:2:1], [0:3:1], [0:64:2], [0:256:2]} | slice | bytes 196608 | tf_op jit(solution)/shard_map/slice | solution.py:89
  154.0 3.5 %slice.1216 = f32[2,3,32,128]{3,2,0,1:T(8,128)S(1)} slice(f32[2,3,64,256]{3,2,0,1:T(8,128)S(1)} %get-tuple-element.67), slice={[0:2:1], [0:3:1], [1:64:2], [0:256:2]} | slice | bytes 196608 | tf_op jit(solution)/shard_map/slice | solution.py:90
  157.5 3.5 %slice.1217 = f32[2,3,32,128]{3,2,0,1:T(8,128)S(1)} slice(f32[2,3,64,256]{3,2,0,1:T(8,128)S(1)} %get-tuple-element.67), slice={[0:2:1], [0:3:1], [0:64:2], [1:256:2]} | slice | bytes 196608 | tf_op jit(solution)/shard_map/slice | solution.py:91
  161.0 3.5 %slice.1218 = f32[2,3,32,128]{3,2,0,1:T(8,128)S(1)} slice(f32[2,3,64,256]{3,2,0,1:T(8,128)S(1)} %get-tuple-element.67), slice={[0:2:1], [0:3:1], [1:64:2], [1:256:2]} | slice | bytes 196608 | tf_op jit(solution)/shard_map/slice | solution.py:91
  164.5 5.2 %collective-permute-start.7 = (f32[2,3,128]{2,0,1:T(2,128)S(1)}, f32[2,3,128]{2,0,1:T(2,128)S(1)}, u32[]{:S(2)}, u32[]{:S(2)}) collective-permute-start(f32[2,3,128]{2,0,1:T(2,128)S(1)} %add_multiply_fusion.2), channel_id=1, source_target_pairs={{0,736},{32,0},{64,32},{96,64},{128,96},{160,128},{192,160},{224,1... | collective-permute-start | bytes 9224 | tf_op jit(solution)/shard_map/ppermute | solution.py:145
  169.7 1.9 collective-permute-start.6
  171.9 8.2 %collective-permute-done.6 = f32[2,3,128]{2,0,1:T(2,128)S(1)} collective-permute-done((f32[2,3,128]{2,0,1:T(2,128)S(1)}, f32[2,3,128]{2,0,1:T(2,128)S(1)}, u32[]{:S(2)}, u32[]{:S(2)}) %collective-permute-start.6) | collective-permute-done | bytes 3104 | tf_op jit(solution)/shard_map/ppermute | solution.py:145
  180.2 0.7 pad.17
  180.9 0.7 fusion.243
  195.6 0.7 fusion.250
  196.3 7.3 %collective-permute-start.10 = (f32[3,32,2]{2,1,0:T(8,128)S(1)}, f32[3,32,2]{2,1,0:T(8,128)S(1)}, u32[]{:S(2)}, u32[]{:S(2)}) collective-permute-start(f32[3,32,2]{2,1,0:T(8,128)S(1)} %get-tuple-element.143), channel_id=1, source_target_pairs={{0,31},{1,0},{2,1},{3,2},{4,3},{5,4},{6,5},{7,6},{8,7},{9,8},{10,9... | collective-permute-start | bytes 2312 | tf_op jit(solution)/shard_map/ppermute | solution.py:150
  203.7 1.9 collective-permute-start.9
  205.6 1.9 collective-permute-start.11
  207.5 3.4 %collective-permute-start.8 = (f32[3,2,128]{2,1,0:T(2,128)S(1)}, f32[3,2,128]{2,1,0:T(2,128)S(1)}, u32[]{:S(2)}, u32[]{:S(2)}) collective-permute-start(f32[3,2,128]{2,1,0:T(2,128)S(1)} %get-tuple-element.141), channel_id=1, source_target_pairs={{0,32},{32,64},{64,96},{96,128},{128,160},{160,192},{192,224},{224... | collective-permute-start | bytes 9224 | tf_op jit(solution)/shard_map/ppermute | solution.py:145
  211.2 0.6 pad_maximum_fusion.28
  211.8 6.2 %collective-permute-done.8 = f32[3,2,128]{2,1,0:T(2,128)S(1)} collective-permute-done((f32[3,2,128]{2,1,0:T(2,128)S(1)}, f32[3,2,128]{2,1,0:T(2,128)S(1)}, u32[]{:S(2)}, u32[]{:S(2)}) %collective-permute-start.8) | collective-permute-done | bytes 3104 | tf_op jit(solution)/shard_map/ppermute | solution.py:145
  219.6 0.8 copy.567
  220.3 20.7 %all-gather.7.cloned.1.call-done = f32[851968]{0:T(1024)} async-done(((f32[26624]{0:T(1024)}), f32[851968]{0:T(1024)}) %all-gather.7.cloned.1.call-update) | async-done | bytes 3407888 | tf_op jit(solution)/shard_map/all_gather | solution.py:118
  241.0 2.2 reshape.1157
  243.3 0.7 dynamic-slice_reduce_fusion.21
  244.0 0.8 reshape.1158
  244.8 1.5 reshape.1159
  246.4 2.2 fusion.72
  248.6 2.2 broadcast_select_fusion.5
  250.8 2.2 fusion.79
  (286 shorter events, 28.3 us)
Async XLA Ops:
  7.2 30.5 %copy-start = (f32[3,32,128]{2,1,0:T(8,128)S(1)}, f32[3,32,128]{2,1,0:T(8,128)}, u32[]{:S(2)}) copy-start(f32[3,32,128]{2,1,0:T(8,128)} %param.3) | copy-start | bytes 147460
  7.2 30.7 %copy-start.9 = (s32[24,64]{1,0:T(8,128)S(1)}, s32[24,64]{1,0:T(8,128)}, u32[]{:S(2)}) copy-start(s32[24,64]{1,0:T(8,128)} %param.5) | copy-start | bytes 18436
  7.2 112.3 %all-gather.5.cloned.1.call-start = ((), (), s32[]{:S(2)}) async-start(), calls=%async_computation | async-start | bytes 2297856 | tf_op jit(solution)/shard_map/all_gather | solution.py:118
  9.1 32.8 %collective-permute-start = (f32[6912]{0:T(1024)S(1)}, f32[6912]{0:T(1024)S(1)}, u32[]{:S(2)}, u32[]{:S(2)}) collective-permute-start(f32[6912]{0:T(1024)S(1)} %pad_maximum_fusion.36), channel_id=1, source_target_pairs={{0,32},{32,64},{64,96},{96,128},{128,160},{160,192},{192,224},{224... | collective-permute-start | bytes 82952 | tf_op jit(solution)/shard_map/ppermute | solution.py:145
  13.9 28.0 %collective-permute-start.1 = (f32[6912]{0:T(1024)S(1)}, f32[6912]{0:T(1024)S(1)}, u32[]{:S(2)}, u32[]{:S(2)}) collective-permute-start(f32[6912]{0:T(1024)S(1)} %pad_maximum_fusion.37), channel_id=1, source_target_pairs={{0,736},{32,0},{64,32},{96,64},{128,96},{160,128},{192,160},{224,1... | collective-permute-start | bytes 82952 | tf_op jit(solution)/shard_map/ppermute | solution.py:145
  32.4 9.2 %collective-permute-start.2 = (f32[3,32,2]{2,1,0:T(8,128)S(1)}, f32[3,32,2]{2,1,0:T(8,128)S(1)}, u32[]{:S(2)}, u32[]{:S(2)}) collective-permute-start(f32[3,32,2]{2,1,0:T(8,128)S(1)} %get-tuple-element.147), channel_id=1, source_target_pairs={{0,1},{1,2},{2,3},{3,4},{4,5},{5,6},{6,7},{7,8},{8,9},{9,10},{10,1... | collective-permute-start | bytes 2312 | tf_op jit(solution)/shard_map/ppermute | solution.py:150
  35.5 6.1 %collective-permute-start.3 = (f32[3,32,2]{2,1,0:T(8,128)S(1)}, f32[3,32,2]{2,1,0:T(8,128)S(1)}, u32[]{:S(2)}, u32[]{:S(2)}) collective-permute-start(f32[3,32,2]{2,1,0:T(8,128)S(1)} %get-tuple-element.148), channel_id=1, source_target_pairs={{0,31},{1,0},{2,1},{3,2},{4,3},{5,4},{6,5},{7,6},{8,7},{9,8},{10,9... | collective-permute-start | bytes 2312 | tf_op jit(solution)/shard_map/ppermute | solution.py:150
  41.9 4.9 %copy-start.2 = (f32[3,32,129]{2,1,0:T(8,128)}, f32[3,32,129]{2,1,0:T(8,128)S(1)}, u32[]{:S(2)}) copy-start(f32[3,32,129]{2,1,0:T(8,128)S(1)} %pad_maximum_fusion.27) | copy-start | bytes 148612
  42.3 0.6 copy-start.3
  42.3 0.6 copy-start.4
  42.3 0.7 copy-start.5
  44.2 196.9 %all-gather.7.cloned.1.call-start = ((), (), s32[]{:S(2)}) async-start(), calls=%async_computation.1 | async-start | bytes 3514368 | tf_op jit(solution)/shard_map/all_gather | solution.py:118
  125.0 17.3 %collective-permute-start.4 = (f32[32,384]{1,0:T(8,128)S(1)}, f32[32,384]{1,0:T(8,128)S(1)}, u32[]{:S(2)}, u32[]{:S(2)}) collective-permute-start(f32[32,384]{1,0:T(8,128)S(1)} %get-tuple-element.75), channel_id=1, source_target_pairs={{0,32},{32,64},{64,96},{96,128},{128,160},{160,192},{192,224},{224... | collective-permute-start | bytes 147464 | tf_op jit(solution)/shard_map/ppermute | solution.py:145
  126.9 15.4 %collective-permute-start.5 = (f32[32,384]{1,0:T(8,128)S(1)}, f32[32,384]{1,0:T(8,128)S(1)}, u32[]{:S(2)}, u32[]{:S(2)}) collective-permute-start(f32[32,384]{1,0:T(8,128)S(1)} %get-tuple-element.76), channel_id=1, source_target_pairs={{0,736},{32,0},{64,32},{96,64},{128,96},{160,128},{192,160},{224,1... | collective-permute-start | bytes 147464 | tf_op jit(solution)/shard_map/ppermute | solution.py:145
  145.0 1.0 copy-start.1
  164.5 7.4 %collective-permute-start.7 = (f32[2,3,128]{2,0,1:T(2,128)S(1)}, f32[2,3,128]{2,0,1:T(2,128)S(1)}, u32[]{:S(2)}, u32[]{:S(2)}) collective-permute-start(f32[2,3,128]{2,0,1:T(2,128)S(1)} %add_multiply_fusion.2), channel_id=1, source_target_pairs={{0,736},{32,0},{64,32},{96,64},{128,96},{160,128},{192,160},{224,1... | collective-permute-start | bytes 9224 | tf_op jit(solution)/shard_map/ppermute | solution.py:145
  169.7 10.4 %collective-permute-start.6 = (f32[2,3,128]{2,0,1:T(2,128)S(1)}, f32[2,3,128]{2,0,1:T(2,128)S(1)}, u32[]{:S(2)}, u32[]{:S(2)}) collective-permute-start(f32[2,3,128]{2,0,1:T(2,128)S(1)} %add_multiply_fusion.3), channel_id=1, source_target_pairs={{0,32},{32,64},{64,96},{96,128},{128,160},{160,192},{192,224},{224... | collective-permute-start | bytes 9224 | tf_op jit(solution)/shard_map/ppermute | solution.py:145
  196.3 14.6 %collective-permute-start.10 = (f32[3,32,2]{2,1,0:T(8,128)S(1)}, f32[3,32,2]{2,1,0:T(8,128)S(1)}, u32[]{:S(2)}, u32[]{:S(2)}) collective-permute-start(f32[3,32,2]{2,1,0:T(8,128)S(1)} %get-tuple-element.143), channel_id=1, source_target_pairs={{0,31},{1,0},{2,1},{3,2},{4,3},{5,4},{6,5},{7,6},{8,7},{9,8},{10,9... | collective-permute-start | bytes 2312 | tf_op jit(solution)/shard_map/ppermute | solution.py:150
  203.7 7.3 %collective-permute-start.9 = (f32[3,32,2]{2,1,0:T(8,128)S(1)}, f32[3,32,2]{2,1,0:T(8,128)S(1)}, u32[]{:S(2)}, u32[]{:S(2)}) collective-permute-start(f32[3,32,2]{2,1,0:T(8,128)S(1)} %get-tuple-element.144), channel_id=1, source_target_pairs={{0,1},{1,2},{2,3},{3,4},{4,5},{5,6},{6,7},{7,8},{8,9},{9,10},{10,1... | collective-permute-start | bytes 2312 | tf_op jit(solution)/shard_map/ppermute | solution.py:150
  205.6 6.2 %collective-permute-start.11 = (f32[3,2,128]{2,1,0:T(2,128)S(1)}, f32[3,2,128]{2,1,0:T(2,128)S(1)}, u32[]{:S(2)}, u32[]{:S(2)}) collective-permute-start(f32[3,2,128]{2,1,0:T(2,128)S(1)} %get-tuple-element.142), channel_id=1, source_target_pairs={{0,736},{32,0},{64,32},{96,64},{128,96},{160,128},{192,160},{224,1... | collective-permute-start | bytes 9224 | tf_op jit(solution)/shard_map/ppermute | solution.py:145
  207.5 10.5 %collective-permute-start.8 = (f32[3,2,128]{2,1,0:T(2,128)S(1)}, f32[3,2,128]{2,1,0:T(2,128)S(1)}, u32[]{:S(2)}, u32[]{:S(2)}) collective-permute-start(f32[3,2,128]{2,1,0:T(2,128)S(1)} %get-tuple-element.141), channel_id=1, source_target_pairs={{0,32},{32,64},{64,96},{96,128},{128,160},{160,192},{192,224},{224... | collective-permute-start | bytes 9224 | tf_op jit(solution)/shard_map/ppermute | solution.py:145
  218.3 0.6 copy-start.6
  218.4 1.2 copy-start.7
  218.4 1.2 copy-start.8
Sparse Core Ops, SparseCore 0:
  44.3 58.7 all-gather.4
  181.0 60.0 all-gather.6

commit v5 on v4

--- a/solution.py
+++ b/solution.py
@@ -188,14 +188,16 @@
     targets_right_high = fine_source(column_right, (parent + 1) % count_y)
 
     strip_size = fine_box[:, :, :4, :].size
-    right_pack = jnp.concatenate([fine_box[:, :, -4:, :].reshape(-1), coarse_state[:, -2:, :].reshape(-1)])
-    left_pack = jnp.concatenate([fine_box[:, :, :4, :].reshape(-1), coarse_state[:, :2, :].reshape(-1)])
+    right_pack = jnp.concatenate([fine_box[:, :, -4:, :].reshape(-1), coarse_state[:, -3:, :].reshape(-1)])
+    left_pack = jnp.concatenate([fine_box[:, :, :4, :].reshape(-1), coarse_state[:, :3, :].reshape(-1)])
     from_left = shift_x(right_pack, 1)
     from_right = shift_x(left_pack, -1)
     strip_shape = fine_box[:, :, :4, :].shape
-    rim_shape = coarse_state[:, :2, :].shape
-    left_rim = from_left[strip_size:].reshape(rim_shape)
-    right_rim = from_right[strip_size:].reshape(rim_shape)
+    rim_shape = coarse_state[:, :3, :].shape
+    left_rows = from_left[strip_size:].reshape(rim_shape)
+    right_rows = from_right[strip_size:].reshape(rim_shape)
+    left_rim = left_rows[:, 1:, :]
+    right_rim = right_rows[:, :2, :]
 
     def coarse_padded(field, ghost_left, ghost_right):
         ghost_low = shift_y(field[:, :, -2:], 1)
@@ -211,22 +213,19 @@
 
     parts = (
         from_left[:strip_size].reshape(strip_shape),
-        left_rim[:, 1, :],
+        left_rows,
         from_right[:strip_size].reshape(strip_shape),
-        right_rim[:, 0, :],
+        right_rows,
         fine_box[..., -4:],
         fine_box[..., :4],
         coarse_state[:, :, -1],
         coarse_state[:, :, 0],
         coarse_one[:, :, -1],
         coarse_one[:, :, 0],
-        coarse_one[:, -1, :],
-        coarse_one[:, 0, :],
+        coarse_state[:, :2, :],
+        coarse_state[:, -2:, :],
     )
     rows, places = gather_rows(parts)
-    column_edges_one = lax.slice_in_dim(rows, places[10][0], places[10][0] + 2 * coarse_one[:, 0, :].size, axis=1)
-    left_edges_one = shift_x(column_edges_one[:, : coarse_one[:, 0, :].size], 1)
-    right_edges_one = shift_x(column_edges_one[:, coarse_one[:, 0, :].size :], -1)
 
     def pick(place, source):
         flag, fine_row, fine_sub, _ = source
@@ -241,22 +240,22 @@
     def pick_edge(place, source):
         return pick_edge_in(rows, place, source)
 
-    def corner(place, edge_place, source, row_slice, col_slice, edge_index):
+    def corner(place, edge_place, source, row_slice, col_slice, edge_row, edge_index):
         fine_part = pick(place, source)[:, :, row_slice, col_slice]
-        edge_part = pick_edge(edge_place, source)[:, :, edge_index]
+        edge_part = pick_edge(edge_place, source)[:, :, edge_row, edge_index]
         return fine_part + edge_part[:, :, None, None]
 
-    corner_left_low = corner(places[0], places[1], targets_left_low, slice(2, 4), slice(-2, None), -1)
-    corner_left_high = corner(places[0], places[1], targets_left_high, slice(2, 4), slice(0, 2), 0)
-    corner_right_low = corner(places[2], places[3], targets_right_low, slice(0, 2), slice(-2, None), -1)
-    corner_right_high = corner(places[2], places[3], targets_right_high, slice(0, 2), slice(0, 2), 0)
+    corner_left_low = corner(places[0], places[1], targets_left_low, slice(2, 4), slice(-2, None), 2, -1)
+    corner_left_high = corner(places[0], places[1], targets_left_high, slice(2, 4), slice(0, 2), 2, 0)
+    corner_right_low = corner(places[2], places[3], targets_right_low, slice(0, 2), slice(-2, None), 0, -1)
+    corner_right_high = corner(places[2], places[3], targets_right_high, slice(0, 2), slice(0, 2), 0, 0)
 
     wide_left = pick(places[0], targets_left)
     wide_right = pick(places[2], targets_right)
     wide_low = pick(places[4], targets_low)
     wide_high = pick(places[5], targets_high)
-    ghost_left = wide_left[:, :, 2:, :] + inject_side(pick_edge(places[1], targets_left))
-    ghost_right = wide_right[:, :, :2, :] + inject_side(pick_edge(places[3], targets_right))
+    ghost_left = wide_left[:, :, 2:, :] + inject_side(pick_edge(places[1], targets_left)[:, :, 2, :])
+    ghost_right = wide_right[:, :, :2, :] + inject_side(pick_edge(places[3], targets_right)[:, :, 0, :])
     ghost_low = wide_low[..., 2:] + inject_end(pick_edge(places[6], targets_low))
     ghost_high = wide_high[..., :2] + inject_end(pick_edge(places[7], targets_high))
     rate_f1, left_one, right_one, low_one, high_one = jax.vmap(fine_section)(
@@ -312,11 +311,35 @@
     rim_low = wide_low[..., 2:] + jax.vmap(rim_rate)(padded_low)
     rim_high = wide_high[..., :2] + jax.vmap(rim_rate)(padded_high)
 
+    def side_step_one(block, far_place, far_row, near_place, far_first):
+        far = take_row(rows, far_place, block)
+        near = take_row(rows, near_place, block)
+        below = take_row(rows, far_place, (block - 1) % count_y)[:, far_row, -2:]
+        above = take_row(rows, far_place, (block + 1) % count_y)[:, far_row, :2]
+        zero_band = jnp.zeros((far.shape[0], 2, 2), jnp.float32)
+        line = jnp.concatenate([below[:, None, :], far[:, far_row : far_row + 1, :], above[:, None, :]], axis=2)
+        if far_first:
+            outer = jnp.concatenate([zero_band, far[:, :2, :], zero_band], axis=2)
+            inner = jnp.concatenate([zero_band, near, zero_band], axis=2)
+            padded = jnp.concatenate([outer, line, inner], axis=1)
+        else:
+            inner = jnp.concatenate([zero_band, near, zero_band], axis=2)
+            outer = jnp.concatenate([zero_band, far[:, 1:, :], zero_band], axis=2)
+            padded = jnp.concatenate([inner, line, outer], axis=1)
+        return far[:, far_row, :] + advance_rate(padded, LAM_COARSE)[0][:, 0, :]
+
+    edge_one_left = jnp.stack(
+        [side_step_one(parent[s], places[1], 2, places[10], True) for s in range(slot_count)]
+    )
+    edge_one_right = jnp.stack(
+        [side_step_one(parent[s], places[3], 0, places[11], False) for s in range(slot_count)]
+    )
+
     def flagged(source, fine_part, coarse_part):
         return jnp.where(source[0].reshape((-1,) + (1,) * (fine_part.ndim - 1)), fine_part, coarse_part)
 
-    ghost2_left = flagged(targets_left, rim_left, inject_side(pick_edge_in(left_edges_one, (0, coarse_one[:, 0, :].shape), targets_left)))
-    ghost2_right = flagged(targets_right, rim_right, inject_side(pick_edge_in(right_edges_one, (0, coarse_one[:, 0, :].shape), targets_right)))
+    ghost2_left = flagged(targets_left, rim_left, inject_side(edge_one_left))
+    ghost2_right = flagged(targets_right, rim_right, inject_side(edge_one_right))
     ghost2_low = flagged(targets_low, rim_low, inject_end(pick_edge(places[8], targets_low)))
     ghost2_high = flagged(targets_high, rim_high, inject_end(pick_edge(places[9], targets_high)))
     rate_f2, left_two, right_two, low_two, high_two = jax.vmap(fine_section)(

time: 262 us -> 288 us (1.099)
  other arithmetic: 18.4 us -> 42.3 us
  local copies, waits for them, and re-layouts: 62.1 us -> 72.8 us
  starting transfers between devices: 60.5 us -> 54 us
  waiting for transfers between devices: 38.3 us -> 33.6 us
    ppermute x8 -> x6, starting transfers between devices: 46.1 us -> 39.2 us  [shift_x(): lax.ppermute(values, 'gx', [(i, (i + step) % count) for i in range(count)])]
    ppermute x8 -> x6, waiting for transfers between devices: 14.4 us -> 8.6 us  [shift_x(): lax.ppermute(values, 'gx', [(i, (i + step) % count) for i in range(count)])]
    select_n x8, other arithmetic: 0.59 us -> 6.01 us  [pick_edge_in(): return jnp.where(flag.reshape((-1,) + (1,) * (taken.ndim - 1)), 0.0, taken)]
    another operation x8 -> x20, local copies, waits for them, and re-layouts: 0.65 us -> 4.52 us  [pick_edge_in(): jnp.stack([take_row(table, place, edge_row[s]) for s in range(slot_count)])]
    gather x8, local copies, waits for them, and re-layouts: 5.16 us -> 8.55 us  [fine_source(): flag = refined[table_column, block]]
    all_gather x2, waiting for transfers between devices: 20.7 us -> 24.1 us  [gather_rows(): rows = lax.all_gather(flat, 'gy', axis=0, tiled=True)]
    add x0 -> x4, other arithmetic: none -> 3.08 us  [side_step_one(): return far[:, far_row, :] + advance_rate(padded, LAM_COARSE)[0][:, 0, :]]
  transfers between devices with their start and end apart: 14 -> 12, of which waited for: 4 -> 4; matrix products, arithmetic and copies ran while one was open for 14% -> 12% of each run, Pallas kernels for 0% -> 0%
where the time goes in v5:
time: 288 us; the launch traced here: 285 us
  between operations  82.7 us (29%)
  local copies, waits for them, and re-layouts  72.8 us (25%)
  starting transfers between devices  54 us (19%)
  other arithmetic  42.3 us (15%)
  waiting for transfers between devices  33.6 us (12%)
    ppermute x6, starting transfers between devices, shift_x(): lax.ppermute(values, 'gx', [(i, (i + step) % count) for i in range(count)])  39.2 us
    all_gather x2, waiting for transfers between devices, gather_rows(): rows = lax.all_gather(flat, 'gy', axis=0, tiled=True)  24.1 us
    ppermute x4, starting transfers between devices, shift_y(): lax.ppermute(values, 'gy', [(i, (i + step) % count) for i in range(count)])  14.7 us
    ppermute x6, waiting for transfers between devices, shift_x(): lax.ppermute(values, 'gx', [(i, (i + step) % count) for i in range(count)])  8.6 us
    gather x8, local copies, waits for them, and re-layouts, fine_source(): flag = refined[table_column, block]  8.55 us
    select_n x8, other arithmetic, pick_edge_in(): return jnp.where(flag.reshape((-1,) + (1,) * (taken.ndim - 1)), 0.0, taken)  6.01 us
  transfers between devices with their start and end apart: 12, of which 4 were waited for; matrix products, arithmetic and copies ran while one was open for 12% of the time, Pallas kernels for 0%

profile of v5, /device:TPU:1, one launch (start us, length us, event | category | flops | bytes accessed | tf_op | source)
XLA Modules:
  0.0 285.5 jit_solution(2776933786065725338)
XLA Ops:
  7.2 1.0 copy.655
  8.3 0.7 fusion.272
  9.0 4.8 %collective-permute-start = (f32[7296]{0:T(1024)S(1)}, f32[7296]{0:T(1024)S(1)}, u32[]{:S(2)}, u32[]{:S(2)}) collective-permute-start(f32[7296]{0:T(1024)S(1)} %pad_maximum_fusion.36), channel_id=1, source_target_pairs={{0,32},{32,64},{64,96},{96,128},{128,160},{160,192},{192,224},{224... | collective-permute-start | bytes 87560 | tf_op jit(solution)/shard_map/ppermute | solution.py:145
  13.9 17.5 %collective-permute-start.1 = (f32[7296]{0:T(1024)S(1)}, f32[7296]{0:T(1024)S(1)}, u32[]{:S(2)}, u32[]{:S(2)}) collective-permute-start(f32[7296]{0:T(1024)S(1)} %pad_maximum_fusion.37), channel_id=1, source_target_pairs={{0,736},{32,0},{64,32},{96,64},{128,96},{160,128},{192,160},{224,1... | collective-permute-start | bytes 87560 | tf_op jit(solution)/shard_map/ppermute | solution.py:145
  31.4 1.0 fusion.271
  32.4 3.1 %collective-permute-start.2 = (f32[3,32,2]{2,1,0:T(8,128)S(1)}, f32[3,32,2]{2,1,0:T(8,128)S(1)}, u32[]{:S(2)}, u32[]{:S(2)}) collective-permute-start(f32[3,32,2]{2,1,0:T(8,128)S(1)} %get-tuple-element.153), channel_id=1, source_target_pairs={{0,1},{1,2},{2,3},{3,4},{4,5},{5,6},{6,7},{7,8},{8,9},{9,10},{10,1... | collective-permute-start | bytes 2312 | tf_op jit(solution)/shard_map/ppermute | solution.py:150
  35.5 1.9 collective-permute-start.3
  37.6 0.7 fusion.270
  38.3 1.0 slice_reduce_fusion.2
  39.4 0.8 constant_dynamic-update-slice_fusion.1
  40.7 0.9 collective-permute-done.3
  95.3 1.2 gather_fusion.8
  101.8 1.2 gather_fusion.12
  102.9 1.2 gather_fusion.10
  104.1 1.2 gather_fusion.14
  105.4 1.2 gather_fusion.2
  106.6 1.2 gather_fusion.4
  107.9 0.7 copy.525
  124.1 2.1 reshape.1348
  126.2 0.8 dynamic-slice_reduce_fusion.22
  127.2 0.7 dynamic-slice_reduce_fusion.33
  139.4 0.7 broadcast_select_fusion.7
  140.6 0.7 stack_reshape.134
  142.9 0.7 broadcast_select_fusion.6
  143.8 0.7 broadcast_select_fusion.4
  144.7 0.7 fusion.164
  146.1 0.7 fusion.162
  146.9 0.7 fusion.146
  149.2 0.7 fusion.237
  151.9 0.8 add_bitcast_fusion.1
  154.0 0.8 add_bitcast_fusion
  155.3 0.8 broadcast_select_fusion.8
  156.5 0.8 broadcast_select_fusion.9
  159.1 0.8 add_bitcast_fusion.3
  160.0 0.8 add_bitcast_fusion.2
  161.5 0.8 maximum_select_fusion.6
  162.7 0.8 stack_reshape.112
  163.6 0.8 stack_reshape.113
  164.5 0.8 maximum_select_fusion.2
  165.5 0.8 fusion.106
  166.5 0.8 broadcast_select_fusion.3
  167.8 0.8 maximum_select_fusion.7
  170.7 0.8 fusion.9
  173.2 0.8 copy-done.1
  176.2 0.8 fusion.6
  178.4 3.5 %slice.1620 = f32[2,3,32,128]{3,2,0,1:T(8,128)S(1)} slice(f32[2,3,64,256]{3,2,0,1:T(8,128)S(1)} %get-tuple-element.69), slice={[0:2:1], [0:3:1], [0:64:2], [0:256:2]} | slice | bytes 196608 | tf_op jit(solution)/shard_map/slice | solution.py:89
  181.9 3.5 %slice.1621 = f32[2,3,32,128]{3,2,0,1:T(8,128)S(1)} slice(f32[2,3,64,256]{3,2,0,1:T(8,128)S(1)} %get-tuple-element.69), slice={[0:2:1], [0:3:1], [1:64:2], [0:256:2]} | slice | bytes 196608 | tf_op jit(solution)/shard_map/slice | solution.py:90
  185.4 3.5 %slice.1622 = f32[2,3,32,128]{3,2,0,1:T(8,128)S(1)} slice(f32[2,3,64,256]{3,2,0,1:T(8,128)S(1)} %get-tuple-element.69), slice={[0:2:1], [0:3:1], [0:64:2], [1:256:2]} | slice | bytes 196608 | tf_op jit(solution)/shard_map/slice | solution.py:91
  188.9 3.5 %slice.1623 = f32[2,3,32,128]{3,2,0,1:T(8,128)S(1)} slice(f32[2,3,64,256]{3,2,0,1:T(8,128)S(1)} %get-tuple-element.69), slice={[0:2:1], [0:3:1], [1:64:2], [1:256:2]} | slice | bytes 196608 | tf_op jit(solution)/shard_map/slice | solution.py:91
  192.4 3.6 %collective-permute-start.5 = (f32[2,3,128]{2,0,1:T(2,128)S(1)}, f32[2,3,128]{2,0,1:T(2,128)S(1)}, u32[]{:S(2)}, u32[]{:S(2)}) collective-permute-start(f32[2,3,128]{2,0,1:T(2,128)S(1)} %add_multiply_fusion.2), channel_id=1, source_target_pairs={{0,736},{32,0},{64,32},{96,64},{128,96},{160,128},{192,160},{224,1... | collective-permute-start | bytes 9224 | tf_op jit(solution)/shard_map/ppermute | solution.py:145
  196.1 1.9 collective-permute-start.4
  198.3 8.2 %collective-permute-done.4 = f32[2,3,128]{2,0,1:T(2,128)S(1)} collective-permute-done((f32[2,3,128]{2,0,1:T(2,128)S(1)}, f32[2,3,128]{2,0,1:T(2,128)S(1)}, u32[]{:S(2)}, u32[]{:S(2)}) %collective-permute-start.4) | collective-permute-done | bytes 3104 | tf_op jit(solution)/shard_map/ppermute | solution.py:145
  221.1 4.1 %collective-permute-start.7 = (f32[3,32,2]{2,1,0:T(8,128)S(1)}, f32[3,32,2]{2,1,0:T(8,128)S(1)}, u32[]{:S(2)}, u32[]{:S(2)}) collective-permute-start(f32[3,32,2]{2,1,0:T(8,128)S(1)} %get-tuple-element.148), channel_id=1, source_target_pairs={{0,1},{1,2},{2,3},{3,4},{4,5},{5,6},{6,7},{7,8},{8,9},{9,10},{10,1... | collective-permute-start | bytes 2312 | tf_op jit(solution)/shard_map/ppermute | solution.py:150
  225.3 5.5 %collective-permute-start.8 = (f32[3,32,2]{2,1,0:T(8,128)S(1)}, f32[3,32,2]{2,1,0:T(8,128)S(1)}, u32[]{:S(2)}, u32[]{:S(2)}) collective-permute-start(f32[3,32,2]{2,1,0:T(8,128)S(1)} %get-tuple-element.147), channel_id=1, source_target_pairs={{0,31},{1,0},{2,1},{3,2},{4,3},{5,4},{6,5},{7,6},{8,7},{9,8},{10,9... | collective-permute-start | bytes 2312 | tf_op jit(solution)/shard_map/ppermute | solution.py:150
  230.8 1.9 collective-permute-start.6
  232.8 9.4 %collective-permute-start.9 = (f32[3,2,128]{2,1,0:T(2,128)S(1)}, f32[3,2,128]{2,1,0:T(2,128)S(1)}, u32[]{:S(2)}, u32[]{:S(2)}) collective-permute-start(f32[3,2,128]{2,1,0:T(2,128)S(1)} %get-tuple-element.146), channel_id=1, source_target_pairs={{0,736},{32,0},{64,32},{96,64},{128,96},{160,128},{192,160},{224,1... | collective-permute-start | bytes 9224 | tf_op jit(solution)/shard_map/ppermute | solution.py:145
  243.2 0.8 copy.571
  244.0 24.1 %all-gather.7.cloned.1.call-done = f32[851968]{0:T(1024)} async-done(((f32[26624]{0:T(1024)}), f32[851968]{0:T(1024)}) %all-gather.7.cloned.1.call-update) | async-done | bytes 3407888 | tf_op jit(solution)/shard_map/all_gather | solution.py:118
  268.1 3.5 %reshape.1349 = f32[32,26624]{1,0:T(8,128)} reshape(f32[851968]{0:T(1024)} %all-gather.7.cloned.1.call-done) | data formatting | bytes 6815744 | tf_op jit(solution)/shard_map/all_gather | solution.py:118
  271.5 0.9 dynamic-slice_reduce_fusion.37
  272.8 1.2 dynamic_slice.249
  273.9 1.2 fusion.72
  275.2 2.1 broadcast_select_fusion.11
  277.2 1.4 fusion.79
  (391 shorter events, 55.3 us)
Async XLA Ops:
  7.2 34.4 %copy-start = (f32[3,32,128]{2,1,0:T(8,128)S(1)}, f32[3,32,128]{2,1,0:T(8,128)}, u32[]{:S(2)}) copy-start(f32[3,32,128]{2,1,0:T(8,128)} %param.3) | copy-start | bytes 147460
  7.2 116.9 %all-gather.5.cloned.1.call-start = ((), (), s32[]{:S(2)}) async-start(), calls=%async_computation | async-start | bytes 2703360 | tf_op jit(solution)/shard_map/all_gather | solution.py:118
  9.0 32.8 %collective-permute-start = (f32[7296]{0:T(1024)S(1)}, f32[7296]{0:T(1024)S(1)}, u32[]{:S(2)}, u32[]{:S(2)}) collective-permute-start(f32[7296]{0:T(1024)S(1)} %pad_maximum_fusion.36), channel_id=1, source_target_pairs={{0,32},{32,64},{64,96},{96,128},{128,160},{160,192},{192,224},{224... | collective-permute-start | bytes 87560 | tf_op jit(solution)/shard_map/ppermute | solution.py:145
  13.9 28.0 %collective-permute-start.1 = (f32[7296]{0:T(1024)S(1)}, f32[7296]{0:T(1024)S(1)}, u32[]{:S(2)}, u32[]{:S(2)}) collective-permute-start(f32[7296]{0:T(1024)S(1)} %pad_maximum_fusion.37), channel_id=1, source_target_pairs={{0,736},{32,0},{64,32},{96,64},{128,96},{160,128},{192,160},{224,1... | collective-permute-start | bytes 87560 | tf_op jit(solution)/shard_map/ppermute | solution.py:145
  32.4 9.2 %collective-permute-start.2 = (f32[3,32,2]{2,1,0:T(8,128)S(1)}, f32[3,32,2]{2,1,0:T(8,128)S(1)}, u32[]{:S(2)}, u32[]{:S(2)}) collective-permute-start(f32[3,32,2]{2,1,0:T(8,128)S(1)} %get-tuple-element.153), channel_id=1, source_target_pairs={{0,1},{1,2},{2,3},{3,4},{4,5},{5,6},{6,7},{7,8},{8,9},{9,10},{10,1... | collective-permute-start | bytes 2312 | tf_op jit(solution)/shard_map/ppermute | solution.py:150
  35.5 8.1 %copy-start.2 = (s32[24,64]{1,0:T(8,128)S(1)}, s32[24,64]{1,0:T(8,128)}, u32[]{:S(2)}) copy-start(s32[24,64]{1,0:T(8,128)} %param.5) | copy-start | bytes 18436
  35.5 6.1 %collective-permute-start.3 = (f32[3,32,2]{2,1,0:T(8,128)S(1)}, f32[3,32,2]{2,1,0:T(8,128)S(1)}, u32[]{:S(2)}, u32[]{:S(2)}) collective-permute-start(f32[3,32,2]{2,1,0:T(8,128)S(1)} %get-tuple-element.154), channel_id=1, source_target_pairs={{0,31},{1,0},{2,1},{3,2},{4,3},{5,4},{6,5},{7,6},{8,7},{9,8},{10,9... | collective-permute-start | bytes 2312 | tf_op jit(solution)/shard_map/ppermute | solution.py:150
  43.5 224.6 %all-gather.7.cloned.1.call-start = ((), (), s32[]{:S(2)}) async-start(), calls=%async_computation.1 | async-start | bytes 3514368 | tf_op jit(solution)/shard_map/all_gather | solution.py:118
  77.7 61.4 %copy-start.18 = (pred[2]{0:T(512)(128)(4,1)}, pred[2]{0:T(512)(128)(4,1)S(1)}, u32[]{:S(2)}) copy-start(pred[2]{0:T(512)(128)(4,1)S(1)} %gather_fusion.6) | copy-start | bytes 10
  78.4 60.8 %copy-start.16 = (pred[2]{0:T(512)(128)(4,1)}, pred[2]{0:T(512)(128)(4,1)S(1)}, u32[]{:S(2)}) copy-start(pred[2]{0:T(512)(128)(4,1)S(1)} %gather_fusion) | copy-start | bytes 10
  127.1 6.2 %copy-start.5 = (f32[3,3,128]{2,1,0:T(4,128)}, f32[3,3,128]{2,1,0:T(4,128)S(1)}, u32[]{:S(2)}) copy-start(f32[3,3,128]{2,1,0:T(4,128)S(1)} %reshape.1234) | copy-start | bytes 13828
  129.9 9.1 %copy-start.6 = (f32[3,3,128]{2,1,0:T(4,128)}, f32[3,3,128]{2,1,0:T(4,128)S(1)}, u32[]{:S(2)}) copy-start(f32[3,3,128]{2,1,0:T(4,128)S(1)} %reshape.1238) | copy-start | bytes 13828
  133.9 2.2 copy-start.4
  136.7 2.4 copy-start.3
  148.2 10.3 %copy-start.12 = (f32[3,1,129]{2,1,0:T(1,128)S(1)}, f32[3,1,129]{2,1,0:T(1,128)}, u32[]{:S(2)}) copy-start(f32[3,1,129]{2,1,0:T(1,128)} %get-tuple-element.244) | copy-start | bytes 4648
  148.2 11.8 %copy-start.11 = (f32[3,1,129]{2,1,0:T(1,128)S(1)}, f32[3,1,129]{2,1,0:T(1,128)}, u32[]{:S(2)}) copy-start(f32[3,1,129]{2,1,0:T(1,128)} %get-tuple-element.246) | copy-start | bytes 4648
  149.9 10.0 %copy-start.13 = (f32[3,2,128]{2,1,0:T(2,128)S(1)}, f32[3,2,128]{2,1,0:T(2,128)}, u32[]{:S(2)}) copy-start(f32[3,2,128]{2,1,0:T(2,128)} %fusion.253) | copy-start | bytes 9220
  149.9 10.0 %copy-start.14 = (f32[3,2,128]{2,1,0:T(2,128)S(1)}, f32[3,2,128]{2,1,0:T(2,128)}, u32[]{:S(2)}) copy-start(f32[3,2,128]{2,1,0:T(2,128)} %subtract_multiply_fusion.2) | copy-start | bytes 9220
  149.9 10.1 %copy-start.15 = (f32[3,1,129]{2,1,0:T(1,128)S(1)}, f32[3,1,129]{2,1,0:T(1,128)}, u32[]{:S(2)}) copy-start(f32[3,1,129]{2,1,0:T(1,128)} %get-tuple-element.245) | copy-start | bytes 4648
  149.9 11.3 %copy-start.28 = (f32[96]{0:T(128)S(1)}, f32[96]{0:T(128)}, u32[]{:S(2)}) copy-start(f32[96]{0:T(128)} %get-tuple-element.45) | copy-start | bytes 1156
  149.9 11.4 %copy-start.27 = (f32[96]{0:T(128)S(1)}, f32[96]{0:T(128)}, u32[]{:S(2)}) copy-start(f32[96]{0:T(128)} %get-tuple-element.44) | copy-start | bytes 1156
  149.9 11.5 %copy-start.26 = (f32[96]{0:T(128)S(1)}, f32[96]{0:T(128)}, u32[]{:S(2)}) copy-start(f32[96]{0:T(128)} %get-tuple-element.41) | copy-start | bytes 1156
  149.9 11.6 %copy-start.25 = (f32[96]{0:T(128)S(1)}, f32[96]{0:T(128)}, u32[]{:S(2)}) copy-start(f32[96]{0:T(128)} %get-tuple-element.40) | copy-start | bytes 1156
  149.9 17.5 %copy-start.24 = (f32[96]{0:T(128)S(1)}, f32[96]{0:T(128)}, u32[]{:S(2)}) copy-start(f32[96]{0:T(128)} %get-tuple-element.43) | copy-start | bytes 1156
  149.9 17.6 %copy-start.23 = (f32[96]{0:T(128)S(1)}, f32[96]{0:T(128)}, u32[]{:S(2)}) copy-start(f32[96]{0:T(128)} %get-tuple-element.42) | copy-start | bytes 1156
  149.9 17.7 %copy-start.22 = (f32[96]{0:T(128)S(1)}, f32[96]{0:T(128)}, u32[]{:S(2)}) copy-start(f32[96]{0:T(128)} %get-tuple-element.38) | copy-start | bytes 1156
  149.9 17.8 %copy-start.21 = (f32[96]{0:T(128)S(1)}, f32[96]{0:T(128)}, u32[]{:S(2)}) copy-start(f32[96]{0:T(128)} %get-tuple-element.39) | copy-start | bytes 1156
  154.8 14.1 %copy-start.10 = (f32[768]{0:T(1024)S(1)}, f32[768]{0:T(1024)}, u32[]{:S(2)}) copy-start(f32[768]{0:T(1024)} %get-tuple-element.58) | copy-start | bytes 9220
  155.0 14.2 %copy-start.9 = (f32[768]{0:T(1024)S(1)}, f32[768]{0:T(1024)}, u32[]{:S(2)}) copy-start(f32[768]{0:T(1024)} %get-tuple-element.59) | copy-start | bytes 9220
  155.0 14.4 %copy-start.20 = (pred[2]{0:T(512)(128)(4,1)S(1)}, pred[2]{0:T(512)(128)(4,1)}, u32[]{:S(2)}) copy-start(pred[2]{0:T(512)(128)(4,1)} %gather_fusion.4) | copy-start | bytes 10
  155.3 14.4 %copy-start.8 = (f32[2,3,64,2]{2,3,1,0:T(2,128)S(1)}, f32[2,3,64,2]{2,3,1,0:T(2,128)}, u32[]{:S(2)}) copy-start(f32[2,3,64,2]{2,3,1,0:T(2,128)} %copy.539) | copy-start | bytes 9220
  163.6 7.9 %copy-start.7 = (f32[1,2,3,256]{3,2,1,0:T(4,128)S(1)}, f32[1,2,3,256]{3,2,1,0:T(4,128)}, u32[]{:S(2)}) copy-start(f32[1,2,3,256]{3,2,1,0:T(4,128)} %get-tuple-element.165) | copy-start | bytes 18436
  164.4 7.2 %copy-start.19 = (pred[2]{0:T(512)(128)(4,1)S(1)}, pred[2]{0:T(512)(128)(4,1)}, u32[]{:S(2)}) copy-start(pred[2]{0:T(512)(128)(4,1)} %copy-done.18) | copy-start | bytes 10
  165.3 6.4 %copy-start.17 = (pred[2]{0:T(512)(128)(4,1)S(1)}, pred[2]{0:T(512)(128)(4,1)}, u32[]{:S(2)}) copy-start(pred[2]{0:T(512)(128)(4,1)} %copy-done.16) | copy-start | bytes 10
  172.9 1.0 copy-start.1
  177.1 1.1 copy-start.29
  192.4 5.8 %collective-permute-start.5 = (f32[2,3,128]{2,0,1:T(2,128)S(1)}, f32[2,3,128]{2,0,1:T(2,128)S(1)}, u32[]{:S(2)}, u32[]{:S(2)}) collective-permute-start(f32[2,3,128]{2,0,1:T(2,128)S(1)} %add_multiply_fusion.2), channel_id=1, source_target_pairs={{0,736},{32,0},{64,32},{96,64},{128,96},{160,128},{192,160},{224,1... | collective-permute-start | bytes 9224 | tf_op jit(solution)/shard_map/ppermute | solution.py:145
  196.1 10.4 %collective-permute-start.4 = (f32[2,3,128]{2,0,1:T(2,128)S(1)}, f32[2,3,128]{2,0,1:T(2,128)S(1)}, u32[]{:S(2)}, u32[]{:S(2)}) collective-permute-start(f32[2,3,128]{2,0,1:T(2,128)S(1)} %add_multiply_fusion.3), channel_id=1, source_target_pairs={{0,32},{32,64},{64,96},{96,128},{128,160},{160,192},{192,224},{224... | collective-permute-start | bytes 9224 | tf_op jit(solution)/shard_map/ppermute | solution.py:145
  221.1 21.0 %collective-permute-start.7 = (f32[3,32,2]{2,1,0:T(8,128)S(1)}, f32[3,32,2]{2,1,0:T(8,128)S(1)}, u32[]{:S(2)}, u32[]{:S(2)}) collective-permute-start(f32[3,32,2]{2,1,0:T(8,128)S(1)} %get-tuple-element.148), channel_id=1, source_target_pairs={{0,1},{1,2},{2,3},{3,4},{4,5},{5,6},{6,7},{7,8},{8,9},{9,10},{10,1... | collective-permute-start | bytes 2312 | tf_op jit(solution)/shard_map/ppermute | solution.py:150
  225.3 16.9 %collective-permute-start.8 = (f32[3,32,2]{2,1,0:T(8,128)S(1)}, f32[3,32,2]{2,1,0:T(8,128)S(1)}, u32[]{:S(2)}, u32[]{:S(2)}) collective-permute-start(f32[3,32,2]{2,1,0:T(8,128)S(1)} %get-tuple-element.147), channel_id=1, source_target_pairs={{0,31},{1,0},{2,1},{3,2},{4,3},{5,4},{6,5},{7,6},{8,7},{9,8},{10,9... | collective-permute-start | bytes 2312 | tf_op jit(solution)/shard_map/ppermute | solution.py:150
  230.8 11.6 %collective-permute-start.6 = (f32[3,2,128]{2,1,0:T(2,128)S(1)}, f32[3,2,128]{2,1,0:T(2,128)S(1)}, u32[]{:S(2)}, u32[]{:S(2)}) collective-permute-start(f32[3,2,128]{2,1,0:T(2,128)S(1)} %get-tuple-element.145), channel_id=1, source_target_pairs={{0,32},{32,64},{64,96},{96,128},{128,160},{160,192},{192,224},{224... | collective-permute-start | bytes 9224 | tf_op jit(solution)/shard_map/ppermute | solution.py:145
  232.8 10.1 %collective-permute-start.9 = (f32[3,2,128]{2,1,0:T(2,128)S(1)}, f32[3,2,128]{2,1,0:T(2,128)S(1)}, u32[]{:S(2)}, u32[]{:S(2)}) collective-permute-start(f32[3,2,128]{2,1,0:T(2,128)S(1)} %get-tuple-element.146), channel_id=1, source_target_pairs={{0,736},{32,0},{64,32},{96,64},{128,96},{160,128},{192,160},{224,1... | collective-permute-start | bytes 9224 | tf_op jit(solution)/shard_map/ppermute | solution.py:145
Sparse Core Ops, SparseCore 0:
  43.6 59.4 all-gather.4
  207.3 60.6 all-gather.6

commit v6 on v4

--- a/solution.py
+++ b/solution.py
@@ -85,11 +85,8 @@
 
 
 def restrict(field):
-    return 0.25 * (
-        field[..., 0::2, 0::2]
-        + field[..., 1::2, 0::2]
-        + (field[..., 0::2, 1::2] + field[..., 1::2, 1::2])
-    )
+    paired = field[..., 0::2, :] + field[..., 1::2, :]
+    return 0.25 * (paired[..., 0::2] + paired[..., 1::2])
 
 
 def coarse_margin(field):

time: 262 us -> 255 us (0.973)
  local copies, waits for them, and re-layouts: 62.1 us -> 55.1 us
    slice x4, local copies, waits for them, and re-layouts: 14.2 us -> 7.24 us  [the longest x2 6.96 us: restrict(): return 0.25 * (paired[..., 0::2] + paired[..., 1::2])]
where the time goes in v6:
time: 255 us; the launch traced here: 253 us
  between operations  80.6 us (32%)
  starting transfers between devices  60.5 us (24%)
  local copies, waits for them, and re-layouts  55.1 us (22%)
  waiting for transfers between devices  38.3 us (15%)
  other arithmetic  18.4 us (7%)
    ppermute x8, starting transfers between devices, shift_x(): lax.ppermute(values, 'gx', [(i, (i + step) % count) for i in range(count)])  46.1 us
    all_gather x2, waiting for transfers between devices, gather_rows(): rows = lax.all_gather(flat, 'gy', axis=0, tiled=True)  20.7 us
    ppermute x8, waiting for transfers between devices, shift_x(): lax.ppermute(values, 'gx', [(i, (i + step) % count) for i in range(count)])  14.3 us
    ppermute x4, starting transfers between devices, shift_y(): lax.ppermute(values, 'gy', [(i, (i + step) % count) for i in range(count)])  14.3 us
    slice x2, local copies, waits for them, and re-layouts, restrict(): return 0.25 * (paired[..., 0::2] + paired[..., 1::2])  6.96 us
    gather x8, local copies, waits for them, and re-layouts, fine_source(): flag = refined[table_column, block]  5.16 us
  transfers between devices with their start and end apart: 14, of which 4 were waited for; matrix products, arithmetic and copies ran while one was open for 14% of the time, Pallas kernels for 0%

profile of v6, /device:TPU:1, one launch (start us, length us, event | category | flops | bytes accessed | tf_op | source)
XLA Modules:
  0.0 252.9 jit_solution(8146782480211612941)
XLA Ops:
  7.2 1.0 copy.649
  8.3 0.7 fusion.240
  9.1 4.8 %collective-permute-start = (f32[6912]{0:T(1024)S(1)}, f32[6912]{0:T(1024)S(1)}, u32[]{:S(2)}, u32[]{:S(2)}) collective-permute-start(f32[6912]{0:T(1024)S(1)} %pad_maximum_fusion.36), channel_id=1, source_target_pairs={{0,32},{32,64},{64,96},{96,128},{128,160},{160,192},{192,224},{224... | collective-permute-start | bytes 82952 | tf_op jit(solution)/shard_map/ppermute | solution.py:142
  13.9 17.5 %collective-permute-start.1 = (f32[6912]{0:T(1024)S(1)}, f32[6912]{0:T(1024)S(1)}, u32[]{:S(2)}, u32[]{:S(2)}) collective-permute-start(f32[6912]{0:T(1024)S(1)} %pad_maximum_fusion.37), channel_id=1, source_target_pairs={{0,736},{32,0},{64,32},{96,64},{128,96},{160,128},{192,160},{224,1... | collective-permute-start | bytes 82952 | tf_op jit(solution)/shard_map/ppermute | solution.py:142
  31.4 1.0 fusion.239
  32.4 3.1 %collective-permute-start.2 = (f32[3,32,2]{2,1,0:T(8,128)S(1)}, f32[3,32,2]{2,1,0:T(8,128)S(1)}, u32[]{:S(2)}, u32[]{:S(2)}) collective-permute-start(f32[3,32,2]{2,1,0:T(8,128)S(1)} %get-tuple-element.147), channel_id=1, source_target_pairs={{0,1},{1,2},{2,3},{3,4},{4,5},{5,6},{6,7},{7,8},{8,9},{9,10},{10,1... | collective-permute-start | bytes 2312 | tf_op jit(solution)/shard_map/ppermute | solution.py:147
  35.5 1.9 collective-permute-start.3
  38.5 3.1 %collective-permute-done.3 = f32[3,32,2]{2,1,0:T(8,128)S(1)} collective-permute-done((f32[3,32,2]{2,1,0:T(8,128)S(1)}, f32[3,32,2]{2,1,0:T(8,128)S(1)}, u32[]{:S(2)}, u32[]{:S(2)}) %collective-permute-start.3) | collective-permute-done | bytes 800 | tf_op jit(solution)/shard_map/ppermute | solution.py:147
  43.5 0.6 pad.16
  44.2 0.6 fusion.263
  47.8 0.6 gather_fusion.3
  48.5 0.7 fusion.268
  51.8 0.7 fusion.269
  55.0 0.6 gather_fusion.5
  55.6 0.6 gather_fusion.7
  56.3 0.6 fusion.261
  58.2 0.6 gather_fusion.1
  66.5 0.7 gather_fusion.6
  67.1 0.6 gather_fusion
  67.8 0.6 gather_fusion.15
  68.4 0.6 gather_fusion.13
  70.8 0.7 fusion.257
  72.8 0.7 fusion.256
  79.2 0.6 gather_fusion.8
  79.8 0.6 gather_fusion.9
  80.5 0.6 gather_fusion.11
  91.2 0.6 gather_fusion.12
  91.8 0.6 gather_fusion.10
  92.5 0.6 gather_fusion.14
  93.1 0.6 gather_fusion.2
  93.8 0.6 fusion.266
  95.7 0.7 fusion.264
  97.8 0.7 fusion.267
  101.2 0.7 fusion.265
  104.4 0.6 gather_fusion.4
  119.5 1.8 reshape.1156
  125.0 1.9 collective-permute-start.4
  126.9 9.6 %collective-permute-start.5 = (f32[32,384]{1,0:T(8,128)S(1)}, f32[32,384]{1,0:T(8,128)S(1)}, u32[]{:S(2)}, u32[]{:S(2)}) collective-permute-start(f32[32,384]{1,0:T(8,128)S(1)} %get-tuple-element.76), channel_id=1, source_target_pairs={{0,736},{32,0},{64,32},{96,64},{128,96},{160,128},{192,160},{224,1... | collective-permute-start | bytes 147464 | tf_op jit(solution)/shard_map/ppermute | solution.py:142
  141.0 0.8 fusion.9
  148.3 0.8 fusion.6
  150.6 3.5 %slice.1217 = f32[2,3,32,128]{3,2,0,1:T(8,128)S(1)} slice(f32[2,3,32,256]{3,2,0,1:T(8,128)S(1)} %add.956), slice={[0:2:1], [0:3:1], [0:32:1], [0:256:2]} | slice | bytes 196608 | tf_op jit(solution)/shard_map/slice | solution.py:89
  154.1 3.5 %slice.1218 = f32[2,3,32,128]{3,2,0,1:T(8,128)S(1)} slice(f32[2,3,32,256]{3,2,0,1:T(8,128)S(1)} %add.956), slice={[0:2:1], [0:3:1], [0:32:1], [1:256:2]} | slice | bytes 196608 | tf_op jit(solution)/shard_map/slice | solution.py:89
  157.6 5.2 %collective-permute-start.7 = (f32[2,3,128]{2,0,1:T(2,128)S(1)}, f32[2,3,128]{2,0,1:T(2,128)S(1)}, u32[]{:S(2)}, u32[]{:S(2)}) collective-permute-start(f32[2,3,128]{2,0,1:T(2,128)S(1)} %add_multiply_fusion.2), channel_id=1, source_target_pairs={{0,736},{32,0},{64,32},{96,64},{128,96},{160,128},{192,160},{224,1... | collective-permute-start | bytes 9224 | tf_op jit(solution)/shard_map/ppermute | solution.py:142
  162.7 1.9 collective-permute-start.6
  164.9 8.2 %collective-permute-done.6 = f32[2,3,128]{2,0,1:T(2,128)S(1)} collective-permute-done((f32[2,3,128]{2,0,1:T(2,128)S(1)}, f32[2,3,128]{2,0,1:T(2,128)S(1)}, u32[]{:S(2)}, u32[]{:S(2)}) %collective-permute-start.6) | collective-permute-done | bytes 3104 | tf_op jit(solution)/shard_map/ppermute | solution.py:142
  173.2 0.7 pad.17
  173.9 0.7 fusion.243
  188.7 0.7 fusion.250
  189.4 7.3 %collective-permute-start.10 = (f32[3,32,2]{2,1,0:T(8,128)S(1)}, f32[3,32,2]{2,1,0:T(8,128)S(1)}, u32[]{:S(2)}, u32[]{:S(2)}) collective-permute-start(f32[3,32,2]{2,1,0:T(8,128)S(1)} %get-tuple-element.143), channel_id=1, source_target_pairs={{0,31},{1,0},{2,1},{3,2},{4,3},{5,4},{6,5},{7,6},{8,7},{9,8},{10,9... | collective-permute-start | bytes 2312 | tf_op jit(solution)/shard_map/ppermute | solution.py:147
  196.7 1.9 collective-permute-start.9
  198.7 1.9 collective-permute-start.11
  200.6 3.4 %collective-permute-start.8 = (f32[3,2,128]{2,1,0:T(2,128)S(1)}, f32[3,2,128]{2,1,0:T(2,128)S(1)}, u32[]{:S(2)}, u32[]{:S(2)}) collective-permute-start(f32[3,2,128]{2,1,0:T(2,128)S(1)} %get-tuple-element.141), channel_id=1, source_target_pairs={{0,32},{32,64},{64,96},{96,128},{128,160},{160,192},{192,224},{224... | collective-permute-start | bytes 9224 | tf_op jit(solution)/shard_map/ppermute | solution.py:142
  204.2 0.6 pad_maximum_fusion.28
  204.9 6.2 %collective-permute-done.8 = f32[3,2,128]{2,1,0:T(2,128)S(1)} collective-permute-done((f32[3,2,128]{2,1,0:T(2,128)S(1)}, f32[3,2,128]{2,1,0:T(2,128)S(1)}, u32[]{:S(2)}, u32[]{:S(2)}) %collective-permute-start.8) | collective-permute-done | bytes 3104 | tf_op jit(solution)/shard_map/ppermute | solution.py:142
  212.0 0.6 pad_maximum_fusion.30
  212.6 0.8 copy.567
  213.4 20.7 %all-gather.7.cloned.1.call-done = f32[851968]{0:T(1024)} async-done(((f32[26624]{0:T(1024)}), f32[851968]{0:T(1024)}) %all-gather.7.cloned.1.call-update) | async-done | bytes 3407888 | tf_op jit(solution)/shard_map/all_gather | solution.py:115
  234.1 2.2 reshape.1157
  236.3 0.7 dynamic-slice_reduce_fusion.21
  237.0 0.8 reshape.1158
  237.8 1.5 reshape.1159
  239.5 2.2 fusion.72
  241.7 2.2 broadcast_select_fusion.5
  243.8 2.2 fusion.79
  (287 shorter events, 27.3 us)
Async XLA Ops:
  7.2 30.5 %copy-start = (f32[3,32,128]{2,1,0:T(8,128)S(1)}, f32[3,32,128]{2,1,0:T(8,128)}, u32[]{:S(2)}) copy-start(f32[3,32,128]{2,1,0:T(8,128)} %param.3) | copy-start | bytes 147460
  7.2 30.7 %copy-start.9 = (s32[24,64]{1,0:T(8,128)S(1)}, s32[24,64]{1,0:T(8,128)}, u32[]{:S(2)}) copy-start(s32[24,64]{1,0:T(8,128)} %param.5) | copy-start | bytes 18436
  7.2 112.3 %all-gather.5.cloned.1.call-start = ((), (), s32[]{:S(2)}) async-start(), calls=%async_computation | async-start | bytes 2297856 | tf_op jit(solution)/shard_map/all_gather | solution.py:115
  9.1 32.8 %collective-permute-start = (f32[6912]{0:T(1024)S(1)}, f32[6912]{0:T(1024)S(1)}, u32[]{:S(2)}, u32[]{:S(2)}) collective-permute-start(f32[6912]{0:T(1024)S(1)} %pad_maximum_fusion.36), channel_id=1, source_target_pairs={{0,32},{32,64},{64,96},{96,128},{128,160},{160,192},{192,224},{224... | collective-permute-start | bytes 82952 | tf_op jit(solution)/shard_map/ppermute | solution.py:142
  13.9 28.0 %collective-permute-start.1 = (f32[6912]{0:T(1024)S(1)}, f32[6912]{0:T(1024)S(1)}, u32[]{:S(2)}, u32[]{:S(2)}) collective-permute-start(f32[6912]{0:T(1024)S(1)} %pad_maximum_fusion.37), channel_id=1, source_target_pairs={{0,736},{32,0},{64,32},{96,64},{128,96},{160,128},{192,160},{224,1... | collective-permute-start | bytes 82952 | tf_op jit(solution)/shard_map/ppermute | solution.py:142
  32.4 9.2 %collective-permute-start.2 = (f32[3,32,2]{2,1,0:T(8,128)S(1)}, f32[3,32,2]{2,1,0:T(8,128)S(1)}, u32[]{:S(2)}, u32[]{:S(2)}) collective-permute-start(f32[3,32,2]{2,1,0:T(8,128)S(1)} %get-tuple-element.147), channel_id=1, source_target_pairs={{0,1},{1,2},{2,3},{3,4},{4,5},{5,6},{6,7},{7,8},{8,9},{9,10},{10,1... | collective-permute-start | bytes 2312 | tf_op jit(solution)/shard_map/ppermute | solution.py:147
  35.5 6.1 %collective-permute-start.3 = (f32[3,32,2]{2,1,0:T(8,128)S(1)}, f32[3,32,2]{2,1,0:T(8,128)S(1)}, u32[]{:S(2)}, u32[]{:S(2)}) collective-permute-start(f32[3,32,2]{2,1,0:T(8,128)S(1)} %get-tuple-element.148), channel_id=1, source_target_pairs={{0,31},{1,0},{2,1},{3,2},{4,3},{5,4},{6,5},{7,6},{8,7},{9,8},{10,9... | collective-permute-start | bytes 2312 | tf_op jit(solution)/shard_map/ppermute | solution.py:147
  41.9 4.9 %copy-start.2 = (f32[3,32,129]{2,1,0:T(8,128)}, f32[3,32,129]{2,1,0:T(8,128)S(1)}, u32[]{:S(2)}) copy-start(f32[3,32,129]{2,1,0:T(8,128)S(1)} %pad_maximum_fusion.27) | copy-start | bytes 148612
  42.3 0.6 copy-start.3
  42.3 0.6 copy-start.4
  42.3 0.7 copy-start.5
  44.2 189.9 %all-gather.7.cloned.1.call-start = ((), (), s32[]{:S(2)}) async-start(), calls=%async_computation.1 | async-start | bytes 3514368 | tf_op jit(solution)/shard_map/all_gather | solution.py:115
  125.0 17.3 %collective-permute-start.4 = (f32[32,384]{1,0:T(8,128)S(1)}, f32[32,384]{1,0:T(8,128)S(1)}, u32[]{:S(2)}, u32[]{:S(2)}) collective-permute-start(f32[32,384]{1,0:T(8,128)S(1)} %get-tuple-element.75), channel_id=1, source_target_pairs={{0,32},{32,64},{64,96},{96,128},{128,160},{160,192},{192,224},{224... | collective-permute-start | bytes 147464 | tf_op jit(solution)/shard_map/ppermute | solution.py:142
  126.9 15.4 %collective-permute-start.5 = (f32[32,384]{1,0:T(8,128)S(1)}, f32[32,384]{1,0:T(8,128)S(1)}, u32[]{:S(2)}, u32[]{:S(2)}) collective-permute-start(f32[32,384]{1,0:T(8,128)S(1)} %get-tuple-element.76), channel_id=1, source_target_pairs={{0,736},{32,0},{64,32},{96,64},{128,96},{160,128},{192,160},{224,1... | collective-permute-start | bytes 147464 | tf_op jit(solution)/shard_map/ppermute | solution.py:142
  145.0 1.0 copy-start.1
  157.6 7.4 %collective-permute-start.7 = (f32[2,3,128]{2,0,1:T(2,128)S(1)}, f32[2,3,128]{2,0,1:T(2,128)S(1)}, u32[]{:S(2)}, u32[]{:S(2)}) collective-permute-start(f32[2,3,128]{2,0,1:T(2,128)S(1)} %add_multiply_fusion.2), channel_id=1, source_target_pairs={{0,736},{32,0},{64,32},{96,64},{128,96},{160,128},{192,160},{224,1... | collective-permute-start | bytes 9224 | tf_op jit(solution)/shard_map/ppermute | solution.py:142
  162.7 10.4 %collective-permute-start.6 = (f32[2,3,128]{2,0,1:T(2,128)S(1)}, f32[2,3,128]{2,0,1:T(2,128)S(1)}, u32[]{:S(2)}, u32[]{:S(2)}) collective-permute-start(f32[2,3,128]{2,0,1:T(2,128)S(1)} %add_multiply_fusion.3), channel_id=1, source_target_pairs={{0,32},{32,64},{64,96},{96,128},{128,160},{160,192},{192,224},{224... | collective-permute-start | bytes 9224 | tf_op jit(solution)/shard_map/ppermute | solution.py:142
  189.4 14.6 %collective-permute-start.10 = (f32[3,32,2]{2,1,0:T(8,128)S(1)}, f32[3,32,2]{2,1,0:T(8,128)S(1)}, u32[]{:S(2)}, u32[]{:S(2)}) collective-permute-start(f32[3,32,2]{2,1,0:T(8,128)S(1)} %get-tuple-element.143), channel_id=1, source_target_pairs={{0,31},{1,0},{2,1},{3,2},{4,3},{5,4},{6,5},{7,6},{8,7},{9,8},{10,9... | collective-permute-start | bytes 2312 | tf_op jit(solution)/shard_map/ppermute | solution.py:147
  196.7 7.3 %collective-permute-start.9 = (f32[3,32,2]{2,1,0:T(8,128)S(1)}, f32[3,32,2]{2,1,0:T(8,128)S(1)}, u32[]{:S(2)}, u32[]{:S(2)}) collective-permute-start(f32[3,32,2]{2,1,0:T(8,128)S(1)} %get-tuple-element.144), channel_id=1, source_target_pairs={{0,1},{1,2},{2,3},{3,4},{4,5},{5,6},{6,7},{7,8},{8,9},{9,10},{10,1... | collective-permute-start | bytes 2312 | tf_op jit(solution)/shard_map/ppermute | solution.py:147
  198.7 6.2 %collective-permute-start.11 = (f32[3,2,128]{2,1,0:T(2,128)S(1)}, f32[3,2,128]{2,1,0:T(2,128)S(1)}, u32[]{:S(2)}, u32[]{:S(2)}) collective-permute-start(f32[3,2,128]{2,1,0:T(2,128)S(1)} %get-tuple-element.142), channel_id=1, source_target_pairs={{0,736},{32,0},{64,32},{96,64},{128,96},{160,128},{192,160},{224,1... | collective-permute-start | bytes 9224 | tf_op jit(solution)/shard_map/ppermute | solution.py:142
  200.6 10.4 %collective-permute-start.8 = (f32[3,2,128]{2,1,0:T(2,128)S(1)}, f32[3,2,128]{2,1,0:T(2,128)S(1)}, u32[]{:S(2)}, u32[]{:S(2)}) collective-permute-start(f32[3,2,128]{2,1,0:T(2,128)S(1)} %get-tuple-element.141), channel_id=1, source_target_pairs={{0,32},{32,64},{64,96},{96,128},{128,160},{160,192},{192,224},{224... | collective-permute-start | bytes 9224 | tf_op jit(solution)/shard_map/ppermute | solution.py:142
  211.4 0.6 copy-start.6
  211.4 1.2 copy-start.7
  211.4 1.2 copy-start.8
Sparse Core Ops, SparseCore 0:
  44.3 58.7 all-gather.4
  174.0 60.0 all-gather.6

commit v7 on v6

--- a/solution.py
+++ b/solution.py
@@ -325,9 +325,7 @@
     reg_low = pair_mean(0.5 * (low_one + low_two))
     reg_high = pair_mean(0.5 * (high_one + high_two))
     restricted = restrict(fine_final)
-    left_regs = shift_x(reg_right, 1)
-    right_regs = shift_x(reg_left, -1)
-    rows, places = gather_rows((restricted, reg_high, reg_low, left_regs, right_regs))
+    rows, places = gather_rows((restricted, reg_high, reg_low, reg_right, reg_left))
 
     def home_pick(place, table_column, block):
         slot_index = slot_of[table_column, block]
@@ -336,8 +334,8 @@
     home_mean = home_pick(places[0], column, device_row)
     got_below = home_pick(places[1], column, below_block)
     got_above = home_pick(places[2], column, above_block)
-    got_left = home_pick(places[3], column_left, device_row)
-    got_right = home_pick(places[4], column_right, device_row)
+    got_left = shift_x(home_pick(places[3], column, device_row), 1)
+    got_right = shift_x(home_pick(places[4], column, device_row), -1)
     face_left = 0.5 * (flux_x1[:, 0] + flux_x2[:, 0])
     face_right = 0.5 * (flux_x1[:, -1] + flux_x2[:, -1])
     face_low = 0.5 * (flux_y1[:, :, 0] + flux_y2[:, :, 0])

time: 255 us -> 251 us (0.984)
  starting transfers between devices: 60.5 us -> 69.2 us
  waiting for transfers between devices: 38.3 us -> 31.8 us
  between operations: 80.6 us -> 75.1 us
    ppermute x8, waiting for transfers between devices: 14.3 us -> 0.02 us  [shift_x(): lax.ppermute(values, 'gx', [(i, (i + step) % count) for i in range(count)])]
    ppermute x8, starting transfers between devices: 46.1 us -> 56.7 us  [shift_x(): lax.ppermute(values, 'gx', [(i, (i + step) % count) for i in range(count)])]
    all_gather x2, waiting for transfers between devices: 20.7 us -> 28.6 us  [gather_rows(): rows = lax.all_gather(flat, 'gy', axis=0, tiled=True)]
    broadcast_in_dim x0 -> x2, other arithmetic: none -> 2.61 us  [the longest x1 1.35 us: shards(): corr_left[:, None, :]]
  transfers between devices with their start and end apart: 14 -> 14, of which waited for: 4 -> 2; matrix products, arithmetic and copies ran while one was open for 14% -> 16% of each run, Pallas kernels for 0% -> 0%
where the time goes in v7:
time: 251 us; the launch traced here: 249 us
  between operations  75.1 us (30%)
  starting transfers between devices  69.2 us (28%)
  local copies, waits for them, and re-layouts  53.8 us (21%)
  waiting for transfers between devices  31.8 us (13%)
  other arithmetic  19.3 us (8%)
    ppermute x8, starting transfers between devices, shift_x(): lax.ppermute(values, 'gx', [(i, (i + step) % count) for i in range(count)])  56.7 us
    all_gather x2, waiting for transfers between devices, gather_rows(): rows = lax.all_gather(flat, 'gy', axis=0, tiled=True)  28.6 us
    ppermute x4, starting transfers between devices, shift_y(): lax.ppermute(values, 'gy', [(i, (i + step) % count) for i in range(count)])  12.4 us
    slice x2, local copies, waits for them, and re-layouts, restrict(): return 0.25 * (paired[..., 0::2] + paired[..., 1::2])  6.96 us
    gather x8, local copies, waits for them, and re-layouts, fine_source(): flag = refined[table_column, block]  5.16 us
    gather x8, local copies, waits for them, and re-layouts, fine_source(): slot_index = slot_of[table_column, block]  5.05 us
  transfers between devices with their start and end apart: 14, of which 2 were waited for; matrix products, arithmetic and copies ran while one was open for 16% of the time, Pallas kernels for 0%

profile of v7, /device:TPU:1, one launch (start us, length us, event | category | flops | bytes accessed | tf_op | source)
XLA Modules:
  0.0 249.3 jit_solution(59173979731188979)
XLA Ops:
  7.2 1.0 copy.677
  8.3 0.7 fusion.244
  9.1 4.8 %collective-permute-start = (f32[6912]{0:T(1024)S(1)}, f32[6912]{0:T(1024)S(1)}, u32[]{:S(2)}, u32[]{:S(2)}) collective-permute-start(f32[6912]{0:T(1024)S(1)} %pad_maximum_fusion.36), channel_id=1, source_target_pairs={{0,32},{32,64},{64,96},{96,128},{128,160},{160,192},{192,224},{224... | collective-permute-start | bytes 82952 | tf_op jit(solution)/shard_map/ppermute | solution.py:142
  13.9 17.5 %collective-permute-start.1 = (f32[6912]{0:T(1024)S(1)}, f32[6912]{0:T(1024)S(1)}, u32[]{:S(2)}, u32[]{:S(2)}) collective-permute-start(f32[6912]{0:T(1024)S(1)} %pad_maximum_fusion.37), channel_id=1, source_target_pairs={{0,736},{32,0},{64,32},{96,64},{128,96},{160,128},{192,160},{224,1... | collective-permute-start | bytes 82952 | tf_op jit(solution)/shard_map/ppermute | solution.py:142
  31.4 1.0 fusion.243
  32.4 3.1 %collective-permute-start.2 = (f32[3,32,2]{2,1,0:T(8,128)S(1)}, f32[3,32,2]{2,1,0:T(8,128)S(1)}, u32[]{:S(2)}, u32[]{:S(2)}) collective-permute-start(f32[3,32,2]{2,1,0:T(8,128)S(1)} %get-tuple-element.149), channel_id=1, source_target_pairs={{0,1},{1,2},{2,3},{3,4},{4,5},{5,6},{6,7},{7,8},{8,9},{9,10},{10,1... | collective-permute-start | bytes 2312 | tf_op jit(solution)/shard_map/ppermute | solution.py:147
  35.5 1.9 collective-permute-start.3
  38.4 3.2 %collective-permute-done.3 = f32[3,32,2]{2,1,0:T(8,128)S(1)} collective-permute-done((f32[3,32,2]{2,1,0:T(8,128)S(1)}, f32[3,32,2]{2,1,0:T(8,128)S(1)}, u32[]{:S(2)}, u32[]{:S(2)}) %collective-permute-start.3) | collective-permute-done | bytes 800 | tf_op jit(solution)/shard_map/ppermute | solution.py:147
  42.9 0.6 pad.16
  43.6 0.6 fusion.267
  47.2 0.6 gather_fusion.3
  50.9 0.6 fusion.273
  54.1 0.6 gather_fusion.5
  54.8 0.6 gather_fusion.7
  55.4 0.6 fusion.265
  57.4 0.6 gather_fusion.1
  58.0 0.7 fusion.263
  60.0 0.6 fusion.266
  66.4 0.6 gather_fusion.6
  67.1 0.6 gather_fusion
  67.7 0.6 gather_fusion.15
  68.3 0.6 gather_fusion.13
  69.0 0.6 fusion.259
  72.7 0.6 fusion.260
  75.8 0.7 fusion.262
  78.9 0.6 gather_fusion.8
  79.6 0.6 gather_fusion.9
  80.2 0.6 gather_fusion.11
  80.9 0.6 fusion.255
  84.7 0.7 fusion.256
  91.2 0.6 gather_fusion.12
  91.9 0.6 gather_fusion.10
  92.5 0.6 gather_fusion.14
  93.1 0.6 gather_fusion.2
  103.2 0.6 gather_fusion.4
  118.3 1.8 reshape.1160
  123.7 1.9 collective-permute-start.4
  125.6 9.6 %collective-permute-start.5 = (f32[32,384]{1,0:T(8,128)S(1)}, f32[32,384]{1,0:T(8,128)S(1)}, u32[]{:S(2)}, u32[]{:S(2)}) collective-permute-start(f32[32,384]{1,0:T(8,128)S(1)} %get-tuple-element.76), channel_id=1, source_target_pairs={{0,736},{32,0},{64,32},{96,64},{128,96},{160,128},{192,160},{224,1... | collective-permute-start | bytes 147464 | tf_op jit(solution)/shard_map/ppermute | solution.py:142
  139.7 0.8 fusion.9
  147.1 0.8 fusion.6
  149.3 3.5 %slice.1217 = f32[2,3,32,128]{3,2,0,1:T(8,128)S(1)} slice(f32[2,3,32,256]{3,2,0,1:T(8,128)S(1)} %add.946), slice={[0:2:1], [0:3:1], [0:32:1], [0:256:2]} | slice | bytes 196608 | tf_op jit(solution)/shard_map/slice | solution.py:89
  152.8 3.5 %slice.1218 = f32[2,3,32,128]{3,2,0,1:T(8,128)S(1)} slice(f32[2,3,32,256]{3,2,0,1:T(8,128)S(1)} %add.946), slice={[0:2:1], [0:3:1], [0:32:1], [1:256:2]} | slice | bytes 196608 | tf_op jit(solution)/shard_map/slice | solution.py:89
  156.7 0.7 pad.17
  157.4 0.7 fusion.247
  166.4 0.7 pad.22.clone
  167.1 0.7 fusion.254
  167.8 2.0 collective-permute-start.7
  169.9 5.3 %collective-permute-start.8 = (f32[3,32,2]{2,1,0:T(8,128)S(1)}, f32[3,32,2]{2,1,0:T(8,128)S(1)}, u32[]{:S(2)}, u32[]{:S(2)}) collective-permute-start(f32[3,32,2]{2,1,0:T(8,128)S(1)} %get-tuple-element.145), channel_id=1, source_target_pairs={{0,31},{1,0},{2,1},{3,2},{4,3},{5,4},{6,5},{7,6},{8,7},{9,8},{10,9... | collective-permute-start | bytes 2312 | tf_op jit(solution)/shard_map/ppermute | solution.py:147
  175.2 1.9 collective-permute-start.6
  177.1 9.4 %collective-permute-start.9 = (f32[3,2,128]{2,1,0:T(2,128)S(1)}, f32[3,2,128]{2,1,0:T(2,128)S(1)}, u32[]{:S(2)}, u32[]{:S(2)}) collective-permute-start(f32[3,2,128]{2,1,0:T(2,128)S(1)} %get-tuple-element.144), channel_id=1, source_target_pairs={{0,736},{32,0},{64,32},{96,64},{128,96},{160,128},{192,160},{224,1... | collective-permute-start | bytes 9224 | tf_op jit(solution)/shard_map/ppermute | solution.py:142
  186.7 0.6 pad_maximum_fusion.28
  188.3 0.6 pad_maximum_fusion.30
  188.9 0.8 copy.591
  189.7 28.6 %all-gather.7.cloned.1.call-done = f32[851968]{0:T(1024)} async-done(((f32[26624]{0:T(1024)}), f32[851968]{0:T(1024)}) %all-gather.7.cloned.1.call-update) | async-done | bytes 3407888 | tf_op jit(solution)/shard_map/all_gather | solution.py:115
  218.3 2.2 reshape.1161
  220.6 0.7 dynamic-slice_reduce_fusion.23
  221.3 0.8 reshape.1162
  222.1 1.5 reshape.1163
  223.7 3.1 %collective-permute-start.10 = (f32[3,128]{1,0:T(4,128)S(1)}, f32[3,128]{1,0:T(4,128)S(1)}, u32[]{:S(2)}, u32[]{:S(2)}) collective-permute-start(f32[3,128]{1,0:T(4,128)S(1)} %bitcast.390), channel_id=1, source_target_pairs={{0,32},{32,64},{64,96},{96,128},{128,160},{160,192},{192,224},{224... | collective-permute-start | bytes 4616 | tf_op jit(solution)/shard_map/ppermute | solution.py:142
  226.7 8.6 %collective-permute-start.11 = (f32[3,128]{1,0:T(4,128)S(1)}, f32[3,128]{1,0:T(4,128)S(1)}, u32[]{:S(2)}, u32[]{:S(2)}) collective-permute-start(f32[3,128]{1,0:T(4,128)S(1)} %bitcast.389), channel_id=1, source_target_pairs={{0,736},{32,0},{64,32},{96,64},{128,96},{160,128},{192,160},{224,1... | collective-permute-start | bytes 4616 | tf_op jit(solution)/shard_map/ppermute | solution.py:142
  235.3 2.1 fusion.72
  237.6 1.3 fusion.196
  239.0 1.3 fusion.193
  240.2 2.2 fusion.79
  (280 shorter events, 26.2 us)
Async XLA Ops:
  7.2 30.4 %copy-start = (f32[3,32,128]{2,1,0:T(8,128)S(1)}, f32[3,32,128]{2,1,0:T(8,128)}, u32[]{:S(2)}) copy-start(f32[3,32,128]{2,1,0:T(8,128)} %param.3) | copy-start | bytes 147460
  7.2 30.7 %copy-start.3 = (s32[24,64]{1,0:T(8,128)S(1)}, s32[24,64]{1,0:T(8,128)}, u32[]{:S(2)}) copy-start(s32[24,64]{1,0:T(8,128)} %param.5) | copy-start | bytes 18436
  7.2 111.1 %all-gather.5.cloned.1.call-start = ((), (), s32[]{:S(2)}) async-start(), calls=%async_computation | async-start | bytes 2297856 | tf_op jit(solution)/shard_map/all_gather | solution.py:115
  9.1 32.8 %collective-permute-start = (f32[6912]{0:T(1024)S(1)}, f32[6912]{0:T(1024)S(1)}, u32[]{:S(2)}, u32[]{:S(2)}) collective-permute-start(f32[6912]{0:T(1024)S(1)} %pad_maximum_fusion.36), channel_id=1, source_target_pairs={{0,32},{32,64},{64,96},{96,128},{128,160},{160,192},{192,224},{224... | collective-permute-start | bytes 82952 | tf_op jit(solution)/shard_map/ppermute | solution.py:142
  13.9 28.0 %collective-permute-start.1 = (f32[6912]{0:T(1024)S(1)}, f32[6912]{0:T(1024)S(1)}, u32[]{:S(2)}, u32[]{:S(2)}) collective-permute-start(f32[6912]{0:T(1024)S(1)} %pad_maximum_fusion.37), channel_id=1, source_target_pairs={{0,736},{32,0},{64,32},{96,64},{128,96},{160,128},{192,160},{224,1... | collective-permute-start | bytes 82952 | tf_op jit(solution)/shard_map/ppermute | solution.py:142
  32.4 9.2 %collective-permute-start.2 = (f32[3,32,2]{2,1,0:T(8,128)S(1)}, f32[3,32,2]{2,1,0:T(8,128)S(1)}, u32[]{:S(2)}, u32[]{:S(2)}) collective-permute-start(f32[3,32,2]{2,1,0:T(8,128)S(1)} %get-tuple-element.149), channel_id=1, source_target_pairs={{0,1},{1,2},{2,3},{3,4},{4,5},{5,6},{6,7},{7,8},{8,9},{9,10},{10,1... | collective-permute-start | bytes 2312 | tf_op jit(solution)/shard_map/ppermute | solution.py:147
  35.5 6.1 %collective-permute-start.3 = (f32[3,32,2]{2,1,0:T(8,128)S(1)}, f32[3,32,2]{2,1,0:T(8,128)S(1)}, u32[]{:S(2)}, u32[]{:S(2)}) collective-permute-start(f32[3,32,2]{2,1,0:T(8,128)S(1)} %get-tuple-element.150), channel_id=1, source_target_pairs={{0,31},{1,0},{2,1},{3,2},{4,3},{5,4},{6,5},{7,6},{8,7},{9,8},{10,9... | collective-permute-start | bytes 2312 | tf_op jit(solution)/shard_map/ppermute | solution.py:147
  41.9 4.2 %copy-start.2 = (f32[3,32,129]{2,1,0:T(8,128)}, f32[3,32,129]{2,1,0:T(8,128)S(1)}, u32[]{:S(2)}) copy-start(f32[3,32,129]{2,1,0:T(8,128)S(1)} %pad_maximum_fusion.27) | copy-start | bytes 148612
  43.5 174.8 %all-gather.7.cloned.1.call-start = ((), (), s32[]{:S(2)}) async-start(), calls=%async_computation.1 | async-start | bytes 3514368 | tf_op jit(solution)/shard_map/all_gather | solution.py:115
  123.7 17.3 %collective-permute-start.4 = (f32[32,384]{1,0:T(8,128)S(1)}, f32[32,384]{1,0:T(8,128)S(1)}, u32[]{:S(2)}, u32[]{:S(2)}) collective-permute-start(f32[32,384]{1,0:T(8,128)S(1)} %get-tuple-element.75), channel_id=1, source_target_pairs={{0,32},{32,64},{64,96},{96,128},{128,160},{160,192},{192,224},{224... | collective-permute-start | bytes 147464 | tf_op jit(solution)/shard_map/ppermute | solution.py:142
  125.6 15.4 %collective-permute-start.5 = (f32[32,384]{1,0:T(8,128)S(1)}, f32[32,384]{1,0:T(8,128)S(1)}, u32[]{:S(2)}, u32[]{:S(2)}) collective-permute-start(f32[32,384]{1,0:T(8,128)S(1)} %get-tuple-element.76), channel_id=1, source_target_pairs={{0,736},{32,0},{64,32},{96,64},{128,96},{160,128},{192,160},{224,1... | collective-permute-start | bytes 147464 | tf_op jit(solution)/shard_map/ppermute | solution.py:142
  143.8 1.0 copy-start.1
  167.8 18.7 %collective-permute-start.7 = (f32[3,32,2]{2,1,0:T(8,128)S(1)}, f32[3,32,2]{2,1,0:T(8,128)S(1)}, u32[]{:S(2)}, u32[]{:S(2)}) collective-permute-start(f32[3,32,2]{2,1,0:T(8,128)S(1)} %get-tuple-element.146), channel_id=1, source_target_pairs={{0,1},{1,2},{2,3},{3,4},{4,5},{5,6},{6,7},{7,8},{8,9},{9,10},{10,1... | collective-permute-start | bytes 2312 | tf_op jit(solution)/shard_map/ppermute | solution.py:147
  169.9 16.6 %collective-permute-start.8 = (f32[3,32,2]{2,1,0:T(8,128)S(1)}, f32[3,32,2]{2,1,0:T(8,128)S(1)}, u32[]{:S(2)}, u32[]{:S(2)}) collective-permute-start(f32[3,32,2]{2,1,0:T(8,128)S(1)} %get-tuple-element.145), channel_id=1, source_target_pairs={{0,31},{1,0},{2,1},{3,2},{4,3},{5,4},{6,5},{7,6},{8,7},{9,8},{10,9... | collective-permute-start | bytes 2312 | tf_op jit(solution)/shard_map/ppermute | solution.py:147
  175.2 12.2 %collective-permute-start.6 = (f32[3,2,128]{2,1,0:T(2,128)S(1)}, f32[3,2,128]{2,1,0:T(2,128)S(1)}, u32[]{:S(2)}, u32[]{:S(2)}) collective-permute-start(f32[3,2,128]{2,1,0:T(2,128)S(1)} %get-tuple-element.143), channel_id=1, source_target_pairs={{0,32},{32,64},{64,96},{96,128},{128,160},{160,192},{192,224},{224... | collective-permute-start | bytes 9224 | tf_op jit(solution)/shard_map/ppermute | solution.py:142
  177.1 10.3 %collective-permute-start.9 = (f32[3,2,128]{2,1,0:T(2,128)S(1)}, f32[3,2,128]{2,1,0:T(2,128)S(1)}, u32[]{:S(2)}, u32[]{:S(2)}) collective-permute-start(f32[3,2,128]{2,1,0:T(2,128)S(1)} %get-tuple-element.144), channel_id=1, source_target_pairs={{0,736},{32,0},{64,32},{96,64},{128,96},{160,128},{192,160},{224,1... | collective-permute-start | bytes 9224 | tf_op jit(solution)/shard_map/ppermute | solution.py:142
  223.7 13.9 %collective-permute-start.10 = (f32[3,128]{1,0:T(4,128)S(1)}, f32[3,128]{1,0:T(4,128)S(1)}, u32[]{:S(2)}, u32[]{:S(2)}) collective-permute-start(f32[3,128]{1,0:T(4,128)S(1)} %bitcast.390), channel_id=1, source_target_pairs={{0,32},{32,64},{64,96},{96,128},{128,160},{160,192},{192,224},{224... | collective-permute-start | bytes 4616 | tf_op jit(solution)/shard_map/ppermute | solution.py:142
  226.7 12.2 %collective-permute-start.11 = (f32[3,128]{1,0:T(4,128)S(1)}, f32[3,128]{1,0:T(4,128)S(1)}, u32[]{:S(2)}, u32[]{:S(2)}) collective-permute-start(f32[3,128]{1,0:T(4,128)S(1)} %bitcast.389), channel_id=1, source_target_pairs={{0,736},{32,0},{64,32},{96,64},{128,96},{160,128},{192,160},{224,1... | collective-permute-start | bytes 4616 | tf_op jit(solution)/shard_map/ppermute | solution.py:142
Sparse Core Ops, SparseCore 0:
  43.7 58.8 all-gather.4
  157.5 60.8 all-gather.6

commit v8 on v7

--- a/solution.py
+++ b/solution.py
@@ -348,22 +348,10 @@
     )
     corr_low = jnp.where(refined[column, below_block], LAM_COARSE * (got_below - face_low), 0.0)
     corr_high = jnp.where(refined[column, above_block], LAM_COARSE * (face_high - got_above), 0.0)
-    corr_x = jnp.concatenate(
-        [
-            corr_left[:, None, :],
-            jnp.zeros((3, span_x - 2, span_y), jnp.float32),
-            corr_right[:, None, :],
-        ],
-        axis=1,
-    )
-    corr_y = jnp.concatenate(
-        [
-            corr_low[:, :, None],
-            jnp.zeros((3, span_x, span_y - 2), jnp.float32),
-            corr_high[:, :, None],
-        ],
-        axis=2,
-    )
+    row_ids = jnp.arange(span_x, dtype=jnp.int32)[None, :, None]
+    col_ids = jnp.arange(span_y, dtype=jnp.int32)[None, None, :]
+    corr_x = jnp.where(row_ids == 0, corr_left[:, None, :], jnp.where(row_ids == span_x - 1, corr_right[:, None, :], 0.0))
+    corr_y = jnp.where(col_ids == 0, corr_low[:, :, None], jnp.where(col_ids == span_y - 1, corr_high[:, :, None], 0.0))
     coarse_next = coarse_heun + corr_x + corr_y
     coarse_next = jnp.where(refined[column, device_row], home_mean, coarse_next)
     fine_next = jnp.where(is_live[:, None, None, None], fine_final, 0.0)[None]

time: 251 us -> 259 us (1.032)
  waiting for transfers between devices: 31.8 us -> 44.4 us
  other arithmetic: 19.3 us -> 15.5 us
    ppermute x8, waiting for transfers between devices: 0.02 us -> 14.5 us  [shift_x(): lax.ppermute(values, 'gx', [(i, (i + step) % count) for i in range(count)])]
    ppermute x8, starting transfers between devices: 56.7 us -> 50.7 us  [shift_x(): lax.ppermute(values, 'gx', [(i, (i + step) % count) for i in range(count)])]
    ppermute x4, starting transfers between devices: 12.4 us -> 17.2 us  [shift_y(): lax.ppermute(values, 'gy', [(i, (i + step) % count) for i in range(count)])]
    broadcast_in_dim x2 -> x0, other arithmetic: 2.61 us -> none  [the longest x1 1.35 us: shards(): corr_left[:, None, :]]
  transfers between devices with their start and end apart: 14 -> 14, of which waited for: 2 -> 5; matrix products, arithmetic and copies ran while one was open for 16% -> 12% of each run, Pallas kernels for 0% -> 0%
where the time goes in v8:
time: 259 us; the launch traced here: 257 us
  between operations  74.6 us (29%)
  starting transfers between devices  68 us (26%)
  local copies, waits for them, and re-layouts  54.9 us (21%)
  waiting for transfers between devices  44.4 us (17%)
  other arithmetic  15.5 us (6%)
    ppermute x8, starting transfers between devices, shift_x(): lax.ppermute(values, 'gx', [(i, (i + step) % count) for i in range(count)])  50.7 us
    all_gather x2, waiting for transfers between devices, gather_rows(): rows = lax.all_gather(flat, 'gy', axis=0, tiled=True)  28.7 us
    ppermute x4, starting transfers between devices, shift_y(): lax.ppermute(values, 'gy', [(i, (i + step) % count) for i in range(count)])  17.2 us
    ppermute x8, waiting for transfers between devices, shift_x(): lax.ppermute(values, 'gx', [(i, (i + step) % count) for i in range(count)])  14.5 us
    slice x2, local copies, waits for them, and re-layouts, restrict(): return 0.25 * (paired[..., 0::2] + paired[..., 1::2])  6.96 us
    all_gather x2, local copies, waits for them, and re-layouts, gather_rows(): rows = lax.all_gather(flat, 'gy', axis=0, tiled=True)  5.25 us
  transfers between devices with their start and end apart: 14, of which 5 were waited for; matrix products, arithmetic and copies ran while one was open for 12% of the time, Pallas kernels for 0%

profile of v8, /device:TPU:1, one launch (start us, length us, event | category | flops | bytes accessed | tf_op | source)
XLA Modules:
  0.0 257.4 jit_solution(7246222904096466751)
XLA Ops:
  7.2 0.7 fusion.244
  8.0 1.0 copy.663
  9.1 4.8 %collective-permute-start = (f32[6912]{0:T(1024)S(1)}, f32[6912]{0:T(1024)S(1)}, u32[]{:S(2)}, u32[]{:S(2)}) collective-permute-start(f32[6912]{0:T(1024)S(1)} %pad_maximum_fusion.36), channel_id=1, source_target_pairs={{0,32},{32,64},{64,96},{96,128},{128,160},{160,192},{192,224},{224... | collective-permute-start | bytes 82952 | tf_op jit(solution)/shard_map/ppermute | solution.py:142
  13.9 17.5 %collective-permute-start.1 = (f32[6912]{0:T(1024)S(1)}, f32[6912]{0:T(1024)S(1)}, u32[]{:S(2)}, u32[]{:S(2)}) collective-permute-start(f32[6912]{0:T(1024)S(1)} %pad_maximum_fusion.37), channel_id=1, source_target_pairs={{0,736},{32,0},{64,32},{96,64},{128,96},{160,128},{192,160},{224,1... | collective-permute-start | bytes 82952 | tf_op jit(solution)/shard_map/ppermute | solution.py:142
  31.4 1.0 fusion.243
  32.4 2.9 %collective-permute-start.3 = (f32[3,32,2]{2,1,0:T(8,128)S(1)}, f32[3,32,2]{2,1,0:T(8,128)S(1)}, u32[]{:S(2)}, u32[]{:S(2)}) collective-permute-start(f32[3,32,2]{2,1,0:T(8,128)S(1)} %get-tuple-element.150), channel_id=1, source_target_pairs={{0,31},{1,0},{2,1},{3,2},{4,3},{5,4},{6,5},{7,6},{8,7},{9,8},{10,9... | collective-permute-start | bytes 2312 | tf_op jit(solution)/shard_map/ppermute | solution.py:147
  35.3 2.7 %collective-permute-start.2 = (f32[3,32,2]{2,1,0:T(8,128)S(1)}, f32[3,32,2]{2,1,0:T(8,128)S(1)}, u32[]{:S(2)}, u32[]{:S(2)}) collective-permute-start(f32[3,32,2]{2,1,0:T(8,128)S(1)} %get-tuple-element.149), channel_id=1, source_target_pairs={{0,1},{1,2},{2,3},{3,4},{4,5},{5,6},{6,7},{7,8},{8,9},{9,10},{10,1... | collective-permute-start | bytes 2312 | tf_op jit(solution)/shard_map/ppermute | solution.py:147
  39.0 1.2 collective-permute-done.2
  41.4 0.6 pad.16
  42.6 0.6 gather_fusion.11
  43.2 0.6 gather_fusion.9
  45.7 0.6 gather_fusion.15
  46.3 0.6 gather_fusion.13
  47.0 0.6 fusion.262
  50.3 0.6 fusion.261
  58.4 0.6 fusion.257
  62.1 0.6 fusion.255
  65.2 0.6 gather_fusion.3
  65.9 0.6 fusion.273
  75.6 0.7 gather_fusion.14
  76.3 0.6 gather_fusion.10
  76.9 0.6 gather_fusion.4
  77.6 0.6 gather_fusion.5
  78.2 0.6 gather_fusion.7
  78.9 0.6 fusion.271
  83.8 0.6 fusion.269
  87.0 0.7 fusion.268
  89.0 0.6 gather_fusion.2
  89.6 0.6 gather_fusion.12
  90.3 0.6 gather_fusion.8
  90.9 0.6 gather_fusion
  91.6 0.6 gather_fusion.1
  92.2 0.7 fusion.263
  101.4 0.6 gather_fusion.6
  116.3 1.8 reshape.1182
  126.1 3.4 %collective-permute-start.5 = (f32[32,384]{1,0:T(8,128)S(1)}, f32[32,384]{1,0:T(8,128)S(1)}, u32[]{:S(2)}, u32[]{:S(2)}) collective-permute-start(f32[32,384]{1,0:T(8,128)S(1)} %get-tuple-element.78), channel_id=1, source_target_pairs={{0,736},{32,0},{64,32},{96,64},{128,96},{160,128},{192,160},{224,1... | collective-permute-start | bytes 147464 | tf_op jit(solution)/shard_map/ppermute | solution.py:142
  129.5 2.1 collective-permute-start.4
  131.6 0.8 fusion.9
  133.1 7.6 %collective-permute-done.4 = f32[32,384]{1,0:T(8,128)S(1)} collective-permute-done((f32[32,384]{1,0:T(8,128)S(1)}, f32[32,384]{1,0:T(8,128)S(1)}, u32[]{:S(2)}, u32[]{:S(2)}) %collective-permute-start.4) | collective-permute-done | bytes 49184 | tf_op jit(solution)/shard_map/ppermute | solution.py:142
  144.5 0.8 fusion.6
  147.0 1.3 slice.1216
  148.3 1.0 add.946
  149.3 3.5 %slice.1217 = f32[2,3,32,128]{3,2,0,1:T(8,128)S(1)} slice(f32[2,3,32,256]{3,2,0,1:T(8,128)S(1)} %add.946), slice={[0:2:1], [0:3:1], [0:32:1], [0:256:2]} | slice | bytes 196608 | tf_op jit(solution)/shard_map/slice | solution.py:89
  152.8 3.5 %slice.1218 = f32[2,3,32,128]{3,2,0,1:T(8,128)S(1)} slice(f32[2,3,32,256]{3,2,0,1:T(8,128)S(1)} %add.946), slice={[0:2:1], [0:3:1], [0:32:1], [1:256:2]} | slice | bytes 196608 | tf_op jit(solution)/shard_map/slice | solution.py:89
  158.3 0.7 pad.17
  159.0 0.6 fusion.247
  167.4 0.7 fusion.254
  168.2 9.7 %collective-permute-start.8 = (f32[3,32,2]{2,1,0:T(8,128)S(1)}, f32[3,32,2]{2,1,0:T(8,128)S(1)}, u32[]{:S(2)}, u32[]{:S(2)}) collective-permute-start(f32[3,32,2]{2,1,0:T(8,128)S(1)} %get-tuple-element.145), channel_id=1, source_target_pairs={{0,31},{1,0},{2,1},{3,2},{4,3},{5,4},{6,5},{7,6},{8,7},{9,8},{10,9... | collective-permute-start | bytes 2312 | tf_op jit(solution)/shard_map/ppermute | solution.py:147
  177.9 1.9 collective-permute-start.7
  179.8 1.9 collective-permute-start.6
  181.8 9.4 %collective-permute-start.9 = (f32[3,2,128]{2,1,0:T(2,128)S(1)}, f32[3,2,128]{2,1,0:T(2,128)S(1)}, u32[]{:S(2)}, u32[]{:S(2)}) collective-permute-start(f32[3,2,128]{2,1,0:T(2,128)S(1)} %get-tuple-element.144), channel_id=1, source_target_pairs={{0,736},{32,0},{64,32},{96,64},{128,96},{160,128},{192,160},{224,1... | collective-permute-start | bytes 9224 | tf_op jit(solution)/shard_map/ppermute | solution.py:142
  192.2 0.8 copy.577
  193.0 28.7 %all-gather.7.cloned.1.call-done = f32[851968]{0:T(1024)} async-done(((f32[26624]{0:T(1024)}), f32[851968]{0:T(1024)}) %all-gather.7.cloned.1.call-update) | async-done | bytes 3407888 | tf_op jit(solution)/shard_map/all_gather | solution.py:115
  221.7 3.5 %reshape.1183 = f32[32,26624]{1,0:T(8,128)} reshape(f32[851968]{0:T(1024)} %all-gather.7.cloned.1.call-done) | data formatting | bytes 6815744 | tf_op jit(solution)/shard_map/all_gather | solution.py:115
  225.2 0.9 dynamic-slice_reduce_fusion.23
  226.4 1.2 dynamic_slice.209
  227.6 0.8 dynamic-slice_reduce_fusion.17
  228.4 9.7 %collective-permute-start.11 = (f32[3,128]{1,0:T(4,128)S(1)}, f32[3,128]{1,0:T(4,128)S(1)}, u32[]{:S(2)}, u32[]{:S(2)}) collective-permute-start(f32[3,128]{1,0:T(4,128)S(1)} %bitcast.382), channel_id=1, source_target_pairs={{0,736},{32,0},{64,32},{96,64},{128,96},{160,128},{192,160},{224,1... | collective-permute-start | bytes 4616 | tf_op jit(solution)/shard_map/ppermute | solution.py:142
  238.1 1.9 collective-permute-start.10
  240.0 1.3 fusion.74
  241.4 0.6 fusion.194
  242.0 6.4 %collective-permute-done.10 = f32[3,128]{1,0:T(4,128)S(1)} collective-permute-done((f32[3,128]{1,0:T(4,128)S(1)}, f32[3,128]{1,0:T(4,128)S(1)}, u32[]{:S(2)}, u32[]{:S(2)}) %collective-permute-start.10) | collective-permute-done | bytes 1568 | tf_op jit(solution)/shard_map/ppermute | solution.py:142
  248.4 0.6 fusion.196
  249.1 1.4 fusion.81
  (274 shorter events, 26.0 us)
Async XLA Ops:
  7.2 31.0 %copy-start = (f32[3,32,128]{2,1,0:T(8,128)S(1)}, f32[3,32,128]{2,1,0:T(8,128)}, u32[]{:S(2)}) copy-start(f32[3,32,128]{2,1,0:T(8,128)} %param.3) | copy-start | bytes 147460
  7.2 31.2 %copy-start.2 = (s32[24,64]{1,0:T(8,128)S(1)}, s32[24,64]{1,0:T(8,128)}, u32[]{:S(2)}) copy-start(s32[24,64]{1,0:T(8,128)} %param.5) | copy-start | bytes 18436
  7.2 109.1 %all-gather.5.cloned.1.call-start = ((), (), s32[]{:S(2)}) async-start(), calls=%async_computation | async-start | bytes 2297856 | tf_op jit(solution)/shard_map/all_gather | solution.py:115
  9.1 31.3 %collective-permute-start = (f32[6912]{0:T(1024)S(1)}, f32[6912]{0:T(1024)S(1)}, u32[]{:S(2)}, u32[]{:S(2)}) collective-permute-start(f32[6912]{0:T(1024)S(1)} %pad_maximum_fusion.36), channel_id=1, source_target_pairs={{0,32},{32,64},{64,96},{96,128},{128,160},{160,192},{192,224},{224... | collective-permute-start | bytes 82952 | tf_op jit(solution)/shard_map/ppermute | solution.py:142
  13.9 26.5 %collective-permute-start.1 = (f32[6912]{0:T(1024)S(1)}, f32[6912]{0:T(1024)S(1)}, u32[]{:S(2)}, u32[]{:S(2)}) collective-permute-start(f32[6912]{0:T(1024)S(1)} %pad_maximum_fusion.37), channel_id=1, source_target_pairs={{0,736},{32,0},{64,32},{96,64},{128,96},{160,128},{192,160},{224,1... | collective-permute-start | bytes 82952 | tf_op jit(solution)/shard_map/ppermute | solution.py:142
  32.4 6.6 %collective-permute-start.3 = (f32[3,32,2]{2,1,0:T(8,128)S(1)}, f32[3,32,2]{2,1,0:T(8,128)S(1)}, u32[]{:S(2)}, u32[]{:S(2)}) collective-permute-start(f32[3,32,2]{2,1,0:T(8,128)S(1)} %get-tuple-element.150), channel_id=1, source_target_pairs={{0,31},{1,0},{2,1},{3,2},{4,3},{5,4},{6,5},{7,6},{8,7},{9,8},{10,9... | collective-permute-start | bytes 2312 | tf_op jit(solution)/shard_map/ppermute | solution.py:147
  35.3 4.9 %collective-permute-start.2 = (f32[3,32,2]{2,1,0:T(8,128)S(1)}, f32[3,32,2]{2,1,0:T(8,128)S(1)}, u32[]{:S(2)}, u32[]{:S(2)}) collective-permute-start(f32[3,32,2]{2,1,0:T(8,128)S(1)} %get-tuple-element.149), channel_id=1, source_target_pairs={{0,1},{1,2},{2,3},{3,4},{4,5},{5,6},{6,7},{7,8},{8,9},{9,10},{10,1... | collective-permute-start | bytes 2312 | tf_op jit(solution)/shard_map/ppermute | solution.py:147
  42.1 179.6 %all-gather.7.cloned.1.call-start = ((), (), s32[]{:S(2)}) async-start(), calls=%async_computation.1 | async-start | bytes 3514368 | tf_op jit(solution)/shard_map/all_gather | solution.py:115
  126.1 7.0 %collective-permute-start.5 = (f32[32,384]{1,0:T(8,128)S(1)}, f32[32,384]{1,0:T(8,128)S(1)}, u32[]{:S(2)}, u32[]{:S(2)}) collective-permute-start(f32[32,384]{1,0:T(8,128)S(1)} %get-tuple-element.78), channel_id=1, source_target_pairs={{0,736},{32,0},{64,32},{96,64},{128,96},{160,128},{192,160},{224,1... | collective-permute-start | bytes 147464 | tf_op jit(solution)/shard_map/ppermute | solution.py:142
  129.5 11.2 %collective-permute-start.4 = (f32[32,384]{1,0:T(8,128)S(1)}, f32[32,384]{1,0:T(8,128)S(1)}, u32[]{:S(2)}, u32[]{:S(2)}) collective-permute-start(f32[32,384]{1,0:T(8,128)S(1)} %get-tuple-element.77), channel_id=1, source_target_pairs={{0,32},{32,64},{64,96},{96,128},{128,160},{160,192},{192,224},{224... | collective-permute-start | bytes 147464 | tf_op jit(solution)/shard_map/ppermute | solution.py:142
  143.3 1.0 copy-start.1
  168.2 23.0 %collective-permute-start.8 = (f32[3,32,2]{2,1,0:T(8,128)S(1)}, f32[3,32,2]{2,1,0:T(8,128)S(1)}, u32[]{:S(2)}, u32[]{:S(2)}) collective-permute-start(f32[3,32,2]{2,1,0:T(8,128)S(1)} %get-tuple-element.145), channel_id=1, source_target_pairs={{0,31},{1,0},{2,1},{3,2},{4,3},{5,4},{6,5},{7,6},{8,7},{9,8},{10,9... | collective-permute-start | bytes 2312 | tf_op jit(solution)/shard_map/ppermute | solution.py:147
  177.9 13.3 %collective-permute-start.7 = (f32[3,32,2]{2,1,0:T(8,128)S(1)}, f32[3,32,2]{2,1,0:T(8,128)S(1)}, u32[]{:S(2)}, u32[]{:S(2)}) collective-permute-start(f32[3,32,2]{2,1,0:T(8,128)S(1)} %get-tuple-element.146), channel_id=1, source_target_pairs={{0,1},{1,2},{2,3},{3,4},{4,5},{5,6},{6,7},{7,8},{8,9},{9,10},{10,1... | collective-permute-start | bytes 2312 | tf_op jit(solution)/shard_map/ppermute | solution.py:147
  179.8 11.6 %collective-permute-start.6 = (f32[3,2,128]{2,1,0:T(2,128)S(1)}, f32[3,2,128]{2,1,0:T(2,128)S(1)}, u32[]{:S(2)}, u32[]{:S(2)}) collective-permute-start(f32[3,2,128]{2,1,0:T(2,128)S(1)} %get-tuple-element.143), channel_id=1, source_target_pairs={{0,32},{32,64},{64,96},{96,128},{128,160},{160,192},{192,224},{224... | collective-permute-start | bytes 9224 | tf_op jit(solution)/shard_map/ppermute | solution.py:142
  181.8 10.1 %collective-permute-start.9 = (f32[3,2,128]{2,1,0:T(2,128)S(1)}, f32[3,2,128]{2,1,0:T(2,128)S(1)}, u32[]{:S(2)}, u32[]{:S(2)}) collective-permute-start(f32[3,2,128]{2,1,0:T(2,128)S(1)} %get-tuple-element.144), channel_id=1, source_target_pairs={{0,736},{32,0},{64,32},{96,64},{128,96},{160,128},{192,160},{224,1... | collective-permute-start | bytes 9224 | tf_op jit(solution)/shard_map/ppermute | solution.py:142
  228.4 13.0 %collective-permute-start.11 = (f32[3,128]{1,0:T(4,128)S(1)}, f32[3,128]{1,0:T(4,128)S(1)}, u32[]{:S(2)}, u32[]{:S(2)}) collective-permute-start(f32[3,128]{1,0:T(4,128)S(1)} %bitcast.382), channel_id=1, source_target_pairs={{0,736},{32,0},{64,32},{96,64},{128,96},{160,128},{192,160},{224,1... | collective-permute-start | bytes 4616 | tf_op jit(solution)/shard_map/ppermute | solution.py:142
  238.1 10.3 %collective-permute-start.10 = (f32[3,128]{1,0:T(4,128)S(1)}, f32[3,128]{1,0:T(4,128)S(1)}, u32[]{:S(2)}, u32[]{:S(2)}) collective-permute-start(f32[3,128]{1,0:T(4,128)S(1)} %bitcast.381), channel_id=1, source_target_pairs={{0,32},{32,64},{64,96},{96,128},{128,160},{160,192},{192,224},{224... | collective-permute-start | bytes 4616 | tf_op jit(solution)/shard_map/ppermute | solution.py:142
Sparse Core Ops, SparseCore 0:
  42.2 59.7 all-gather.4
  159.1 62.5 all-gather.6
